TPU v7x, 512 devices: a whole 4x4x16 slice. The times are simulated.
512 devices in a mesh: row: 32 (over z, core), band: 16 (over y, x).
Axes of the slice: x: 4, y: 4, z: 16, core: 2. Of those that a mesh axis runs over, the one named last changes fastest.
Arguments:
- band_blocks: bfloat16 [1024, 16, 128, 128], P('row', 'band'), may hold values from 0 to 0.006591797, as said below
- distant_block_slots: bfloat16 [32, 16, 32, 2, 128, 128], P('row', 'band'), may hold values from 0 to 0.00033203125, as said below
- far_rows: int32 [32, 16, 32, 2], P('row', 'band'), may hold values from 0 to 31
- far_columns: int32 [32, 16, 32, 2], P('row', 'band'), may hold values from 0 to 31
- far_counts: int32 [32, 16, 32], P('row', 'band'), may hold values from 0 to 2, as said below
Outputs:
- scaling: float32 [1024, 128], P('row')
- residual: float32 [1024, 128], P('row')
Inputs may be any that keep to these rules, and one draw needn't show every extreme that they name: `band_blocks`: positive entries; offset-0 blocks symmetric. `distant_block_slots`: positive entries. `far_counts`: some target range receives 2 live slots from every device.
All inputs are finite; a program needn't handle non-finite values.
Results may differ from a plain program's by a relative error of at most 0.0116.
The roundings to bfloat16 on the way count: a program that leaves them out, or rounds other values in their place, can miss the bound.
Values may be sent and summed in bfloat16 or wider, within the bound.
No kernel may reach another device: no remote copies, remote signals or barrier semaphores. Data moves between devices by JAX's collectives and lax.ppermute only.
A program may use at most 64 MiB of HBM per device.

v0:
```python
import jax
import jax.numpy as jnp
from jax import lax
from jax.sharding import PartitionSpec as P

OUTER = 2
INNER = 2


def shifted(value, axis, steps):
    count = lax.axis_size(axis)
    leading, last = (max(0, -steps), min(count, count - steps))
    return lax.ppermute(value, axis, [(source, source + steps) for source in range(leading, last)])


def on_device(band_blocks, distant_block_slots, far_rows, far_columns, far_counts):
    rows_dev = band_blocks.shape[0]
    block_size = band_blocks.shape[2]
    band_count = lax.axis_size("band")
    row_count = lax.axis_size("row")
    offset = lax.axis_index("band")
    row_index = lax.axis_index("row")
    blocks = band_blocks[:, 0]
    distant_local_part = distant_block_slots[0, 0]
    local_row_values = far_rows[0, 0]
    columns_local = far_columns[0, 0]
    counts = far_counts[0, 0]
    slots = local_row_values.shape[1]
    live_mask = (jnp.arange(slots)[None, :] < counts[:, None]).astype(jnp.float32)[..., None]
    block_ids = row_index * rows_dev + jnp.arange(rows_dev)
    valid_mask = (block_ids + offset < row_count * rows_dev).astype(jnp.float32)[:, None]
    upper_mask = (offset > 0).astype(jnp.float32)
    wanted = lax.all_to_all(columns_local, "row", split_axis=0, concat_axis=0, tiled=True)
    targets = jnp.arange(rows_dev)[None, :]
    selection_output = (wanted.reshape(-1)[:, None] == targets).astype(jnp.float32)
    pick_in = (local_row_values.reshape(-1)[:, None] == targets).astype(jnp.float32)

    def multiply(vector):
        narrow_band_part = vector.astype(jnp.bfloat16)
        ahead_rows = shifted(narrow_band_part[:band_count], "row", -1)
        extended = jnp.concatenate([narrow_band_part, ahead_rows], 0)
        columns = lax.dynamic_slice_in_dim(extended, offset, rows_dev, 0)
        forward = (
            jnp.einsum("kij,kj->ki", blocks, columns, preferred_element_type=jnp.float32)
            * valid_mask
        )
        backward = jnp.einsum(
            "kij,ki->kj", blocks, narrow_band_part, preferred_element_type=jnp.float32
        ) * (valid_mask * upper_mask)
        spread = lax.dynamic_update_slice_in_dim(
            jnp.zeros((rows_dev + band_count, block_size), jnp.float32), backward, offset, 0
        )
        outgoing = narrow_band_part[wanted]
        gathered_values = lax.all_to_all(outgoing, "row", split_axis=0, concat_axis=0, tiled=True)
        far_forward = (
            jnp.einsum(
                "oqht,oqt->oqh",
                distant_local_part,
                gathered_values,
                preferred_element_type=jnp.float32,
            )
            * live_mask
        )
        far_backward = (
            jnp.einsum(
                "nquo,nqu->nqo",
                distant_local_part,
                narrow_band_part[local_row_values],
                preferred_element_type=jnp.float32,
            )
            * live_mask
        )
        returned = lax.all_to_all(far_backward, "row", split_axis=0, concat_axis=0, tiled=True)
        summed = forward + spread[:rows_dev]
        summed = summed + jnp.dot(
            pick_in.T, far_forward.reshape(-1, block_size), precision=lax.Precision.HIGHEST
        )
        summed = summed + jnp.dot(
            selection_output.T, returned.reshape(-1, block_size), precision=lax.Precision.HIGHEST
        )
        carried = shifted(spread[rows_dev:], "row", 1)
        summed = jnp.concatenate([summed[:band_count] + carried, summed[band_count:]], 0)
        return lax.psum(summed, "band")

    row_sums = multiply(jnp.ones((rows_dev, block_size), jnp.float32))
    scaling = 1.0 / jnp.sqrt(row_sums)
    residual = jnp.zeros_like(scaling)
    for outer_step in range(OUTER):
        balance = scaling * multiply(scaling)
        residual = 1.0 - balance
        scaled = residual / balance
        direction = scaled
        current_residual_product = lax.psum(jnp.sum(residual * scaled), "row")
        growth = jnp.ones_like(scaling)
        for inner_step in range(INNER):
            curved = scaling * multiply(scaling * direction) + balance * direction
            curvature = lax.psum(jnp.sum(direction * curved), "row")
            step_size = current_residual_product / curvature
            growth = growth + step_size * direction
            residual = residual - step_size * curved
            if inner_step + 1 < INNER:
                scaled = residual / balance
                rho_next = lax.psum(jnp.sum(residual * scaled), "row")
                direction = scaled + rho_next / current_residual_product * direction
                current_residual_product = rho_next
        scaling = scaling * growth
    return (scaling, residual)


def solution(mesh):
    return jax.shard_map(
        on_device,
        mesh=mesh,
        in_specs=(
            P("row", "band", None, None),
            P("row", "band", None, None, None, None),
            P("row", "band", None, None),
            P("row", "band", None, None),
            P("row", "band", None),
        ),
        out_specs=(P("row", None), P("row", None)),
        check_vma=False,
    )
```

profile of v0, /device:TPU:1, one launch (start us, length us, event | category | flops | bytes accessed | tf_op | source)
XLA Modules:
  0.0 1086.6 jit_solution(9231055719620302037)
XLA Ops:
  0.7 9.0 collective-permute-start
  11.1 10.0 all-to-all-start
  35.0 6.2 all-to-all-start.1
  44.7 8.2 all-to-all-done.1
  59.5 12.0 %all-to-all-done.2 = f32[32,2,128]{2,1,0:T(2,128)S(1)} async-done(((f32[32,2,128]{2,1,0:T(2,128)}), f32[32,2,128]{2,1,0:T(2,128)S(1)}, u32[]{:S(2)}, u32[]{:S(2)}) %all-to-all-start.2) | async-done | bytes 32800 | tf_op jit(solution)/shard_map/all_to_all | solution.py:73
  71.8 60.6 %psum.105 = f32[32,128]{1,0:T(8,128)S(1)} all-reduce(f32[32,128]{1,0:T(8,128)S(1)} %pad_maximum_fusion), channel_id=1, replica_groups=mesh['row'=32,'band'=16] {'band'}, use_global_device_ids=true, to_apply=%region_0.0 | all-reduce | flops 4096 | bytes 32768 | tf_op jit(solution)/shard_map/psum | solution.py:83
  134.3 16.9 %collective-permute-start.2 = (bf16[16,128]{1,0:T(8,128)(2,1)S(1)}, bf16[16,128]{1,0:T(8,128)(2,1)S(1)}, u32[]{:S(2)}, u32[]{:S(2)}) collective-permute-start(bf16[16,128]{1,0:T(8,128)(2,1)S(1)} %slice.172), channel_id=1, source_target_pairs={{16,0},{32,16},{48,32},{64,48},{80,64},{96,80},{112,96},{128,112},... | collective-permute-start | bytes 12296 | tf_op jit(solution)/shard_map/ppermute | solution.py:13
  159.7 6.2 all-to-all-done.3
  172.8 11.8 %all-to-all-done.4 = f32[32,2,128]{2,1,0:T(2,128)S(1)} async-done(((f32[32,2,128]{2,1,0:T(2,128)}), f32[32,2,128]{2,1,0:T(2,128)S(1)}, u32[]{:S(2)}, u32[]{:S(2)}) %all-to-all-start.4) | async-done | bytes 32800 | tf_op jit(solution)/shard_map/all_to_all | solution.py:73
  184.9 55.9 %psum.106 = f32[32,128]{1,0:T(8,128)S(1)} all-reduce(f32[32,128]{1,0:T(8,128)S(1)} %pad_maximum_fusion.1), channel_id=1, replica_groups=mesh['row'=32,'band'=16] {'band'}, use_global_device_ids=true, to_apply=%region_1.0 | all-reduce | flops 4096 | bytes 32768 | tf_op jit(solution)/shard_map/psum | solution.py:83
  242.7 16.7 %collective-permute-start.4 = (bf16[16,128]{1,0:T(8,128)(2,1)S(1)}, bf16[16,128]{1,0:T(8,128)(2,1)S(1)}, u32[]{:S(2)}, u32[]{:S(2)}) collective-permute-start(bf16[16,128]{1,0:T(8,128)(2,1)S(1)} %slice.177), channel_id=1, source_target_pairs={{16,0},{32,16},{48,32},{64,48},{80,64},{96,80},{112,96},{128,112},... | collective-permute-start | bytes 12296 | tf_op jit(solution)/shard_map/ppermute | solution.py:13
  267.9 6.2 all-to-all-done.5
  281.0 11.8 %all-to-all-done.6 = f32[32,2,128]{2,1,0:T(2,128)S(1)} async-done(((f32[32,2,128]{2,1,0:T(2,128)}), f32[32,2,128]{2,1,0:T(2,128)S(1)}, u32[]{:S(2)}, u32[]{:S(2)}) %all-to-all-start.6) | async-done | bytes 32800 | tf_op jit(solution)/shard_map/all_to_all | solution.py:73
  293.1 55.9 %psum.108 = f32[32,128]{1,0:T(8,128)S(1)} all-reduce(f32[32,128]{1,0:T(8,128)S(1)} %pad_maximum_fusion.2), channel_id=1, replica_groups=mesh['row'=32,'band'=16] {'band'}, use_global_device_ids=true, to_apply=%region_4.0 | all-reduce | flops 4096 | bytes 32768 | tf_op jit(solution)/shard_map/psum | solution.py:83
  349.6 60.6 %all-reduce.2 = (f32[]{:T(128)}, f32[]{:T(128)}) all-reduce(f32[]{:T(128)} %get-tuple-element.3, f32[]{:T(128)} %get-tuple-element.2), channel_id=1, replica_groups=mesh['row'=32,'band'=16] {'row'}, use_global_device_ids=true, to_apply=%region_3.0 | all-reduce | flops 2 | bytes 16 | tf_op jit(solution)/shard_map/psum | solution.py:93
  412.1 46.4 %psum.110 = f32[]{:T(128)} all-reduce(f32[]{:T(128)} %multiply_reduce_fusion.4), channel_id=1, replica_groups=mesh['row'=32,'band'=16] {'row'}, use_global_device_ids=true, to_apply=%region_8.0 | all-reduce | flops 1 | bytes 8 | tf_op jit(solution)/shard_map/psum | solution.py:103
  473.1 6.0 all-to-all-done.7
  486.0 11.8 %all-to-all-done.8 = f32[32,2,128]{2,1,0:T(2,128)S(1)} async-done(((f32[32,2,128]{2,1,0:T(2,128)}), f32[32,2,128]{2,1,0:T(2,128)S(1)}, u32[]{:S(2)}, u32[]{:S(2)}) %all-to-all-start.8) | async-done | bytes 32800 | tf_op jit(solution)/shard_map/all_to_all | solution.py:73
  498.1 55.9 %psum.111 = f32[32,128]{1,0:T(8,128)S(1)} all-reduce(f32[32,128]{1,0:T(8,128)S(1)} %pad_maximum_fusion.3), channel_id=1, replica_groups=mesh['row'=32,'band'=16] {'band'}, use_global_device_ids=true, to_apply=%region_9.0 | all-reduce | flops 4096 | bytes 32768 | tf_op jit(solution)/shard_map/psum | solution.py:83
  554.6 60.6 %psum.112 = f32[]{:T(128)} all-reduce(f32[]{:T(128)} %multiply_reduce_fusion.3), channel_id=1, replica_groups=mesh['row'=32,'band'=16] {'row'}, use_global_device_ids=true, to_apply=%region_11.0 | all-reduce | flops 1 | bytes 8 | tf_op jit(solution)/shard_map/psum | solution.py:97
  629.6 6.0 all-to-all-done.9
  642.5 11.8 %all-to-all-done.10 = f32[32,2,128]{2,1,0:T(2,128)S(1)} async-done(((f32[32,2,128]{2,1,0:T(2,128)}), f32[32,2,128]{2,1,0:T(2,128)S(1)}, u32[]{:S(2)}, u32[]{:S(2)}) %all-to-all-start.10) | async-done | bytes 32800 | tf_op jit(solution)/shard_map/all_to_all | solution.py:73
  654.6 55.9 %psum.113 = f32[32,128]{1,0:T(8,128)S(1)} all-reduce(f32[32,128]{1,0:T(8,128)S(1)} %pad_maximum_fusion.4), channel_id=1, replica_groups=mesh['row'=32,'band'=16] {'band'}, use_global_device_ids=true, to_apply=%region_12.0 | all-reduce | flops 4096 | bytes 32768 | tf_op jit(solution)/shard_map/psum | solution.py:83
  712.4 16.7 %collective-permute-start.10 = (bf16[16,128]{1,0:T(8,128)(2,1)S(1)}, bf16[16,128]{1,0:T(8,128)(2,1)S(1)}, u32[]{:S(2)}, u32[]{:S(2)}) collective-permute-start(bf16[16,128]{1,0:T(8,128)(2,1)S(1)} %slice.192), channel_id=1, source_target_pairs={{16,0},{32,16},{48,32},{64,48},{80,64},{96,80},{112,96},{128,112},... | collective-permute-start | bytes 12296 | tf_op jit(solution)/shard_map/ppermute | solution.py:13
  737.6 6.2 all-to-all-done.11
  750.7 11.8 %all-to-all-done.12 = f32[32,2,128]{2,1,0:T(2,128)S(1)} async-done(((f32[32,2,128]{2,1,0:T(2,128)}), f32[32,2,128]{2,1,0:T(2,128)S(1)}, u32[]{:S(2)}, u32[]{:S(2)}) %all-to-all-start.12) | async-done | bytes 32800 | tf_op jit(solution)/shard_map/all_to_all | solution.py:73
  762.8 55.9 %psum.115 = f32[32,128]{1,0:T(8,128)S(1)} all-reduce(f32[32,128]{1,0:T(8,128)S(1)} %pad_maximum_fusion.5), channel_id=1, replica_groups=mesh['row'=32,'band'=16] {'band'}, use_global_device_ids=true, to_apply=%region_15.0 | all-reduce | flops 4096 | bytes 32768 | tf_op jit(solution)/shard_map/psum | solution.py:83
  819.3 60.6 %all-reduce.1 = (f32[]{:T(128)}, f32[]{:T(128)}) all-reduce(f32[]{:T(128)} %get-tuple-element.5, f32[]{:T(128)} %get-tuple-element.4), channel_id=1, replica_groups=mesh['row'=32,'band'=16] {'row'}, use_global_device_ids=true, to_apply=%region_14.0 | all-reduce | flops 2 | bytes 16 | tf_op jit(solution)/shard_map/psum | solution.py:93
  881.9 46.4 %psum.117 = f32[]{:T(128)} all-reduce(f32[]{:T(128)} %get-tuple-element.10), channel_id=1, replica_groups=mesh['row'=32,'band'=16] {'row'}, use_global_device_ids=true, to_apply=%region_19.0 | all-reduce | flops 1 | bytes 8 | tf_op jit(solution)/shard_map/psum | solution.py:103
  955.6 11.8 %all-to-all-done.14 = f32[32,2,128]{2,1,0:T(2,128)S(1)} async-done(((f32[32,2,128]{2,1,0:T(2,128)}), f32[32,2,128]{2,1,0:T(2,128)S(1)}, u32[]{:S(2)}, u32[]{:S(2)}) %all-to-all-start.14) | async-done | bytes 32800 | tf_op jit(solution)/shard_map/all_to_all | solution.py:73
  967.7 55.9 %psum.118 = f32[32,128]{1,0:T(8,128)S(1)} all-reduce(f32[32,128]{1,0:T(8,128)S(1)} %pad_maximum_fusion.6), channel_id=1, replica_groups=mesh['row'=32,'band'=16] {'band'}, use_global_device_ids=true, to_apply=%region_20.0 | all-reduce | flops 4096 | bytes 32768 | tf_op jit(solution)/shard_map/psum | solution.py:83
  1024.2 60.6 %psum.119 = f32[]{:T(128)} all-reduce(f32[]{:T(128)} %multiply_reduce_fusion), channel_id=1, replica_groups=mesh['row'=32,'band'=16] {'row'}, use_global_device_ids=true, to_apply=%region_22.0 | all-reduce | flops 1 | bytes 8 | tf_op jit(solution)/shard_map/psum | solution.py:97
  (194 shorter events, 149.3 us)
Async XLA Ops:
  0.6 41.4 %copy-start = (bf16[1,1,32,2,128,128]{5,4,3,2,1,0:T(8,128)(2,1)S(1)}, bf16[1,1,32,2,128,128]{5,4,3,2,1,0:T(8,128)(2,1)}, u32[]{:S(2)}) copy-start(bf16[1,1,32,2,128,128]{5,4,3,2,1,0:T(8,128)(2,1)} %param.6) | copy-start | bytes 6291460
  0.6 43.4 %copy-start.1 = (bf16[32,1,128,128]{3,2,1,0:T(8,128)(2,1)S(1)}, bf16[32,1,128,128]{3,2,1,0:T(8,128)(2,1)}, u32[]{:S(2)}) copy-start(bf16[32,1,128,128]{3,2,1,0:T(8,128)(2,1)} %param.5) | copy-start | bytes 3145732
  0.7 43.3 %collective-permute-start = (bf16[16,128]{1,0:T(8,128)(2,1)S(1)}, bf16[16,128]{1,0:T(8,128)(2,1)S(1)}, u32[]{:S(2)}, u32[]{:S(2)}) collective-permute-start(bf16[16,128]{1,0:T(8,128)(2,1)S(1)} %slice.105), channel_id=1, source_target_pairs={{16,0},{32,16},{48,32},{64,48},{80,64},{96,80},{112,96},{128,112},... | collective-permute-start | bytes 12296 | tf_op jit(solution)/shard_map/ppermute | solution.py:13
  11.1 21.8 %all-to-all-start = ((s32[32,1,2]{2,1,0:T(1,128)}), s32[32,1,2]{2,1,0:T(1,128)S(1)}, u32[]{:S(2)}, u32[]{:S(2)}) async-start(s32[32,1,2]{2,1,0:T(1,128)} %copy.16), calls=%async_computation | async-start | bytes 32768 | tf_op jit(solution)/shard_map/all_to_all | solution.py:33
  23.0 48.8 %collective-permute-start.1 = (f32[16,128]{1,0:T(8,128)S(1)}, f32[16,128]{1,0:T(8,128)S(1)}, u32[]{:S(2)}, u32[]{:S(2)}) collective-permute-start(f32[16,128]{1,0:T(8,128)S(1)} %slice.170), channel_id=1, source_target_pairs={{0,16},{16,32},{32,48},{48,64},{64,80},{80,96},{96,112},{112,128},... | collective-permute-start | bytes 24584 | tf_op jit(solution)/shard_map/ppermute | solution.py:13
  35.0 17.9 %all-to-all-start.1 = ((bf16[32,2,128]{2,1,0:T(2,128)(2,1)}), bf16[32,2,128]{2,1,0:T(2,128)(2,1)S(1)}, u32[]{:S(2)}, u32[]{:S(2)}) async-start(bf16[32,2,128]{2,1,0:T(2,128)(2,1)} %bitcast.8), calls=%async_computation.1 | async-start | bytes 32768 | tf_op jit(solution)/shard_map/all_to_all | solution.py:54
  54.8 16.6 %all-to-all-start.2 = ((f32[32,2,128]{2,1,0:T(2,128)}), f32[32,2,128]{2,1,0:T(2,128)S(1)}, u32[]{:S(2)}, u32[]{:S(2)}) async-start(f32[32,2,128]{2,1,0:T(2,128)} %get-tuple-element.45), calls=%async_computation.2 | async-start | bytes 65536 | tf_op jit(solution)/shard_map/all_to_all | solution.py:73
  134.3 24.7 %collective-permute-start.2 = (bf16[16,128]{1,0:T(8,128)(2,1)S(1)}, bf16[16,128]{1,0:T(8,128)(2,1)S(1)}, u32[]{:S(2)}, u32[]{:S(2)}) collective-permute-start(bf16[16,128]{1,0:T(8,128)(2,1)S(1)} %slice.172), channel_id=1, source_target_pairs={{16,0},{32,16},{48,32},{64,48},{80,64},{96,80},{112,96},{128,112},... | collective-permute-start | bytes 12296 | tf_op jit(solution)/shard_map/ppermute | solution.py:13
  151.2 14.7 %all-to-all-start.3 = ((bf16[32,2,128]{2,1,0:T(2,128)(2,1)}), bf16[32,2,128]{2,1,0:T(2,128)(2,1)S(1)}, u32[]{:S(2)}, u32[]{:S(2)}) async-start(bf16[32,2,128]{2,1,0:T(2,128)(2,1)} %bitcast.27), calls=%async_computation.3 | async-start | bytes 32768 | tf_op jit(solution)/shard_map/all_to_all | solution.py:54
  156.2 28.7 %collective-permute-start.3 = (f32[16,128]{1,0:T(8,128)S(1)}, f32[16,128]{1,0:T(8,128)S(1)}, u32[]{:S(2)}, u32[]{:S(2)}) collective-permute-start(f32[16,128]{1,0:T(8,128)S(1)} %slice.175), channel_id=1, source_target_pairs={{0,16},{16,32},{32,48},{48,64},{64,80},{80,96},{96,112},{112,128},... | collective-permute-start | bytes 24584 | tf_op jit(solution)/shard_map/ppermute | solution.py:13
  167.8 16.8 %all-to-all-start.4 = ((f32[32,2,128]{2,1,0:T(2,128)}), f32[32,2,128]{2,1,0:T(2,128)S(1)}, u32[]{:S(2)}, u32[]{:S(2)}) async-start(f32[32,2,128]{2,1,0:T(2,128)} %get-tuple-element.41), calls=%async_computation.4 | async-start | bytes 65536 | tf_op jit(solution)/shard_map/all_to_all | solution.py:73
  242.7 24.5 %collective-permute-start.4 = (bf16[16,128]{1,0:T(8,128)(2,1)S(1)}, bf16[16,128]{1,0:T(8,128)(2,1)S(1)}, u32[]{:S(2)}, u32[]{:S(2)}) collective-permute-start(bf16[16,128]{1,0:T(8,128)(2,1)S(1)} %slice.177), channel_id=1, source_target_pairs={{16,0},{32,16},{48,32},{64,48},{80,64},{96,80},{112,96},{128,112},... | collective-permute-start | bytes 12296 | tf_op jit(solution)/shard_map/ppermute | solution.py:13
  259.4 14.7 %all-to-all-start.5 = ((bf16[32,2,128]{2,1,0:T(2,128)(2,1)}), bf16[32,2,128]{2,1,0:T(2,128)(2,1)S(1)}, u32[]{:S(2)}, u32[]{:S(2)}) async-start(bf16[32,2,128]{2,1,0:T(2,128)(2,1)} %bitcast.43), calls=%async_computation.5 | async-start | bytes 32768 | tf_op jit(solution)/shard_map/all_to_all | solution.py:54
  264.4 28.7 %collective-permute-start.5 = (f32[16,128]{1,0:T(8,128)S(1)}, f32[16,128]{1,0:T(8,128)S(1)}, u32[]{:S(2)}, u32[]{:S(2)}) collective-permute-start(f32[16,128]{1,0:T(8,128)S(1)} %slice.180), channel_id=1, source_target_pairs={{0,16},{16,32},{32,48},{48,64},{64,80},{80,96},{96,112},{112,128},... | collective-permute-start | bytes 24584 | tf_op jit(solution)/shard_map/ppermute | solution.py:13
  276.0 16.8 %all-to-all-start.6 = ((f32[32,2,128]{2,1,0:T(2,128)}), f32[32,2,128]{2,1,0:T(2,128)S(1)}, u32[]{:S(2)}, u32[]{:S(2)}) async-start(f32[32,2,128]{2,1,0:T(2,128)} %get-tuple-element.37), calls=%async_computation.6 | async-start | bytes 65536 | tf_op jit(solution)/shard_map/all_to_all | solution.py:73
  461.7 10.7 collective-permute-start.6
  464.3 14.8 %all-to-all-start.7 = ((bf16[32,2,128]{2,1,0:T(2,128)(2,1)}), bf16[32,2,128]{2,1,0:T(2,128)(2,1)S(1)}, u32[]{:S(2)}, u32[]{:S(2)}) async-start(bf16[32,2,128]{2,1,0:T(2,128)(2,1)} %bitcast.59), calls=%async_computation.7 | async-start | bytes 32768 | tf_op jit(solution)/shard_map/all_to_all | solution.py:54
  469.4 28.7 %collective-permute-start.7 = (f32[16,128]{1,0:T(8,128)S(1)}, f32[16,128]{1,0:T(8,128)S(1)}, u32[]{:S(2)}, u32[]{:S(2)}) collective-permute-start(f32[16,128]{1,0:T(8,128)S(1)} %slice.185), channel_id=1, source_target_pairs={{0,16},{16,32},{32,48},{48,64},{64,80},{80,96},{96,112},{112,128},... | collective-permute-start | bytes 24584 | tf_op jit(solution)/shard_map/ppermute | solution.py:13
  481.0 16.8 %all-to-all-start.8 = ((f32[32,2,128]{2,1,0:T(2,128)}), f32[32,2,128]{2,1,0:T(2,128)S(1)}, u32[]{:S(2)}, u32[]{:S(2)}) async-start(f32[32,2,128]{2,1,0:T(2,128)} %get-tuple-element.33), calls=%async_computation.8 | async-start | bytes 65536 | tf_op jit(solution)/shard_map/all_to_all | solution.py:73
  618.4 10.5 collective-permute-start.8
  620.9 14.7 %all-to-all-start.9 = ((bf16[32,2,128]{2,1,0:T(2,128)(2,1)}), bf16[32,2,128]{2,1,0:T(2,128)(2,1)S(1)}, u32[]{:S(2)}, u32[]{:S(2)}) async-start(bf16[32,2,128]{2,1,0:T(2,128)(2,1)} %bitcast.75), calls=%async_computation.9 | async-start | bytes 32768 | tf_op jit(solution)/shard_map/all_to_all | solution.py:54
  625.9 28.7 %collective-permute-start.9 = (f32[16,128]{1,0:T(8,128)S(1)}, f32[16,128]{1,0:T(8,128)S(1)}, u32[]{:S(2)}, u32[]{:S(2)}) collective-permute-start(f32[16,128]{1,0:T(8,128)S(1)} %slice.190), channel_id=1, source_target_pairs={{0,16},{16,32},{32,48},{48,64},{64,80},{80,96},{96,112},{112,128},... | collective-permute-start | bytes 24584 | tf_op jit(solution)/shard_map/ppermute | solution.py:13
  637.5 16.8 %all-to-all-start.10 = ((f32[32,2,128]{2,1,0:T(2,128)}), f32[32,2,128]{2,1,0:T(2,128)S(1)}, u32[]{:S(2)}, u32[]{:S(2)}) async-start(f32[32,2,128]{2,1,0:T(2,128)} %get-tuple-element.29), calls=%async_computation.10 | async-start | bytes 65536 | tf_op jit(solution)/shard_map/all_to_all | solution.py:73
  712.4 24.5 %collective-permute-start.10 = (bf16[16,128]{1,0:T(8,128)(2,1)S(1)}, bf16[16,128]{1,0:T(8,128)(2,1)S(1)}, u32[]{:S(2)}, u32[]{:S(2)}) collective-permute-start(bf16[16,128]{1,0:T(8,128)(2,1)S(1)} %slice.192), channel_id=1, source_target_pairs={{16,0},{32,16},{48,32},{64,48},{80,64},{96,80},{112,96},{128,112},... | collective-permute-start | bytes 12296 | tf_op jit(solution)/shard_map/ppermute | solution.py:13
  729.1 14.7 %all-to-all-start.11 = ((bf16[32,2,128]{2,1,0:T(2,128)(2,1)}), bf16[32,2,128]{2,1,0:T(2,128)(2,1)S(1)}, u32[]{:S(2)}, u32[]{:S(2)}) async-start(bf16[32,2,128]{2,1,0:T(2,128)(2,1)} %bitcast.91), calls=%async_computation.11 | async-start | bytes 32768 | tf_op jit(solution)/shard_map/all_to_all | solution.py:54
  734.1 28.7 %collective-permute-start.11 = (f32[16,128]{1,0:T(8,128)S(1)}, f32[16,128]{1,0:T(8,128)S(1)}, u32[]{:S(2)}, u32[]{:S(2)}) collective-permute-start(f32[16,128]{1,0:T(8,128)S(1)} %slice.195), channel_id=1, source_target_pairs={{0,16},{16,32},{32,48},{48,64},{64,80},{80,96},{96,112},{112,128},... | collective-permute-start | bytes 24584 | tf_op jit(solution)/shard_map/ppermute | solution.py:13
  745.7 16.8 %all-to-all-start.12 = ((f32[32,2,128]{2,1,0:T(2,128)}), f32[32,2,128]{2,1,0:T(2,128)S(1)}, u32[]{:S(2)}, u32[]{:S(2)}) async-start(f32[32,2,128]{2,1,0:T(2,128)} %get-tuple-element.25), calls=%async_computation.12 | async-start | bytes 65536 | tf_op jit(solution)/shard_map/all_to_all | solution.py:73
  931.4 10.5 collective-permute-start.12
  934.0 14.7 %all-to-all-start.13 = ((bf16[32,2,128]{2,1,0:T(2,128)(2,1)}), bf16[32,2,128]{2,1,0:T(2,128)(2,1)S(1)}, u32[]{:S(2)}, u32[]{:S(2)}) async-start(bf16[32,2,128]{2,1,0:T(2,128)(2,1)} %bitcast.107), calls=%async_computation.13 | async-start | bytes 32768 | tf_op jit(solution)/shard_map/all_to_all | solution.py:54
  938.9 28.7 %collective-permute-start.13 = (f32[16,128]{1,0:T(8,128)S(1)}, f32[16,128]{1,0:T(8,128)S(1)}, u32[]{:S(2)}, u32[]{:S(2)}) collective-permute-start(f32[16,128]{1,0:T(8,128)S(1)} %slice.200), channel_id=1, source_target_pairs={{0,16},{16,32},{32,48},{48,64},{64,80},{80,96},{96,112},{112,128},... | collective-permute-start | bytes 24584 | tf_op jit(solution)/shard_map/ppermute | solution.py:13
  950.5 16.8 %all-to-all-start.14 = ((f32[32,2,128]{2,1,0:T(2,128)}), f32[32,2,128]{2,1,0:T(2,128)S(1)}, u32[]{:S(2)}, u32[]{:S(2)}) async-start(f32[32,2,128]{2,1,0:T(2,128)} %get-tuple-element.21), calls=%async_computation.14 | async-start | bytes 65536 | tf_op jit(solution)/shard_map/all_to_all | solution.py:73
where the time goes:
time: 1090 us
  blocking collectives  731 us (67%)
  starting transfers between devices  159 us (15%)
  waiting for transfers between devices  132 us (12%)
  matrix products  24.9 us (2%)
  local copies, waits for them, and re-layouts  17.9 us (2%)
  other arithmetic  12.5 us (1%)
    psum x7, blocking collectives, multiply(): return lax.psum(summed, 'band')  396 us
    psum x2, blocking collectives, on_device(): current_residual_product = lax.psum(jnp.sum(residual * scaled), 'row')  121 us
    psum x2, blocking collectives, on_device(): curvature = lax.psum(jnp.sum(direction * curved), 'row')  121 us
    psum x2, blocking collectives, on_device(): rho_next = lax.psum(jnp.sum(residual * scaled), 'row')  92.8 us
    ppermute x14, starting transfers between devices, shifted(): lax.ppermute(value, axis, [(source, source + steps) for source in range(l...  87.9 us
    all_to_all x7, waiting for transfers between devices, multiply(): lax.all_to_all(far_backward, 'row', split_axis=0, concat_axis=0, tiled=True)  82.6 us
    all_to_all x7, waiting for transfers between devices, multiply(): lax.all_to_all(outgoing, 'row', split_axis=0, concat_axis=0, tiled=True)  44.9 us
    all_to_all x7, starting transfers between devices, multiply(): lax.all_to_all(far_backward, 'row', split_axis=0, concat_axis=0, tiled=True)  32.8 us
  transfers between devices with their start and end apart: 29, of which 15 were waited for; matrix products, arithmetic and copies ran while one was open for 4% of the time, Pallas kernels for 0%

commit v1 on v0

--- a/solution.py
+++ b/solution.py
@@ -11,6 +11,17 @@
     count = lax.axis_size(axis)
     leading, last = (max(0, -steps), min(count, count - steps))
     return lax.ppermute(value, axis, [(source, source + steps) for source in range(leading, last)])
+
+
+def all_sum(value, axis):
+    count = lax.axis_size(axis)
+    if count & (count - 1):
+        return lax.psum(value, axis)
+    step = 1
+    while step < count:
+        value = value + lax.ppermute(value, axis, [(source, source ^ step) for source in range(count)])
+        step *= 2
+    return value
 
 
 def on_device(band_blocks, distant_block_slots, far_rows, far_columns, far_counts):
@@ -80,7 +91,7 @@
         )
         carried = shifted(spread[rows_dev:], "row", 1)
         summed = jnp.concatenate([summed[:band_count] + carried, summed[band_count:]], 0)
-        return lax.psum(summed, "band")
+        return all_sum(summed, "band")
 
     row_sums = multiply(jnp.ones((rows_dev, block_size), jnp.float32))
     scaling = 1.0 / jnp.sqrt(row_sums)
@@ -90,17 +101,17 @@
         residual = 1.0 - balance
         scaled = residual / balance
         direction = scaled
-        current_residual_product = lax.psum(jnp.sum(residual * scaled), "row")
+        current_residual_product = all_sum(jnp.sum(residual * scaled), "row")
         growth = jnp.ones_like(scaling)
         for inner_step in range(INNER):
             curved = scaling * multiply(scaling * direction) + balance * direction
-            curvature = lax.psum(jnp.sum(direction * curved), "row")
+            curvature = all_sum(jnp.sum(direction * curved), "row")
             step_size = current_residual_product / curvature
             growth = growth + step_size * direction
             residual = residual - step_size * curved
             if inner_step + 1 < INNER:
                 scaled = residual / balance
-                rho_next = lax.psum(jnp.sum(residual * scaled), "row")
+                rho_next = all_sum(jnp.sum(residual * scaled), "row")
                 direction = scaled + rho_next / current_residual_product * direction
                 current_residual_product = rho_next
         scaling = scaling * growth

time: 1090 us -> 797 us (0.73)
  blocking collectives: 731 us -> 0 us
  starting transfers between devices: 159 us -> 487 us
  waiting for transfers between devices: 132 us -> 216 us
  between operations: 9.24 us -> 31.7 us
    psum x13 -> x0, blocking collectives: 731 us -> none  [the longest x7 396 us: multiply(): return lax.psum(summed, 'band')]
    ppermute x0 -> x68, starting transfers between devices: none -> 324 us  [all_sum(): lax.ppermute(value, axis, [(source, source ^ step) for source in range(co...]
    ppermute x0 -> x68, waiting for transfers between devices: none -> 82.7 us  [all_sum(): lax.ppermute(value, axis, [(source, source ^ step) for source in range(co...]
    all_to_all x7, starting transfers between devices: 28.1 us -> 44.3 us  [multiply(): lax.all_to_all(outgoing, 'row', split_axis=0, concat_axis=0, tiled=True)]
    ppermute x14, starting transfers between devices: 87.9 us -> 75.9 us  [shifted(): lax.ppermute(value, axis, [(source, source + steps) for source in range(l...]
  transfers between devices with their start and end apart: 29 -> 97, of which waited for: 15 -> 63; matrix products, arithmetic and copies ran while one was open for 4% -> 5% of each run, Pallas kernels for 0% -> 0%
where the time goes in v1:
time: 797 us; the launch traced here: 789 us
  starting transfers between devices  487 us (61%)
  waiting for transfers between devices  216 us (27%)
  between operations  31.7 us (4%)
  matrix products  24.9 us (3%)
  local copies, waits for them, and re-layouts  17.8 us (2%)
  other arithmetic  12.5 us (2%)
    ppermute x68, starting transfers between devices, all_sum(): lax.ppermute(value, axis, [(source, source ^ step) for source in range(co...  324 us
    all_to_all x7, waiting for transfers between devices, multiply(): lax.all_to_all(far_backward, 'row', split_axis=0, concat_axis=0, tiled=True)  82.9 us
    ppermute x68, waiting for transfers between devices, all_sum(): lax.ppermute(value, axis, [(source, source ^ step) for source in range(co...  82.7 us
    ppermute x14, starting transfers between devices, shifted(): lax.ppermute(value, axis, [(source, source + steps) for source in range(l...  75.9 us
    all_to_all x7, waiting for transfers between devices, multiply(): lax.all_to_all(outgoing, 'row', split_axis=0, concat_axis=0, tiled=True)  45.5 us
    all_to_all x7, starting transfers between devices, multiply(): lax.all_to_all(outgoing, 'row', split_axis=0, concat_axis=0, tiled=True)  44.3 us
    all_to_all x7, starting transfers between devices, multiply(): lax.all_to_all(far_backward, 'row', split_axis=0, concat_axis=0, tiled=True)  32.6 us
  transfers between devices with their start and end apart: 97, of which 63 were waited for; matrix products, arithmetic and copies ran while one was open for 5% of the time, Pallas kernels for 0%

profile of v1, /device:TPU:1, one launch (start us, length us, event | category | flops | bytes accessed | tf_op | source)
XLA Modules:
  0.0 789.3 jit_solution(13606241933098439464)
XLA Ops:
  0.7 9.0 %collective-permute-start = (bf16[16,128]{1,0:T(8,128)(2,1)S(1)}, bf16[16,128]{1,0:T(8,128)(2,1)S(1)}, u32[]{:S(2)}, u32[]{:S(2)}) collective-permute-start(bf16[16,128]{1,0:T(8,128)(2,1)S(1)} %slice.105), channel_id=1, source_target_pairs={{16,0},{32,16},{48,32},{64,48},{80,64},{96,80},{112,96},{128,112},... | collective-permute-start | bytes 12296 | tf_op jit(solution)/shard_map/ppermute | solution.py:13
  11.1 10.0 %all-to-all-start = ((s32[32,1,2]{2,1,0:T(1,128)}), s32[32,1,2]{2,1,0:T(1,128)S(1)}, u32[]{:S(2)}, u32[]{:S(2)}) async-start(s32[32,1,2]{2,1,0:T(1,128)} %copy.16), calls=%async_computation | async-start | bytes 32768 | tf_op jit(solution)/shard_map/all_to_all | solution.py:44
  44.7 8.2 %all-to-all-done.1 = bf16[32,2,128]{2,1,0:T(2,128)(2,1)S(1)} async-done(((bf16[32,2,128]{2,1,0:T(2,128)(2,1)}), bf16[32,2,128]{2,1,0:T(2,128)(2,1)S(1)}, u32[]{:S(2)}, u32[]{:S(2)}) %all-to-all-start.1) | async-done | bytes 16416 | tf_op jit(solution)/shard_map/all_to_all | solution.py:65
  59.5 12.0 %all-to-all-done.2 = f32[32,2,128]{2,1,0:T(2,128)S(1)} async-done(((f32[32,2,128]{2,1,0:T(2,128)}), f32[32,2,128]{2,1,0:T(2,128)S(1)}, u32[]{:S(2)}, u32[]{:S(2)}) %all-to-all-start.2) | async-done | bytes 32800 | tf_op jit(solution)/shard_map/all_to_all | solution.py:84
  94.6 7.5 collective-permute-start.6
  123.8 11.8 %all-to-all-done.4 = f32[32,2,128]{2,1,0:T(2,128)S(1)} async-done(((f32[32,2,128]{2,1,0:T(2,128)}), f32[32,2,128]{2,1,0:T(2,128)S(1)}, u32[]{:S(2)}, u32[]{:S(2)}) %all-to-all-start.4) | async-done | bytes 32800 | tf_op jit(solution)/shard_map/all_to_all | solution.py:84
  158.7 7.6 collective-permute-start.17
  187.9 11.8 %all-to-all-done.6 = f32[32,2,128]{2,1,0:T(2,128)S(1)} async-done(((f32[32,2,128]{2,1,0:T(2,128)}), f32[32,2,128]{2,1,0:T(2,128)S(1)}, u32[]{:S(2)}, u32[]{:S(2)}) %all-to-all-start.6) | async-done | bytes 32800 | tf_op jit(solution)/shard_map/all_to_all | solution.py:84
  221.6 7.6 collective-permute-start.23
  253.4 7.8 collective-permute-start.15
  265.3 12.6 %collective-permute-start.16 = (f32[]{:T(128)}, f32[]{:T(128)}, u32[]{:S(2)}, u32[]{:S(2)}) collective-permute-start(f32[]{:T(128)} %add.414), channel_id=1, source_target_pairs={{0,256},{16,272},{32,288},{48,304},{64,320},{80,336},{96,352},{112... | collective-permute-start | bytes 20 | tf_op jit(solution)/shard_map/ppermute | solution.py:22
  279.8 9.4 %collective-permute-start.28 = (f32[]{:T(128)}, f32[]{:T(128)}, u32[]{:S(2)}, u32[]{:S(2)}) collective-permute-start(f32[]{:T(128)} %multiply_reduce_fusion.4), channel_id=1, source_target_pairs={{0,16},{16,0},{32,48},{48,32},{64,80},{80,64},{96,112},{112,96},{1... | collective-permute-start | bytes 20 | tf_op jit(solution)/shard_map/ppermute | solution.py:22
  302.1 7.8 collective-permute-start.31
  310.8 12.6 %collective-permute-start.32 = (f32[]{:T(128)}, f32[]{:T(128)}, u32[]{:S(2)}, u32[]{:S(2)}) collective-permute-start(f32[]{:T(128)} %add.433), channel_id=1, source_target_pairs={{0,256},{16,272},{32,288},{48,304},{64,320},{80,336},{96,352},{112... | collective-permute-start | bytes 20 | tf_op jit(solution)/shard_map/ppermute | solution.py:22
  333.8 11.8 %all-to-all-start.7 = ((bf16[32,2,128]{2,1,0:T(2,128)(2,1)}), bf16[32,2,128]{2,1,0:T(2,128)(2,1)S(1)}, u32[]{:S(2)}, u32[]{:S(2)}) async-start(bf16[32,2,128]{2,1,0:T(2,128)(2,1)} %bitcast.59), calls=%async_computation.7 | async-start | bytes 32768 | tf_op jit(solution)/shard_map/all_to_all | solution.py:65
  364.2 11.8 %all-to-all-done.8 = f32[32,2,128]{2,1,0:T(2,128)S(1)} async-done(((f32[32,2,128]{2,1,0:T(2,128)}), f32[32,2,128]{2,1,0:T(2,128)S(1)}, u32[]{:S(2)}, u32[]{:S(2)}) %all-to-all-start.8) | async-done | bytes 32800 | tf_op jit(solution)/shard_map/all_to_all | solution.py:84
  397.9 7.6 collective-permute-start.39
  430.0 10.2 %collective-permute-done.43 = f32[]{:T(128)} collective-permute-done((f32[]{:T(128)}, f32[]{:T(128)}, u32[]{:S(2)}, u32[]{:S(2)}) %collective-permute-start.43) | collective-permute-done | bytes 36 | tf_op jit(solution)/shard_map/ppermute | solution.py:22
  442.6 7.5 collective-permute-start.44
  471.7 11.8 %all-to-all-done.10 = f32[32,2,128]{2,1,0:T(2,128)S(1)} async-done(((f32[32,2,128]{2,1,0:T(2,128)}), f32[32,2,128]{2,1,0:T(2,128)S(1)}, u32[]{:S(2)}, u32[]{:S(2)}) %all-to-all-start.10) | async-done | bytes 32800 | tf_op jit(solution)/shard_map/all_to_all | solution.py:84
  506.6 7.6 collective-permute-start.55
  535.9 11.8 %all-to-all-done.12 = f32[32,2,128]{2,1,0:T(2,128)S(1)} async-done(((f32[32,2,128]{2,1,0:T(2,128)}), f32[32,2,128]{2,1,0:T(2,128)S(1)}, u32[]{:S(2)}, u32[]{:S(2)}) %all-to-all-start.12) | async-done | bytes 32800 | tf_op jit(solution)/shard_map/all_to_all | solution.py:84
  569.5 7.6 collective-permute-start.61
  601.3 7.8 collective-permute-start.53
  613.2 12.6 %collective-permute-start.54 = (f32[]{:T(128)}, f32[]{:T(128)}, u32[]{:S(2)}, u32[]{:S(2)}) collective-permute-start(f32[]{:T(128)} %add.462), channel_id=1, source_target_pairs={{0,256},{16,272},{32,288},{48,304},{64,320},{80,336},{96,352},{112... | collective-permute-start | bytes 20 | tf_op jit(solution)/shard_map/ppermute | solution.py:22
  627.7 9.4 %collective-permute-start.66 = (f32[]{:T(128)}, f32[]{:T(128)}, u32[]{:S(2)}, u32[]{:S(2)}) collective-permute-start(f32[]{:T(128)} %multiply_reduce_fusion.1), channel_id=1, source_target_pairs={{0,16},{16,0},{32,48},{48,32},{64,80},{80,64},{96,112},{112,96},{1... | collective-permute-start | bytes 20 | tf_op jit(solution)/shard_map/ppermute | solution.py:22
  650.1 7.8 collective-permute-start.69
  658.8 12.6 %collective-permute-start.70 = (f32[]{:T(128)}, f32[]{:T(128)}, u32[]{:S(2)}, u32[]{:S(2)}) collective-permute-start(f32[]{:T(128)} %add.481), channel_id=1, source_target_pairs={{0,256},{16,272},{32,288},{48,304},{64,320},{80,336},{96,352},{112... | collective-permute-start | bytes 20 | tf_op jit(solution)/shard_map/ppermute | solution.py:22
  681.7 11.8 %all-to-all-start.13 = ((bf16[32,2,128]{2,1,0:T(2,128)(2,1)}), bf16[32,2,128]{2,1,0:T(2,128)(2,1)S(1)}, u32[]{:S(2)}, u32[]{:S(2)}) async-start(bf16[32,2,128]{2,1,0:T(2,128)(2,1)} %bitcast.107), calls=%async_computation.13 | async-start | bytes 32768 | tf_op jit(solution)/shard_map/all_to_all | solution.py:65
  712.1 11.8 %all-to-all-done.14 = f32[32,2,128]{2,1,0:T(2,128)S(1)} async-done(((f32[32,2,128]{2,1,0:T(2,128)}), f32[32,2,128]{2,1,0:T(2,128)S(1)}, u32[]{:S(2)}, u32[]{:S(2)}) %all-to-all-start.14) | async-done | bytes 32800 | tf_op jit(solution)/shard_map/all_to_all | solution.py:84
  745.8 7.6 collective-permute-start.77
  777.9 10.2 %collective-permute-done.81 = f32[]{:T(128)} collective-permute-done((f32[]{:T(128)}, f32[]{:T(128)}, u32[]{:S(2)}, u32[]{:S(2)}) %collective-permute-start.81) | collective-permute-done | bytes 36 | tf_op jit(solution)/shard_map/ppermute | solution.py:22
  (337 shorter events, 442.7 us)
Async XLA Ops:
  0.7 43.3 %collective-permute-start = (bf16[16,128]{1,0:T(8,128)(2,1)S(1)}, bf16[16,128]{1,0:T(8,128)(2,1)S(1)}, u32[]{:S(2)}, u32[]{:S(2)}) collective-permute-start(bf16[16,128]{1,0:T(8,128)(2,1)S(1)} %slice.105), channel_id=1, source_target_pairs={{16,0},{32,16},{48,32},{64,48},{80,64},{96,80},{112,96},{128,112},... | collective-permute-start | bytes 12296 | tf_op jit(solution)/shard_map/ppermute | solution.py:13
  11.1 21.8 %all-to-all-start = ((s32[32,1,2]{2,1,0:T(1,128)}), s32[32,1,2]{2,1,0:T(1,128)S(1)}, u32[]{:S(2)}, u32[]{:S(2)}) async-start(s32[32,1,2]{2,1,0:T(1,128)} %copy.16), calls=%async_computation | async-start | bytes 32768 | tf_op jit(solution)/shard_map/all_to_all | solution.py:44
  23.0 48.8 %collective-permute-start.1 = (f32[16,128]{1,0:T(8,128)S(1)}, f32[16,128]{1,0:T(8,128)S(1)}, u32[]{:S(2)}, u32[]{:S(2)}) collective-permute-start(f32[16,128]{1,0:T(8,128)S(1)} %slice.170), channel_id=1, source_target_pairs={{0,16},{16,32},{32,48},{48,64},{64,80},{80,96},{96,112},{112,128},... | collective-permute-start | bytes 24584 | tf_op jit(solution)/shard_map/ppermute | solution.py:13
  35.0 17.9 %all-to-all-start.1 = ((bf16[32,2,128]{2,1,0:T(2,128)(2,1)}), bf16[32,2,128]{2,1,0:T(2,128)(2,1)S(1)}, u32[]{:S(2)}, u32[]{:S(2)}) async-start(bf16[32,2,128]{2,1,0:T(2,128)(2,1)} %bitcast.8), calls=%async_computation.1 | async-start | bytes 32768 | tf_op jit(solution)/shard_map/all_to_all | solution.py:65
  54.8 16.7 %all-to-all-start.2 = ((f32[32,2,128]{2,1,0:T(2,128)}), f32[32,2,128]{2,1,0:T(2,128)S(1)}, u32[]{:S(2)}, u32[]{:S(2)}) async-start(f32[32,2,128]{2,1,0:T(2,128)} %get-tuple-element.48), calls=%async_computation.2 | async-start | bytes 65536 | tf_op jit(solution)/shard_map/all_to_all | solution.py:84
  94.6 15.3 %collective-permute-start.6 = (bf16[16,128]{1,0:T(8,128)(2,1)S(1)}, bf16[16,128]{1,0:T(8,128)(2,1)S(1)}, u32[]{:S(2)}, u32[]{:S(2)}) collective-permute-start(bf16[16,128]{1,0:T(8,128)(2,1)S(1)} %slice.172), channel_id=1, source_target_pairs={{16,0},{32,16},{48,32},{64,48},{80,64},{96,80},{112,96},{128,112},... | collective-permute-start | bytes 12296 | tf_op jit(solution)/shard_map/ppermute | solution.py:13
  102.2 14.7 %all-to-all-start.3 = ((bf16[32,2,128]{2,1,0:T(2,128)(2,1)}), bf16[32,2,128]{2,1,0:T(2,128)(2,1)S(1)}, u32[]{:S(2)}, u32[]{:S(2)}) async-start(bf16[32,2,128]{2,1,0:T(2,128)(2,1)} %bitcast.27), calls=%async_computation.3 | async-start | bytes 32768 | tf_op jit(solution)/shard_map/all_to_all | solution.py:65
  107.1 28.7 %collective-permute-start.7 = (f32[16,128]{1,0:T(8,128)S(1)}, f32[16,128]{1,0:T(8,128)S(1)}, u32[]{:S(2)}, u32[]{:S(2)}) collective-permute-start(f32[16,128]{1,0:T(8,128)S(1)} %slice.175), channel_id=1, source_target_pairs={{0,16},{16,32},{32,48},{48,64},{64,80},{80,96},{96,112},{112,128},... | collective-permute-start | bytes 24584 | tf_op jit(solution)/shard_map/ppermute | solution.py:13
  118.8 16.8 %all-to-all-start.4 = ((f32[32,2,128]{2,1,0:T(2,128)}), f32[32,2,128]{2,1,0:T(2,128)S(1)}, u32[]{:S(2)}, u32[]{:S(2)}) async-start(f32[32,2,128]{2,1,0:T(2,128)} %get-tuple-element.44), calls=%async_computation.4 | async-start | bytes 65536 | tf_op jit(solution)/shard_map/all_to_all | solution.py:84
  158.7 15.4 %collective-permute-start.17 = (bf16[16,128]{1,0:T(8,128)(2,1)S(1)}, bf16[16,128]{1,0:T(8,128)(2,1)S(1)}, u32[]{:S(2)}, u32[]{:S(2)}) collective-permute-start(bf16[16,128]{1,0:T(8,128)(2,1)S(1)} %slice.177), channel_id=1, source_target_pairs={{16,0},{32,16},{48,32},{64,48},{80,64},{96,80},{112,96},{128,112},... | collective-permute-start | bytes 12296 | tf_op jit(solution)/shard_map/ppermute | solution.py:13
  166.3 14.7 %all-to-all-start.5 = ((bf16[32,2,128]{2,1,0:T(2,128)(2,1)}), bf16[32,2,128]{2,1,0:T(2,128)(2,1)S(1)}, u32[]{:S(2)}, u32[]{:S(2)}) async-start(bf16[32,2,128]{2,1,0:T(2,128)(2,1)} %bitcast.43), calls=%async_computation.5 | async-start | bytes 32768 | tf_op jit(solution)/shard_map/all_to_all | solution.py:65
  171.3 28.7 %collective-permute-start.18 = (f32[16,128]{1,0:T(8,128)S(1)}, f32[16,128]{1,0:T(8,128)S(1)}, u32[]{:S(2)}, u32[]{:S(2)}) collective-permute-start(f32[16,128]{1,0:T(8,128)S(1)} %slice.180), channel_id=1, source_target_pairs={{0,16},{16,32},{32,48},{48,64},{64,80},{80,96},{96,112},{112,128},... | collective-permute-start | bytes 24584 | tf_op jit(solution)/shard_map/ppermute | solution.py:13
  182.9 16.8 %all-to-all-start.6 = ((f32[32,2,128]{2,1,0:T(2,128)}), f32[32,2,128]{2,1,0:T(2,128)S(1)}, u32[]{:S(2)}, u32[]{:S(2)}) async-start(f32[32,2,128]{2,1,0:T(2,128)} %get-tuple-element.40), calls=%async_computation.6 | async-start | bytes 65536 | tf_op jit(solution)/shard_map/all_to_all | solution.py:84
  261.9 16.0 %collective-permute-start.27 = (f32[]{:T(128)}, f32[]{:T(128)}, u32[]{:S(2)}, u32[]{:S(2)}) collective-permute-start(f32[]{:T(128)} %add.428), channel_id=1, source_target_pairs={{0,256},{16,272},{32,288},{48,304},{64,320},{80,336},{96,352},{112... | collective-permute-start | bytes 20 | tf_op jit(solution)/shard_map/ppermute | solution.py:22
  265.3 13.3 %collective-permute-start.16 = (f32[]{:T(128)}, f32[]{:T(128)}, u32[]{:S(2)}, u32[]{:S(2)}) collective-permute-start(f32[]{:T(128)} %add.414), channel_id=1, source_target_pairs={{0,256},{16,272},{32,288},{48,304},{64,320},{80,336},{96,352},{112... | collective-permute-start | bytes 20 | tf_op jit(solution)/shard_map/ppermute | solution.py:22
  326.3 24.1 %collective-permute-start.33 = (bf16[16,128]{1,0:T(8,128)(2,1)S(1)}, bf16[16,128]{1,0:T(8,128)(2,1)S(1)}, u32[]{:S(2)}, u32[]{:S(2)}) collective-permute-start(bf16[16,128]{1,0:T(8,128)(2,1)S(1)} %slice.182), channel_id=1, source_target_pairs={{16,0},{32,16},{48,32},{64,48},{80,64},{96,80},{112,96},{128,112},... | collective-permute-start | bytes 12296 | tf_op jit(solution)/shard_map/ppermute | solution.py:13
  333.8 23.6 %all-to-all-start.7 = ((bf16[32,2,128]{2,1,0:T(2,128)(2,1)}), bf16[32,2,128]{2,1,0:T(2,128)(2,1)S(1)}, u32[]{:S(2)}, u32[]{:S(2)}) async-start(bf16[32,2,128]{2,1,0:T(2,128)(2,1)} %bitcast.59), calls=%async_computation.7 | async-start | bytes 32768 | tf_op jit(solution)/shard_map/all_to_all | solution.py:65
  346.9 29.4 %collective-permute-start.34 = (f32[16,128]{1,0:T(8,128)S(1)}, f32[16,128]{1,0:T(8,128)S(1)}, u32[]{:S(2)}, u32[]{:S(2)}) collective-permute-start(f32[16,128]{1,0:T(8,128)S(1)} %slice.185), channel_id=1, source_target_pairs={{0,16},{16,32},{32,48},{48,64},{64,80},{80,96},{96,112},{112,128},... | collective-permute-start | bytes 24584 | tf_op jit(solution)/shard_map/ppermute | solution.py:13
  359.2 16.8 %all-to-all-start.8 = ((f32[32,2,128]{2,1,0:T(2,128)}), f32[32,2,128]{2,1,0:T(2,128)S(1)}, u32[]{:S(2)}, u32[]{:S(2)}) async-start(f32[32,2,128]{2,1,0:T(2,128)} %get-tuple-element.36), calls=%async_computation.8 | async-start | bytes 65536 | tf_op jit(solution)/shard_map/all_to_all | solution.py:84
  442.6 15.2 %collective-permute-start.44 = (bf16[16,128]{1,0:T(8,128)(2,1)S(1)}, bf16[16,128]{1,0:T(8,128)(2,1)S(1)}, u32[]{:S(2)}, u32[]{:S(2)}) collective-permute-start(bf16[16,128]{1,0:T(8,128)(2,1)S(1)} %slice.187), channel_id=1, source_target_pairs={{16,0},{32,16},{48,32},{64,48},{80,64},{96,80},{112,96},{128,112},... | collective-permute-start | bytes 12296 | tf_op jit(solution)/shard_map/ppermute | solution.py:13
  450.1 14.7 %all-to-all-start.9 = ((bf16[32,2,128]{2,1,0:T(2,128)(2,1)}), bf16[32,2,128]{2,1,0:T(2,128)(2,1)S(1)}, u32[]{:S(2)}, u32[]{:S(2)}) async-start(bf16[32,2,128]{2,1,0:T(2,128)(2,1)} %bitcast.75), calls=%async_computation.9 | async-start | bytes 32768 | tf_op jit(solution)/shard_map/all_to_all | solution.py:65
  455.1 28.7 %collective-permute-start.45 = (f32[16,128]{1,0:T(8,128)S(1)}, f32[16,128]{1,0:T(8,128)S(1)}, u32[]{:S(2)}, u32[]{:S(2)}) collective-permute-start(f32[16,128]{1,0:T(8,128)S(1)} %slice.190), channel_id=1, source_target_pairs={{0,16},{16,32},{32,48},{48,64},{64,80},{80,96},{96,112},{112,128},... | collective-permute-start | bytes 24584 | tf_op jit(solution)/shard_map/ppermute | solution.py:13
  466.7 16.8 %all-to-all-start.10 = ((f32[32,2,128]{2,1,0:T(2,128)}), f32[32,2,128]{2,1,0:T(2,128)S(1)}, u32[]{:S(2)}, u32[]{:S(2)}) async-start(f32[32,2,128]{2,1,0:T(2,128)} %get-tuple-element.32), calls=%async_computation.10 | async-start | bytes 65536 | tf_op jit(solution)/shard_map/all_to_all | solution.py:84
  506.6 15.4 %collective-permute-start.55 = (bf16[16,128]{1,0:T(8,128)(2,1)S(1)}, bf16[16,128]{1,0:T(8,128)(2,1)S(1)}, u32[]{:S(2)}, u32[]{:S(2)}) collective-permute-start(bf16[16,128]{1,0:T(8,128)(2,1)S(1)} %slice.192), channel_id=1, source_target_pairs={{16,0},{32,16},{48,32},{64,48},{80,64},{96,80},{112,96},{128,112},... | collective-permute-start | bytes 12296 | tf_op jit(solution)/shard_map/ppermute | solution.py:13
  514.3 14.7 %all-to-all-start.11 = ((bf16[32,2,128]{2,1,0:T(2,128)(2,1)}), bf16[32,2,128]{2,1,0:T(2,128)(2,1)S(1)}, u32[]{:S(2)}, u32[]{:S(2)}) async-start(bf16[32,2,128]{2,1,0:T(2,128)(2,1)} %bitcast.91), calls=%async_computation.11 | async-start | bytes 32768 | tf_op jit(solution)/shard_map/all_to_all | solution.py:65
  519.2 28.7 %collective-permute-start.56 = (f32[16,128]{1,0:T(8,128)S(1)}, f32[16,128]{1,0:T(8,128)S(1)}, u32[]{:S(2)}, u32[]{:S(2)}) collective-permute-start(f32[16,128]{1,0:T(8,128)S(1)} %slice.195), channel_id=1, source_target_pairs={{0,16},{16,32},{32,48},{48,64},{64,80},{80,96},{96,112},{112,128},... | collective-permute-start | bytes 24584 | tf_op jit(solution)/shard_map/ppermute | solution.py:13
  530.9 16.8 %all-to-all-start.12 = ((f32[32,2,128]{2,1,0:T(2,128)}), f32[32,2,128]{2,1,0:T(2,128)S(1)}, u32[]{:S(2)}, u32[]{:S(2)}) async-start(f32[32,2,128]{2,1,0:T(2,128)} %get-tuple-element.28), calls=%async_computation.12 | async-start | bytes 65536 | tf_op jit(solution)/shard_map/all_to_all | solution.py:84
  609.8 16.0 %collective-permute-start.65 = (f32[]{:T(128)}, f32[]{:T(128)}, u32[]{:S(2)}, u32[]{:S(2)}) collective-permute-start(f32[]{:T(128)} %add.476), channel_id=1, source_target_pairs={{0,256},{16,272},{32,288},{48,304},{64,320},{80,336},{96,352},{112... | collective-permute-start | bytes 20 | tf_op jit(solution)/shard_map/ppermute | solution.py:22
  674.3 24.1 %collective-permute-start.71 = (bf16[16,128]{1,0:T(8,128)(2,1)S(1)}, bf16[16,128]{1,0:T(8,128)(2,1)S(1)}, u32[]{:S(2)}, u32[]{:S(2)}) collective-permute-start(bf16[16,128]{1,0:T(8,128)(2,1)S(1)} %slice.197), channel_id=1, source_target_pairs={{16,0},{32,16},{48,32},{64,48},{80,64},{96,80},{112,96},{128,112},... | collective-permute-start | bytes 12296 | tf_op jit(solution)/shard_map/ppermute | solution.py:13
  681.7 23.6 %all-to-all-start.13 = ((bf16[32,2,128]{2,1,0:T(2,128)(2,1)}), bf16[32,2,128]{2,1,0:T(2,128)(2,1)S(1)}, u32[]{:S(2)}, u32[]{:S(2)}) async-start(bf16[32,2,128]{2,1,0:T(2,128)(2,1)} %bitcast.107), calls=%async_computation.13 | async-start | bytes 32768 | tf_op jit(solution)/shard_map/all_to_all | solution.py:65
  694.9 29.4 %collective-permute-start.72 = (f32[16,128]{1,0:T(8,128)S(1)}, f32[16,128]{1,0:T(8,128)S(1)}, u32[]{:S(2)}, u32[]{:S(2)}) collective-permute-start(f32[16,128]{1,0:T(8,128)S(1)} %slice.200), channel_id=1, source_target_pairs={{0,16},{16,32},{32,48},{48,64},{64,80},{80,96},{96,112},{112,128},... | collective-permute-start | bytes 24584 | tf_op jit(solution)/shard_map/ppermute | solution.py:13
  707.2 16.8 %all-to-all-start.14 = ((f32[32,2,128]{2,1,0:T(2,128)}), f32[32,2,128]{2,1,0:T(2,128)S(1)}, u32[]{:S(2)}, u32[]{:S(2)}) async-start(f32[32,2,128]{2,1,0:T(2,128)} %get-tuple-element.24), calls=%async_computation.14 | async-start | bytes 65536 | tf_op jit(solution)/shard_map/all_to_all | solution.py:84
  (67 other events, 545.0 us)

commit v2 on v0

--- a/solution.py
+++ b/solution.py
@@ -11,6 +11,12 @@
     count = lax.axis_size(axis)
     leading, last = (max(0, -steps), min(count, count - steps))
     return lax.ppermute(value, axis, [(source, source + steps) for source in range(leading, last)])
+
+
+def all_sum(value, axis):
+    count = lax.axis_size(axis)
+    copies = jnp.broadcast_to(value[None], (count,) + value.shape)
+    return jnp.sum(lax.all_to_all(copies, axis, 0, 0, tiled=True), 0)
 
 
 def on_device(band_blocks, distant_block_slots, far_rows, far_columns, far_counts):
@@ -50,8 +56,21 @@
         spread = lax.dynamic_update_slice_in_dim(
             jnp.zeros((rows_dev + band_count, block_size), jnp.float32), backward, offset, 0
         )
-        outgoing = narrow_band_part[wanted]
-        gathered_values = lax.all_to_all(outgoing, "row", split_axis=0, concat_axis=0, tiled=True)
+        outgoing = narrow_band_part[wanted].astype(jnp.float32)
+        far_backward = (
+            jnp.einsum(
+                "nquo,nqu->nqo",
+                distant_local_part,
+                narrow_band_part[local_row_values],
+                preferred_element_type=jnp.float32,
+            )
+            * live_mask
+        )
+        exchanged = lax.all_to_all(
+            jnp.concatenate([outgoing, far_backward], 1), "row", split_axis=0, concat_axis=0, tiled=True
+        )
+        gathered_values = exchanged[:, :slots].astype(jnp.bfloat16)
+        returned = exchanged[:, slots:]
         far_forward = (
             jnp.einsum(
                 "oqht,oqt->oqh",
@@ -61,16 +80,6 @@
             )
             * live_mask
         )
-        far_backward = (
-            jnp.einsum(
-                "nquo,nqu->nqo",
-                distant_local_part,
-                narrow_band_part[local_row_values],
-                preferred_element_type=jnp.float32,
-            )
-            * live_mask
-        )
-        returned = lax.all_to_all(far_backward, "row", split_axis=0, concat_axis=0, tiled=True)
         summed = forward + spread[:rows_dev]
         summed = summed + jnp.dot(
             pick_in.T, far_forward.reshape(-1, block_size), precision=lax.Precision.HIGHEST
@@ -80,7 +89,7 @@
         )
         carried = shifted(spread[rows_dev:], "row", 1)
         summed = jnp.concatenate([summed[:band_count] + carried, summed[band_count:]], 0)
-        return lax.psum(summed, "band")
+        return all_sum(summed, "band")
 
     row_sums = multiply(jnp.ones((rows_dev, block_size), jnp.float32))
     scaling = 1.0 / jnp.sqrt(row_sums)
@@ -90,17 +99,22 @@
         residual = 1.0 - balance
         scaled = residual / balance
         direction = scaled
-        current_residual_product = lax.psum(jnp.sum(residual * scaled), "row")
+        local_product = jnp.sum(residual * scaled)
         growth = jnp.ones_like(scaling)
         for inner_step in range(INNER):
             curved = scaling * multiply(scaling * direction) + balance * direction
-            curvature = lax.psum(jnp.sum(direction * curved), "row")
+            local_curvature = jnp.sum(direction * curved)
+            if inner_step == 0:
+                totals = all_sum(jnp.stack([local_product, local_curvature]), "row")
+                current_residual_product, curvature = totals[0], totals[1]
+            else:
+                curvature = all_sum(local_curvature[None], "row")[0]
             step_size = current_residual_product / curvature
             growth = growth + step_size * direction
             residual = residual - step_size * curved
             if inner_step + 1 < INNER:
                 scaled = residual / balance
-                rho_next = lax.psum(jnp.sum(residual * scaled), "row")
+                rho_next = all_sum(jnp.sum(residual * scaled)[None], "row")[0]
                 direction = scaled + rho_next / current_residual_product * direction
                 current_residual_product = rho_next
         scaling = scaling * growth

time: 1090 us -> 410 us (0.38)
  blocking collectives: 731 us -> 176 us
  waiting for transfers between devices: 132 us -> 62.2 us
  starting transfers between devices: 159 us -> 97.9 us
    psum x13 -> x0, blocking collectives: 731 us -> none  [the longest x7 396 us: multiply(): return lax.psum(summed, 'band')]
    all_to_all x0 -> x13, blocking collectives: none -> 176 us  [all_sum(): return jnp.sum(lax.all_to_all(copies, axis, 0, 0, tiled=True), 0)]
    all_to_all x14 -> x7, waiting for transfers between devices: 128 us -> 59.6 us  [multiply(): lax.all_to_all(jnp.concatenate([outgoing, far_backward], 1), 'row', split...]
    ppermute x14, starting transfers between devices: 87.9 us -> 48.6 us  [shifted(): lax.ppermute(value, axis, [(source, source + steps) for source in range(l...]
    all_to_all x14 -> x7, starting transfers between devices: 60.9 us -> 32.5 us  [multiply(): lax.all_to_all(jnp.concatenate([outgoing, far_backward], 1), 'row', split...]
  transfers between devices with their start and end apart: 29 -> 22, of which waited for: 15 -> 8; matrix products, arithmetic and copies ran while one was open for 4% -> 10% of each run, Pallas kernels for 0% -> 0%
where the time goes in v2:
time: 410 us; the launch traced here: 408 us
  blocking collectives  176 us (43%)
  starting transfers between devices  97.9 us (24%)
  waiting for transfers between devices  62.2 us (15%)
  matrix products  25 us (6%)
  other arithmetic  19.1 us (5%)
  local copies, waits for them, and re-layouts  18 us (4%)
  between operations  9.92 us (2%)
    all_to_all x13, blocking collectives, all_sum(): return jnp.sum(lax.all_to_all(copies, axis, 0, 0, tiled=True), 0)  176 us
    all_to_all x7, waiting for transfers between devices, multiply(): lax.all_to_all(jnp.concatenate([outgoing, far_backward], 1), 'row', split...  59.6 us
    ppermute x14, starting transfers between devices, shifted(): lax.ppermute(value, axis, [(source, source + steps) for source in range(l...  48.6 us
    all_to_all x7, starting transfers between devices, multiply(): lax.all_to_all(jnp.concatenate([outgoing, far_backward], 1), 'row', split...  32.5 us
    all_to_all x1, starting transfers between devices, on_device(): lax.all_to_all(columns_local, 'row', split_axis=0, concat_axis=0, tiled=T...  16.7 us
    dot_general x7, matrix products, multiply(): jnp.einsum('oqht,oqt->oqh', distant_local_part, gathered_values, preferre...  8.22 us
  transfers between devices with their start and end apart: 22, of which 8 were waited for; matrix products, arithmetic and copies ran while one was open for 10% of the time, Pallas kernels for 0%

profile of v2, /device:TPU:1, one launch (start us, length us, event | category | flops | bytes accessed | tf_op | source)
XLA Modules:
  0.0 408.0 jit_solution(1473980373645884220)
XLA Ops:
  2.2 16.7 %all-to-all-start = ((s32[32,1,2]{2,1,0:T(1,128)}), s32[32,1,2]{2,1,0:T(1,128)S(1)}, u32[]{:S(2)}, u32[]{:S(2)}) async-start(s32[32,1,2]{2,1,0:T(1,128)} %copy.26), calls=%async_computation | async-start | bytes 32768 | tf_op jit(solution)/shard_map/all_to_all | solution.py:39
  34.6 9.4 %all-to-all-start.1 = ((f32[32,4,128]{2,1,0:T(4,128)}), f32[32,4,128]{2,1,0:T(4,128)S(1)}, u32[]{:S(2)}, u32[]{:S(2)}) async-start(f32[32,4,128]{2,1,0:T(4,128)} %pad_maximum_fusion), calls=%async_computation.1 | async-start | bytes 131072 | tf_op jit(solution)/shard_map/all_to_all | solution.py:69
  45.9 11.0 %all-to-all-done.1 = f32[32,4,128]{2,1,0:T(4,128)S(1)} async-done(((f32[32,4,128]{2,1,0:T(4,128)}), f32[32,4,128]{2,1,0:T(4,128)S(1)}, u32[]{:S(2)}, u32[]{:S(2)}) %all-to-all-start.1) | async-done | bytes 65568 | tf_op jit(solution)/shard_map/all_to_all | solution.py:69
  58.9 14.1 %all_to_all.118 = f32[16,32,128]{2,1,0:T(8,128)S(1)} all-to-all(f32[16,32,128]{2,1,0:T(8,128)S(1)} %broadcast_in_dim.26), channel_id=1, replica_groups=mesh['row'=32,'band'=16] {'band'}, dimensions={0} | all-to-all | bytes 524288 | tf_op jit(solution)/shard_map/all_to_all | solution.py:19
  74.3 4.9 %collective-permute-start.2 = (bf16[16,128]{1,0:T(8,128)(2,1)S(1)}, bf16[16,128]{1,0:T(8,128)(2,1)S(1)}, u32[]{:S(2)}, u32[]{:S(2)}) collective-permute-start(bf16[16,128]{1,0:T(8,128)(2,1)S(1)} %slice.253), channel_id=1, source_target_pairs={{16,0},{32,16},{48,32},{64,48},{80,64},{96,80},{112,96},{128,112},... | collective-permute-start | bytes 12296 | tf_op jit(solution)/shard_map/ppermute | solution.py:13
  80.7 3.6 all-to-all-start.3
  88.9 8.2 %all-to-all-done.3 = f32[32,4,128]{2,1,0:T(4,128)S(1)} async-done(((f32[32,4,128]{2,1,0:T(4,128)}), f32[32,4,128]{2,1,0:T(4,128)S(1)}, u32[]{:S(2)}, u32[]{:S(2)}) %all-to-all-start.3) | async-done | bytes 65568 | tf_op jit(solution)/shard_map/all_to_all | solution.py:69
  99.0 10.3 %all_to_all.119 = f32[16,32,128]{2,1,0:T(8,128)S(1)} all-to-all(f32[16,32,128]{2,1,0:T(8,128)S(1)} %broadcast_in_dim.27), channel_id=1, replica_groups=mesh['row'=32,'band'=16] {'band'}, dimensions={0} | all-to-all | bytes 524288 | tf_op jit(solution)/shard_map/all_to_all | solution.py:19
  110.6 4.6 %collective-permute-start.4 = (bf16[16,128]{1,0:T(8,128)(2,1)S(1)}, bf16[16,128]{1,0:T(8,128)(2,1)S(1)}, u32[]{:S(2)}, u32[]{:S(2)}) collective-permute-start(bf16[16,128]{1,0:T(8,128)(2,1)S(1)} %slice.260), channel_id=1, source_target_pairs={{16,0},{32,16},{48,32},{64,48},{80,64},{96,80},{112,96},{128,112},... | collective-permute-start | bytes 12296 | tf_op jit(solution)/shard_map/ppermute | solution.py:13
  116.6 3.6 all-to-all-start.5
  124.8 8.0 %all-to-all-done.5 = f32[32,4,128]{2,1,0:T(4,128)S(1)} async-done(((f32[32,4,128]{2,1,0:T(4,128)}), f32[32,4,128]{2,1,0:T(4,128)S(1)}, u32[]{:S(2)}, u32[]{:S(2)}) %all-to-all-start.5) | async-done | bytes 65568 | tf_op jit(solution)/shard_map/all_to_all | solution.py:69
  134.8 10.3 %all_to_all.120 = f32[16,32,128]{2,1,0:T(8,128)S(1)} all-to-all(f32[16,32,128]{2,1,0:T(8,128)S(1)} %broadcast_in_dim.28), channel_id=1, replica_groups=mesh['row'=32,'band'=16] {'band'}, dimensions={0} | all-to-all | bytes 524288 | tf_op jit(solution)/shard_map/all_to_all | solution.py:19
  147.1 17.3 %all_to_all.121 = f32[32,1,2]{2,1,0:T(1,128)S(1)} all-to-all(f32[32,1,2]{2,1,0:T(1,128)S(1)} %broadcast_in_dim.29), channel_id=1, replica_groups=mesh['row'=32,'band'=16] {'row'}, dimensions={0} | all-to-all | bytes 512 | tf_op jit(solution)/shard_map/all_to_all | solution.py:19
  167.6 15.4 %all_to_all.122 = f32[32,1,1]{2,1,0:T(1,128)S(1)} all-to-all(f32[32,1,1]{2,1,0:T(1,128)S(1)} %broadcast_in_dim.30), channel_id=1, replica_groups=mesh['row'=32,'band'=16] {'row'}, dimensions={0} | all-to-all | bytes 256 | tf_op jit(solution)/shard_map/all_to_all | solution.py:19
  190.8 4.1 %all-to-all-start.9 = ((f32[32,4,128]{2,1,0:T(4,128)}), f32[32,4,128]{2,1,0:T(4,128)S(1)}, u32[]{:S(2)}, u32[]{:S(2)}) async-start(f32[32,4,128]{2,1,0:T(4,128)} %pad_maximum_fusion.3), calls=%async_computation.9 | async-start | bytes 131072 | tf_op jit(solution)/shard_map/all_to_all | solution.py:69
  195.5 3.5 collective-permute-start.7
  199.8 8.1 %all-to-all-done.9 = f32[32,4,128]{2,1,0:T(4,128)S(1)} async-done(((f32[32,4,128]{2,1,0:T(4,128)}), f32[32,4,128]{2,1,0:T(4,128)S(1)}, u32[]{:S(2)}, u32[]{:S(2)}) %all-to-all-start.9) | async-done | bytes 65568 | tf_op jit(solution)/shard_map/all_to_all | solution.py:69
  209.8 10.2 %all_to_all.123 = f32[16,32,128]{2,1,0:T(8,128)S(1)} all-to-all(f32[16,32,128]{2,1,0:T(8,128)S(1)} %broadcast_in_dim.31), channel_id=1, replica_groups=mesh['row'=32,'band'=16] {'band'}, dimensions={0} | all-to-all | bytes 524288 | tf_op jit(solution)/shard_map/all_to_all | solution.py:19
  221.3 17.5 %all_to_all.124 = f32[32,1,1]{2,1,0:T(1,128)S(1)} all-to-all(f32[32,1,1]{2,1,0:T(1,128)S(1)} %broadcast_in_dim.32), channel_id=1, replica_groups=mesh['row'=32,'band'=16] {'row'}, dimensions={0} | all-to-all | bytes 256 | tf_op jit(solution)/shard_map/all_to_all | solution.py:19
  246.4 4.1 %all-to-all-start.12 = ((f32[32,4,128]{2,1,0:T(4,128)}), f32[32,4,128]{2,1,0:T(4,128)S(1)}, u32[]{:S(2)}, u32[]{:S(2)}) async-start(f32[32,4,128]{2,1,0:T(4,128)} %pad_maximum_fusion.4), calls=%async_computation.12 | async-start | bytes 131072 | tf_op jit(solution)/shard_map/all_to_all | solution.py:69
  255.4 8.1 %all-to-all-done.12 = f32[32,4,128]{2,1,0:T(4,128)S(1)} async-done(((f32[32,4,128]{2,1,0:T(4,128)}), f32[32,4,128]{2,1,0:T(4,128)S(1)}, u32[]{:S(2)}, u32[]{:S(2)}) %all-to-all-start.12) | async-done | bytes 65568 | tf_op jit(solution)/shard_map/all_to_all | solution.py:69
  265.5 10.2 %all_to_all.125 = f32[16,32,128]{2,1,0:T(8,128)S(1)} all-to-all(f32[16,32,128]{2,1,0:T(8,128)S(1)} %broadcast_in_dim.33), channel_id=1, replica_groups=mesh['row'=32,'band'=16] {'band'}, dimensions={0} | all-to-all | bytes 524288 | tf_op jit(solution)/shard_map/all_to_all | solution.py:19
  277.0 4.9 %collective-permute-start.10 = (bf16[16,128]{1,0:T(8,128)(2,1)S(1)}, bf16[16,128]{1,0:T(8,128)(2,1)S(1)}, u32[]{:S(2)}, u32[]{:S(2)}) collective-permute-start(bf16[16,128]{1,0:T(8,128)(2,1)S(1)} %slice.281), channel_id=1, source_target_pairs={{16,0},{32,16},{48,32},{64,48},{80,64},{96,80},{112,96},{128,112},... | collective-permute-start | bytes 12296 | tf_op jit(solution)/shard_map/ppermute | solution.py:13
  283.3 3.6 all-to-all-start.14
  291.5 8.2 %all-to-all-done.14 = f32[32,4,128]{2,1,0:T(4,128)S(1)} async-done(((f32[32,4,128]{2,1,0:T(4,128)}), f32[32,4,128]{2,1,0:T(4,128)S(1)}, u32[]{:S(2)}, u32[]{:S(2)}) %all-to-all-start.14) | async-done | bytes 65568 | tf_op jit(solution)/shard_map/all_to_all | solution.py:69
  301.6 10.3 %all_to_all.126 = f32[16,32,128]{2,1,0:T(8,128)S(1)} all-to-all(f32[16,32,128]{2,1,0:T(8,128)S(1)} %broadcast_in_dim.34), channel_id=1, replica_groups=mesh['row'=32,'band'=16] {'band'}, dimensions={0} | all-to-all | bytes 524288 | tf_op jit(solution)/shard_map/all_to_all | solution.py:19
  313.9 17.3 %all_to_all.127 = f32[32,1,2]{2,1,0:T(1,128)S(1)} all-to-all(f32[32,1,2]{2,1,0:T(1,128)S(1)} %broadcast_in_dim.35), channel_id=1, replica_groups=mesh['row'=32,'band'=16] {'row'}, dimensions={0} | all-to-all | bytes 512 | tf_op jit(solution)/shard_map/all_to_all | solution.py:19
  334.4 15.4 %all_to_all.128 = f32[32,1,1]{2,1,0:T(1,128)S(1)} all-to-all(f32[32,1,1]{2,1,0:T(1,128)S(1)} %broadcast_in_dim.36), channel_id=1, replica_groups=mesh['row'=32,'band'=16] {'row'}, dimensions={0} | all-to-all | bytes 256 | tf_op jit(solution)/shard_map/all_to_all | solution.py:19
  357.3 4.1 %all-to-all-start.18 = ((f32[32,4,128]{2,1,0:T(4,128)}), f32[32,4,128]{2,1,0:T(4,128)S(1)}, u32[]{:S(2)}, u32[]{:S(2)}) async-start(f32[32,4,128]{2,1,0:T(4,128)} %pad_maximum_fusion.6), calls=%async_computation.18 | async-start | bytes 131072 | tf_op jit(solution)/shard_map/all_to_all | solution.py:69
  366.3 8.1 %all-to-all-done.18 = f32[32,4,128]{2,1,0:T(4,128)S(1)} async-done(((f32[32,4,128]{2,1,0:T(4,128)}), f32[32,4,128]{2,1,0:T(4,128)S(1)}, u32[]{:S(2)}, u32[]{:S(2)}) %all-to-all-start.18) | async-done | bytes 65568 | tf_op jit(solution)/shard_map/all_to_all | solution.py:69
  376.4 10.2 %all_to_all.129 = f32[16,32,128]{2,1,0:T(8,128)S(1)} all-to-all(f32[16,32,128]{2,1,0:T(8,128)S(1)} %broadcast_in_dim.37), channel_id=1, replica_groups=mesh['row'=32,'band'=16] {'band'}, dimensions={0} | all-to-all | bytes 524288 | tf_op jit(solution)/shard_map/all_to_all | solution.py:19
  387.9 17.5 %all_to_all.130 = f32[32,1,1]{2,1,0:T(1,128)S(1)} all-to-all(f32[32,1,1]{2,1,0:T(1,128)S(1)} %broadcast_in_dim.38), channel_id=1, replica_groups=mesh['row'=32,'band'=16] {'row'}, dimensions={0} | all-to-all | bytes 256 | tf_op jit(solution)/shard_map/all_to_all | solution.py:19
  (245 shorter events, 95.3 us)
Async XLA Ops:
  0.6 32.5 %copy-start = (bf16[1,1,32,2,128,128]{5,4,3,2,1,0:T(8,128)(2,1)S(1)}, bf16[1,1,32,2,128,128]{5,4,3,2,1,0:T(8,128)(2,1)}, u32[]{:S(2)}) copy-start(bf16[1,1,32,2,128,128]{5,4,3,2,1,0:T(8,128)(2,1)} %param.6) | copy-start | bytes 6291460
  2.2 28.5 %all-to-all-start = ((s32[32,1,2]{2,1,0:T(1,128)}), s32[32,1,2]{2,1,0:T(1,128)S(1)}, u32[]{:S(2)}, u32[]{:S(2)}) async-start(s32[32,1,2]{2,1,0:T(1,128)} %copy.26), calls=%async_computation | async-start | bytes 32768 | tf_op jit(solution)/shard_map/all_to_all | solution.py:39
  18.9 26.3 %collective-permute-start = (bf16[16,128]{1,0:T(8,128)(2,1)S(1)}, bf16[16,128]{1,0:T(8,128)(2,1)S(1)}, u32[]{:S(2)}, u32[]{:S(2)}) collective-permute-start(bf16[16,128]{1,0:T(8,128)(2,1)S(1)} %slice.166), channel_id=1, source_target_pairs={{16,0},{32,16},{48,32},{64,48},{80,64},{96,80},{112,96},{128,112},... | collective-permute-start | bytes 12296 | tf_op jit(solution)/shard_map/ppermute | solution.py:13
  21.1 24.2 %copy-start.1 = (bf16[32,1,128,128]{3,2,1,0:T(8,128)(2,1)S(1)}, bf16[32,1,128,128]{3,2,1,0:T(8,128)(2,1)}, u32[]{:S(2)}) copy-start(bf16[32,1,128,128]{3,2,1,0:T(8,128)(2,1)} %param.5) | copy-start | bytes 3145732
  23.1 35.8 %collective-permute-start.1 = (f32[16,128]{1,0:T(8,128)S(1)}, f32[16,128]{1,0:T(8,128)S(1)}, u32[]{:S(2)}, u32[]{:S(2)}) collective-permute-start(f32[16,128]{1,0:T(8,128)S(1)} %slice.251), channel_id=1, source_target_pairs={{0,16},{16,32},{32,48},{48,64},{64,80},{80,96},{96,112},{112,128},... | collective-permute-start | bytes 24584 | tf_op jit(solution)/shard_map/ppermute | solution.py:13
  34.6 22.4 %all-to-all-start.1 = ((f32[32,4,128]{2,1,0:T(4,128)}), f32[32,4,128]{2,1,0:T(4,128)S(1)}, u32[]{:S(2)}, u32[]{:S(2)}) async-start(f32[32,4,128]{2,1,0:T(4,128)} %pad_maximum_fusion), calls=%async_computation.1 | async-start | bytes 131072 | tf_op jit(solution)/shard_map/all_to_all | solution.py:69
  74.3 13.8 %collective-permute-start.2 = (bf16[16,128]{1,0:T(8,128)(2,1)S(1)}, bf16[16,128]{1,0:T(8,128)(2,1)S(1)}, u32[]{:S(2)}, u32[]{:S(2)}) collective-permute-start(bf16[16,128]{1,0:T(8,128)(2,1)S(1)} %slice.253), channel_id=1, source_target_pairs={{16,0},{32,16},{48,32},{64,48},{80,64},{96,80},{112,96},{128,112},... | collective-permute-start | bytes 12296 | tf_op jit(solution)/shard_map/ppermute | solution.py:13
  80.7 16.3 %all-to-all-start.3 = ((f32[32,4,128]{2,1,0:T(4,128)}), f32[32,4,128]{2,1,0:T(4,128)S(1)}, u32[]{:S(2)}, u32[]{:S(2)}) async-start(f32[32,4,128]{2,1,0:T(4,128)} %pad_maximum_fusion.1), calls=%async_computation.3 | async-start | bytes 131072 | tf_op jit(solution)/shard_map/all_to_all | solution.py:69
  85.0 13.9 %collective-permute-start.3 = (f32[16,128]{1,0:T(8,128)S(1)}, f32[16,128]{1,0:T(8,128)S(1)}, u32[]{:S(2)}, u32[]{:S(2)}) collective-permute-start(f32[16,128]{1,0:T(8,128)S(1)} %slice.258), channel_id=1, source_target_pairs={{0,16},{16,32},{32,48},{48,64},{64,80},{80,96},{96,112},{112,128},... | collective-permute-start | bytes 24584 | tf_op jit(solution)/shard_map/ppermute | solution.py:13
  110.6 13.5 %collective-permute-start.4 = (bf16[16,128]{1,0:T(8,128)(2,1)S(1)}, bf16[16,128]{1,0:T(8,128)(2,1)S(1)}, u32[]{:S(2)}, u32[]{:S(2)}) collective-permute-start(bf16[16,128]{1,0:T(8,128)(2,1)S(1)} %slice.260), channel_id=1, source_target_pairs={{16,0},{32,16},{48,32},{64,48},{80,64},{96,80},{112,96},{128,112},... | collective-permute-start | bytes 12296 | tf_op jit(solution)/shard_map/ppermute | solution.py:13
  116.6 16.2 %all-to-all-start.5 = ((f32[32,4,128]{2,1,0:T(4,128)}), f32[32,4,128]{2,1,0:T(4,128)S(1)}, u32[]{:S(2)}, u32[]{:S(2)}) async-start(f32[32,4,128]{2,1,0:T(4,128)} %pad_maximum_fusion.2), calls=%async_computation.5 | async-start | bytes 131072 | tf_op jit(solution)/shard_map/all_to_all | solution.py:69
  120.9 13.8 %collective-permute-start.5 = (f32[16,128]{1,0:T(8,128)S(1)}, f32[16,128]{1,0:T(8,128)S(1)}, u32[]{:S(2)}, u32[]{:S(2)}) collective-permute-start(f32[16,128]{1,0:T(8,128)S(1)} %slice.265), channel_id=1, source_target_pairs={{0,16},{16,32},{32,48},{48,64},{64,80},{80,96},{96,112},{112,128},... | collective-permute-start | bytes 24584 | tf_op jit(solution)/shard_map/ppermute | solution.py:13
  186.3 12.7 %collective-permute-start.6 = (bf16[16,128]{1,0:T(8,128)(2,1)S(1)}, bf16[16,128]{1,0:T(8,128)(2,1)S(1)}, u32[]{:S(2)}, u32[]{:S(2)}) collective-permute-start(bf16[16,128]{1,0:T(8,128)(2,1)S(1)} %slice.267), channel_id=1, source_target_pairs={{16,0},{32,16},{48,32},{64,48},{80,64},{96,80},{112,96},{128,112},... | collective-permute-start | bytes 12296 | tf_op jit(solution)/shard_map/ppermute | solution.py:13
  190.8 17.1 %all-to-all-start.9 = ((f32[32,4,128]{2,1,0:T(4,128)}), f32[32,4,128]{2,1,0:T(4,128)S(1)}, u32[]{:S(2)}, u32[]{:S(2)}) async-start(f32[32,4,128]{2,1,0:T(4,128)} %pad_maximum_fusion.3), calls=%async_computation.9 | async-start | bytes 131072 | tf_op jit(solution)/shard_map/all_to_all | solution.py:69
  195.5 14.2 %collective-permute-start.7 = (f32[16,128]{1,0:T(8,128)S(1)}, f32[16,128]{1,0:T(8,128)S(1)}, u32[]{:S(2)}, u32[]{:S(2)}) collective-permute-start(f32[16,128]{1,0:T(8,128)S(1)} %slice.272), channel_id=1, source_target_pairs={{0,16},{16,32},{32,48},{48,64},{64,80},{80,96},{96,112},{112,128},... | collective-permute-start | bytes 24584 | tf_op jit(solution)/shard_map/ppermute | solution.py:13
  242.2 12.5 %collective-permute-start.8 = (bf16[16,128]{1,0:T(8,128)(2,1)S(1)}, bf16[16,128]{1,0:T(8,128)(2,1)S(1)}, u32[]{:S(2)}, u32[]{:S(2)}) collective-permute-start(bf16[16,128]{1,0:T(8,128)(2,1)S(1)} %slice.274), channel_id=1, source_target_pairs={{16,0},{32,16},{48,32},{64,48},{80,64},{96,80},{112,96},{128,112},... | collective-permute-start | bytes 12296 | tf_op jit(solution)/shard_map/ppermute | solution.py:13
  246.4 17.1 %all-to-all-start.12 = ((f32[32,4,128]{2,1,0:T(4,128)}), f32[32,4,128]{2,1,0:T(4,128)S(1)}, u32[]{:S(2)}, u32[]{:S(2)}) async-start(f32[32,4,128]{2,1,0:T(4,128)} %pad_maximum_fusion.4), calls=%async_computation.12 | async-start | bytes 131072 | tf_op jit(solution)/shard_map/all_to_all | solution.py:69
  251.1 14.2 %collective-permute-start.9 = (f32[16,128]{1,0:T(8,128)S(1)}, f32[16,128]{1,0:T(8,128)S(1)}, u32[]{:S(2)}, u32[]{:S(2)}) collective-permute-start(f32[16,128]{1,0:T(8,128)S(1)} %slice.279), channel_id=1, source_target_pairs={{0,16},{16,32},{32,48},{48,64},{64,80},{80,96},{96,112},{112,128},... | collective-permute-start | bytes 24584 | tf_op jit(solution)/shard_map/ppermute | solution.py:13
  277.0 13.8 %collective-permute-start.10 = (bf16[16,128]{1,0:T(8,128)(2,1)S(1)}, bf16[16,128]{1,0:T(8,128)(2,1)S(1)}, u32[]{:S(2)}, u32[]{:S(2)}) collective-permute-start(bf16[16,128]{1,0:T(8,128)(2,1)S(1)} %slice.281), channel_id=1, source_target_pairs={{16,0},{32,16},{48,32},{64,48},{80,64},{96,80},{112,96},{128,112},... | collective-permute-start | bytes 12296 | tf_op jit(solution)/shard_map/ppermute | solution.py:13
  283.3 16.3 %all-to-all-start.14 = ((f32[32,4,128]{2,1,0:T(4,128)}), f32[32,4,128]{2,1,0:T(4,128)S(1)}, u32[]{:S(2)}, u32[]{:S(2)}) async-start(f32[32,4,128]{2,1,0:T(4,128)} %pad_maximum_fusion.5), calls=%async_computation.14 | async-start | bytes 131072 | tf_op jit(solution)/shard_map/all_to_all | solution.py:69
  287.6 13.9 %collective-permute-start.11 = (f32[16,128]{1,0:T(8,128)S(1)}, f32[16,128]{1,0:T(8,128)S(1)}, u32[]{:S(2)}, u32[]{:S(2)}) collective-permute-start(f32[16,128]{1,0:T(8,128)S(1)} %slice.286), channel_id=1, source_target_pairs={{0,16},{16,32},{32,48},{48,64},{64,80},{80,96},{96,112},{112,128},... | collective-permute-start | bytes 24584 | tf_op jit(solution)/shard_map/ppermute | solution.py:13
  353.1 12.5 %collective-permute-start.12 = (bf16[16,128]{1,0:T(8,128)(2,1)S(1)}, bf16[16,128]{1,0:T(8,128)(2,1)S(1)}, u32[]{:S(2)}, u32[]{:S(2)}) collective-permute-start(bf16[16,128]{1,0:T(8,128)(2,1)S(1)} %slice.288), channel_id=1, source_target_pairs={{16,0},{32,16},{48,32},{64,48},{80,64},{96,80},{112,96},{128,112},... | collective-permute-start | bytes 12296 | tf_op jit(solution)/shard_map/ppermute | solution.py:13
  357.3 17.1 %all-to-all-start.18 = ((f32[32,4,128]{2,1,0:T(4,128)}), f32[32,4,128]{2,1,0:T(4,128)S(1)}, u32[]{:S(2)}, u32[]{:S(2)}) async-start(f32[32,4,128]{2,1,0:T(4,128)} %pad_maximum_fusion.6), calls=%async_computation.18 | async-start | bytes 131072 | tf_op jit(solution)/shard_map/all_to_all | solution.py:69
  362.1 14.2 %collective-permute-start.13 = (f32[16,128]{1,0:T(8,128)S(1)}, f32[16,128]{1,0:T(8,128)S(1)}, u32[]{:S(2)}, u32[]{:S(2)}) collective-permute-start(f32[16,128]{1,0:T(8,128)S(1)} %slice.293), channel_id=1, source_target_pairs={{0,16},{16,32},{32,48},{48,64},{64,80},{80,96},{96,112},{112,128},... | collective-permute-start | bytes 24584 | tf_op jit(solution)/shard_map/ppermute | solution.py:13

commit v3 on v2

--- a/solution.py
+++ b/solution.py
@@ -103,18 +103,24 @@
         growth = jnp.ones_like(scaling)
         for inner_step in range(INNER):
             curved = scaling * multiply(scaling * direction) + balance * direction
-            local_curvature = jnp.sum(direction * curved)
+            last = inner_step + 1 == INNER
+            parts = [jnp.sum(direction * curved)]
             if inner_step == 0:
-                totals = all_sum(jnp.stack([local_product, local_curvature]), "row")
-                current_residual_product, curvature = totals[0], totals[1]
-            else:
-                curvature = all_sum(local_curvature[None], "row")[0]
+                parts.append(local_product)
+            if not last:
+                parts.append(jnp.sum(residual * curved / balance))
+                parts.append(jnp.sum(curved * curved / balance))
+            totals = all_sum(jnp.stack(parts), "row")
+            curvature = totals[0]
+            if inner_step == 0:
+                current_residual_product = totals[1]
             step_size = current_residual_product / curvature
             growth = growth + step_size * direction
             residual = residual - step_size * curved
-            if inner_step + 1 < INNER:
+            if not last:
+                cross, square = totals[-2], totals[-1]
+                rho_next = current_residual_product - 2.0 * step_size * cross + step_size * step_size * square
                 scaled = residual / balance
-                rho_next = all_sum(jnp.sum(residual * scaled)[None], "row")[0]
                 direction = scaled + rho_next / current_residual_product * direction
                 current_residual_product = rho_next
         scaling = scaling * growth

time: 410 us -> 379 us (0.924)
  blocking collectives: 176 us -> 145 us
    all_to_all x13 -> x11, blocking collectives: 176 us -> 145 us  [all_sum(): return jnp.sum(lax.all_to_all(copies, axis, 0, 0, tiled=True), 0)]
where the time goes in v3:
time: 379 us; the launch traced here: 377 us
  blocking collectives  145 us (38%)
  starting transfers between devices  97.7 us (26%)
  waiting for transfers between devices  62.2 us (16%)
  matrix products  25 us (7%)
  other arithmetic  19.3 us (5%)
  local copies, waits for them, and re-layouts  16.9 us (4%)
  between operations  10.7 us (3%)
    all_to_all x11, blocking collectives, all_sum(): return jnp.sum(lax.all_to_all(copies, axis, 0, 0, tiled=True), 0)  145 us
    all_to_all x7, waiting for transfers between devices, multiply(): lax.all_to_all(jnp.concatenate([outgoing, far_backward], 1), 'row', split...  59.6 us
    ppermute x14, starting transfers between devices, shifted(): lax.ppermute(value, axis, [(source, source + steps) for source in range(l...  48.4 us
    all_to_all x7, starting transfers between devices, multiply(): lax.all_to_all(jnp.concatenate([outgoing, far_backward], 1), 'row', split...  32.5 us
    all_to_all x1, starting transfers between devices, on_device(): lax.all_to_all(columns_local, 'row', split_axis=0, concat_axis=0, tiled=T...  16.7 us
    dot_general x7, matrix products, multiply(): jnp.einsum('oqht,oqt->oqh', distant_local_part, gathered_values, preferre...  8.23 us
  transfers between devices with their start and end apart: 22, of which 8 were waited for; matrix products, arithmetic and copies ran while one was open for 10% of the time, Pallas kernels for 0%

profile of v3, /device:TPU:1, one launch (start us, length us, event | category | flops | bytes accessed | tf_op | source)
XLA Modules:
  0.0 376.9 jit_solution(10169665148691423075)
XLA Ops:
  2.2 16.7 %all-to-all-start = ((s32[32,1,2]{2,1,0:T(1,128)}), s32[32,1,2]{2,1,0:T(1,128)S(1)}, u32[]{:S(2)}, u32[]{:S(2)}) async-start(s32[32,1,2]{2,1,0:T(1,128)} %copy.26), calls=%async_computation | async-start | bytes 32768 | tf_op jit(solution)/shard_map/all_to_all | solution.py:39
  34.6 9.4 %all-to-all-start.1 = ((f32[32,4,128]{2,1,0:T(4,128)}), f32[32,4,128]{2,1,0:T(4,128)S(1)}, u32[]{:S(2)}, u32[]{:S(2)}) async-start(f32[32,4,128]{2,1,0:T(4,128)} %pad_maximum_fusion), calls=%async_computation.1 | async-start | bytes 131072 | tf_op jit(solution)/shard_map/all_to_all | solution.py:69
  45.9 11.0 %all-to-all-done.1 = f32[32,4,128]{2,1,0:T(4,128)S(1)} async-done(((f32[32,4,128]{2,1,0:T(4,128)}), f32[32,4,128]{2,1,0:T(4,128)S(1)}, u32[]{:S(2)}, u32[]{:S(2)}) %all-to-all-start.1) | async-done | bytes 65568 | tf_op jit(solution)/shard_map/all_to_all | solution.py:69
  58.9 14.1 %all_to_all.106 = f32[16,32,128]{2,1,0:T(8,128)S(1)} all-to-all(f32[16,32,128]{2,1,0:T(8,128)S(1)} %broadcast_in_dim.22), channel_id=1, replica_groups=mesh['row'=32,'band'=16] {'band'}, dimensions={0} | all-to-all | bytes 524288 | tf_op jit(solution)/shard_map/all_to_all | solution.py:19
  74.4 4.9 %collective-permute-start.2 = (bf16[16,128]{1,0:T(8,128)(2,1)S(1)}, bf16[16,128]{1,0:T(8,128)(2,1)S(1)}, u32[]{:S(2)}, u32[]{:S(2)}) collective-permute-start(bf16[16,128]{1,0:T(8,128)(2,1)S(1)} %slice.269), channel_id=1, source_target_pairs={{16,0},{32,16},{48,32},{64,48},{80,64},{96,80},{112,96},{128,112},... | collective-permute-start | bytes 12296 | tf_op jit(solution)/shard_map/ppermute | solution.py:13
  80.7 3.6 all-to-all-start.3
  88.9 8.2 %all-to-all-done.3 = f32[32,4,128]{2,1,0:T(4,128)S(1)} async-done(((f32[32,4,128]{2,1,0:T(4,128)}), f32[32,4,128]{2,1,0:T(4,128)S(1)}, u32[]{:S(2)}, u32[]{:S(2)}) %all-to-all-start.3) | async-done | bytes 65568 | tf_op jit(solution)/shard_map/all_to_all | solution.py:69
  99.0 10.3 %all_to_all.107 = f32[16,32,128]{2,1,0:T(8,128)S(1)} all-to-all(f32[16,32,128]{2,1,0:T(8,128)S(1)} %broadcast_in_dim.23), channel_id=1, replica_groups=mesh['row'=32,'band'=16] {'band'}, dimensions={0} | all-to-all | bytes 524288 | tf_op jit(solution)/shard_map/all_to_all | solution.py:19
  110.6 4.6 %collective-permute-start.4 = (bf16[16,128]{1,0:T(8,128)(2,1)S(1)}, bf16[16,128]{1,0:T(8,128)(2,1)S(1)}, u32[]{:S(2)}, u32[]{:S(2)}) collective-permute-start(bf16[16,128]{1,0:T(8,128)(2,1)S(1)} %slice.276), channel_id=1, source_target_pairs={{16,0},{32,16},{48,32},{64,48},{80,64},{96,80},{112,96},{128,112},... | collective-permute-start | bytes 12296 | tf_op jit(solution)/shard_map/ppermute | solution.py:13
  116.6 3.6 all-to-all-start.5
  124.8 8.0 %all-to-all-done.5 = f32[32,4,128]{2,1,0:T(4,128)S(1)} async-done(((f32[32,4,128]{2,1,0:T(4,128)}), f32[32,4,128]{2,1,0:T(4,128)S(1)}, u32[]{:S(2)}, u32[]{:S(2)}) %all-to-all-start.5) | async-done | bytes 65568 | tf_op jit(solution)/shard_map/all_to_all | solution.py:69
  134.8 10.3 %all_to_all.108 = f32[16,32,128]{2,1,0:T(8,128)S(1)} all-to-all(f32[16,32,128]{2,1,0:T(8,128)S(1)} %broadcast_in_dim.24), channel_id=1, replica_groups=mesh['row'=32,'band'=16] {'band'}, dimensions={0} | all-to-all | bytes 524288 | tf_op jit(solution)/shard_map/all_to_all | solution.py:19
  148.5 17.3 %all_to_all.109 = f32[32,1,4]{2,1,0:T(1,128)S(1)} all-to-all(f32[32,1,4]{2,1,0:T(1,128)S(1)} %broadcast_in_dim.25), channel_id=1, replica_groups=mesh['row'=32,'band'=16] {'row'}, dimensions={0} | all-to-all | bytes 1024 | tf_op jit(solution)/shard_map/all_to_all | solution.py:19
  175.7 4.1 %all-to-all-start.8 = ((f32[32,4,128]{2,1,0:T(4,128)}), f32[32,4,128]{2,1,0:T(4,128)S(1)}, u32[]{:S(2)}, u32[]{:S(2)}) async-start(f32[32,4,128]{2,1,0:T(4,128)} %pad_maximum_fusion.3), calls=%async_computation.8 | async-start | bytes 131072 | tf_op jit(solution)/shard_map/all_to_all | solution.py:69
  180.5 3.5 collective-permute-start.7
  184.8 8.1 %all-to-all-done.8 = f32[32,4,128]{2,1,0:T(4,128)S(1)} async-done(((f32[32,4,128]{2,1,0:T(4,128)}), f32[32,4,128]{2,1,0:T(4,128)S(1)}, u32[]{:S(2)}, u32[]{:S(2)}) %all-to-all-start.8) | async-done | bytes 65568 | tf_op jit(solution)/shard_map/all_to_all | solution.py:69
  194.8 10.2 %all_to_all.110 = f32[16,32,128]{2,1,0:T(8,128)S(1)} all-to-all(f32[16,32,128]{2,1,0:T(8,128)S(1)} %broadcast_in_dim.26), channel_id=1, replica_groups=mesh['row'=32,'band'=16] {'band'}, dimensions={0} | all-to-all | bytes 524288 | tf_op jit(solution)/shard_map/all_to_all | solution.py:19
  206.3 17.5 %all_to_all.111 = f32[32,1,1]{2,1,0:T(1,128)S(1)} all-to-all(f32[32,1,1]{2,1,0:T(1,128)S(1)} %broadcast_in_dim.27), channel_id=1, replica_groups=mesh['row'=32,'band'=16] {'row'}, dimensions={0} | all-to-all | bytes 256 | tf_op jit(solution)/shard_map/all_to_all | solution.py:19
  230.7 4.1 %all-to-all-start.11 = ((f32[32,4,128]{2,1,0:T(4,128)}), f32[32,4,128]{2,1,0:T(4,128)S(1)}, u32[]{:S(2)}, u32[]{:S(2)}) async-start(f32[32,4,128]{2,1,0:T(4,128)} %pad_maximum_fusion.4), calls=%async_computation.11 | async-start | bytes 131072 | tf_op jit(solution)/shard_map/all_to_all | solution.py:69
  235.5 3.5 collective-permute-start.9
  239.7 8.1 %all-to-all-done.11 = f32[32,4,128]{2,1,0:T(4,128)S(1)} async-done(((f32[32,4,128]{2,1,0:T(4,128)}), f32[32,4,128]{2,1,0:T(4,128)S(1)}, u32[]{:S(2)}, u32[]{:S(2)}) %all-to-all-start.11) | async-done | bytes 65568 | tf_op jit(solution)/shard_map/all_to_all | solution.py:69
  249.8 10.2 %all_to_all.112 = f32[16,32,128]{2,1,0:T(8,128)S(1)} all-to-all(f32[16,32,128]{2,1,0:T(8,128)S(1)} %broadcast_in_dim.28), channel_id=1, replica_groups=mesh['row'=32,'band'=16] {'band'}, dimensions={0} | all-to-all | bytes 524288 | tf_op jit(solution)/shard_map/all_to_all | solution.py:19
  261.3 4.9 %collective-permute-start.10 = (bf16[16,128]{1,0:T(8,128)(2,1)S(1)}, bf16[16,128]{1,0:T(8,128)(2,1)S(1)}, u32[]{:S(2)}, u32[]{:S(2)}) collective-permute-start(bf16[16,128]{1,0:T(8,128)(2,1)S(1)} %slice.297), channel_id=1, source_target_pairs={{16,0},{32,16},{48,32},{64,48},{80,64},{96,80},{112,96},{128,112},... | collective-permute-start | bytes 12296 | tf_op jit(solution)/shard_map/ppermute | solution.py:13
  267.7 3.6 all-to-all-start.13
  275.8 8.2 %all-to-all-done.13 = f32[32,4,128]{2,1,0:T(4,128)S(1)} async-done(((f32[32,4,128]{2,1,0:T(4,128)}), f32[32,4,128]{2,1,0:T(4,128)S(1)}, u32[]{:S(2)}, u32[]{:S(2)}) %all-to-all-start.13) | async-done | bytes 65568 | tf_op jit(solution)/shard_map/all_to_all | solution.py:69
  285.9 10.3 %all_to_all.113 = f32[16,32,128]{2,1,0:T(8,128)S(1)} all-to-all(f32[16,32,128]{2,1,0:T(8,128)S(1)} %broadcast_in_dim.29), channel_id=1, replica_groups=mesh['row'=32,'band'=16] {'band'}, dimensions={0} | all-to-all | bytes 524288 | tf_op jit(solution)/shard_map/all_to_all | solution.py:19
  299.6 17.3 %all_to_all.114 = f32[32,1,4]{2,1,0:T(1,128)S(1)} all-to-all(f32[32,1,4]{2,1,0:T(1,128)S(1)} %broadcast_in_dim.30), channel_id=1, replica_groups=mesh['row'=32,'band'=16] {'row'}, dimensions={0} | all-to-all | bytes 1024 | tf_op jit(solution)/shard_map/all_to_all | solution.py:19
  326.8 4.1 %all-to-all-start.16 = ((f32[32,4,128]{2,1,0:T(4,128)}), f32[32,4,128]{2,1,0:T(4,128)S(1)}, u32[]{:S(2)}, u32[]{:S(2)}) async-start(f32[32,4,128]{2,1,0:T(4,128)} %pad_maximum_fusion.6), calls=%async_computation.16 | async-start | bytes 131072 | tf_op jit(solution)/shard_map/all_to_all | solution.py:69
  331.6 3.5 collective-permute-start.13
  335.8 8.1 %all-to-all-done.16 = f32[32,4,128]{2,1,0:T(4,128)S(1)} async-done(((f32[32,4,128]{2,1,0:T(4,128)}), f32[32,4,128]{2,1,0:T(4,128)S(1)}, u32[]{:S(2)}, u32[]{:S(2)}) %all-to-all-start.16) | async-done | bytes 65568 | tf_op jit(solution)/shard_map/all_to_all | solution.py:69
  345.9 10.2 %all_to_all.115 = f32[16,32,128]{2,1,0:T(8,128)S(1)} all-to-all(f32[16,32,128]{2,1,0:T(8,128)S(1)} %broadcast_in_dim.31), channel_id=1, replica_groups=mesh['row'=32,'band'=16] {'band'}, dimensions={0} | all-to-all | bytes 524288 | tf_op jit(solution)/shard_map/all_to_all | solution.py:19
  357.4 17.5 %all_to_all.116 = f32[32,1,1]{2,1,0:T(1,128)S(1)} all-to-all(f32[32,1,1]{2,1,0:T(1,128)S(1)} %broadcast_in_dim.32), channel_id=1, replica_groups=mesh['row'=32,'band'=16] {'row'}, dimensions={0} | all-to-all | bytes 256 | tf_op jit(solution)/shard_map/all_to_all | solution.py:19
  (237 shorter events, 87.1 us)
Async XLA Ops:
  0.6 32.5 %copy-start = (bf16[1,1,32,2,128,128]{5,4,3,2,1,0:T(8,128)(2,1)S(1)}, bf16[1,1,32,2,128,128]{5,4,3,2,1,0:T(8,128)(2,1)}, u32[]{:S(2)}) copy-start(bf16[1,1,32,2,128,128]{5,4,3,2,1,0:T(8,128)(2,1)} %param.6) | copy-start | bytes 6291460
  2.2 28.5 %all-to-all-start = ((s32[32,1,2]{2,1,0:T(1,128)}), s32[32,1,2]{2,1,0:T(1,128)S(1)}, u32[]{:S(2)}, u32[]{:S(2)}) async-start(s32[32,1,2]{2,1,0:T(1,128)} %copy.26), calls=%async_computation | async-start | bytes 32768 | tf_op jit(solution)/shard_map/all_to_all | solution.py:39
  18.9 26.3 %collective-permute-start = (bf16[16,128]{1,0:T(8,128)(2,1)S(1)}, bf16[16,128]{1,0:T(8,128)(2,1)S(1)}, u32[]{:S(2)}, u32[]{:S(2)}) collective-permute-start(bf16[16,128]{1,0:T(8,128)(2,1)S(1)} %slice.178), channel_id=1, source_target_pairs={{16,0},{32,16},{48,32},{64,48},{80,64},{96,80},{112,96},{128,112},... | collective-permute-start | bytes 12296 | tf_op jit(solution)/shard_map/ppermute | solution.py:13
  21.1 24.2 %copy-start.1 = (bf16[32,1,128,128]{3,2,1,0:T(8,128)(2,1)S(1)}, bf16[32,1,128,128]{3,2,1,0:T(8,128)(2,1)}, u32[]{:S(2)}) copy-start(bf16[32,1,128,128]{3,2,1,0:T(8,128)(2,1)} %param.5) | copy-start | bytes 3145732
  23.1 35.8 %collective-permute-start.1 = (f32[16,128]{1,0:T(8,128)S(1)}, f32[16,128]{1,0:T(8,128)S(1)}, u32[]{:S(2)}, u32[]{:S(2)}) collective-permute-start(f32[16,128]{1,0:T(8,128)S(1)} %slice.267), channel_id=1, source_target_pairs={{0,16},{16,32},{32,48},{48,64},{64,80},{80,96},{96,112},{112,128},... | collective-permute-start | bytes 24584 | tf_op jit(solution)/shard_map/ppermute | solution.py:13
  34.6 22.4 %all-to-all-start.1 = ((f32[32,4,128]{2,1,0:T(4,128)}), f32[32,4,128]{2,1,0:T(4,128)S(1)}, u32[]{:S(2)}, u32[]{:S(2)}) async-start(f32[32,4,128]{2,1,0:T(4,128)} %pad_maximum_fusion), calls=%async_computation.1 | async-start | bytes 131072 | tf_op jit(solution)/shard_map/all_to_all | solution.py:69
  74.4 13.8 %collective-permute-start.2 = (bf16[16,128]{1,0:T(8,128)(2,1)S(1)}, bf16[16,128]{1,0:T(8,128)(2,1)S(1)}, u32[]{:S(2)}, u32[]{:S(2)}) collective-permute-start(bf16[16,128]{1,0:T(8,128)(2,1)S(1)} %slice.269), channel_id=1, source_target_pairs={{16,0},{32,16},{48,32},{64,48},{80,64},{96,80},{112,96},{128,112},... | collective-permute-start | bytes 12296 | tf_op jit(solution)/shard_map/ppermute | solution.py:13
  80.7 16.3 %all-to-all-start.3 = ((f32[32,4,128]{2,1,0:T(4,128)}), f32[32,4,128]{2,1,0:T(4,128)S(1)}, u32[]{:S(2)}, u32[]{:S(2)}) async-start(f32[32,4,128]{2,1,0:T(4,128)} %pad_maximum_fusion.1), calls=%async_computation.3 | async-start | bytes 131072 | tf_op jit(solution)/shard_map/all_to_all | solution.py:69
  85.0 13.9 %collective-permute-start.3 = (f32[16,128]{1,0:T(8,128)S(1)}, f32[16,128]{1,0:T(8,128)S(1)}, u32[]{:S(2)}, u32[]{:S(2)}) collective-permute-start(f32[16,128]{1,0:T(8,128)S(1)} %slice.274), channel_id=1, source_target_pairs={{0,16},{16,32},{32,48},{48,64},{64,80},{80,96},{96,112},{112,128},... | collective-permute-start | bytes 24584 | tf_op jit(solution)/shard_map/ppermute | solution.py:13
  110.6 13.5 %collective-permute-start.4 = (bf16[16,128]{1,0:T(8,128)(2,1)S(1)}, bf16[16,128]{1,0:T(8,128)(2,1)S(1)}, u32[]{:S(2)}, u32[]{:S(2)}) collective-permute-start(bf16[16,128]{1,0:T(8,128)(2,1)S(1)} %slice.276), channel_id=1, source_target_pairs={{16,0},{32,16},{48,32},{64,48},{80,64},{96,80},{112,96},{128,112},... | collective-permute-start | bytes 12296 | tf_op jit(solution)/shard_map/ppermute | solution.py:13
  116.6 16.2 %all-to-all-start.5 = ((f32[32,4,128]{2,1,0:T(4,128)}), f32[32,4,128]{2,1,0:T(4,128)S(1)}, u32[]{:S(2)}, u32[]{:S(2)}) async-start(f32[32,4,128]{2,1,0:T(4,128)} %pad_maximum_fusion.2), calls=%async_computation.5 | async-start | bytes 131072 | tf_op jit(solution)/shard_map/all_to_all | solution.py:69
  120.9 13.8 %collective-permute-start.5 = (f32[16,128]{1,0:T(8,128)S(1)}, f32[16,128]{1,0:T(8,128)S(1)}, u32[]{:S(2)}, u32[]{:S(2)}) collective-permute-start(f32[16,128]{1,0:T(8,128)S(1)} %slice.281), channel_id=1, source_target_pairs={{0,16},{16,32},{32,48},{48,64},{64,80},{80,96},{96,112},{112,128},... | collective-permute-start | bytes 24584 | tf_op jit(solution)/shard_map/ppermute | solution.py:13
  171.5 12.5 %collective-permute-start.6 = (bf16[16,128]{1,0:T(8,128)(2,1)S(1)}, bf16[16,128]{1,0:T(8,128)(2,1)S(1)}, u32[]{:S(2)}, u32[]{:S(2)}) collective-permute-start(bf16[16,128]{1,0:T(8,128)(2,1)S(1)} %slice.283), channel_id=1, source_target_pairs={{16,0},{32,16},{48,32},{64,48},{80,64},{96,80},{112,96},{128,112},... | collective-permute-start | bytes 12296 | tf_op jit(solution)/shard_map/ppermute | solution.py:13
  175.7 17.1 %all-to-all-start.8 = ((f32[32,4,128]{2,1,0:T(4,128)}), f32[32,4,128]{2,1,0:T(4,128)S(1)}, u32[]{:S(2)}, u32[]{:S(2)}) async-start(f32[32,4,128]{2,1,0:T(4,128)} %pad_maximum_fusion.3), calls=%async_computation.8 | async-start | bytes 131072 | tf_op jit(solution)/shard_map/all_to_all | solution.py:69
  180.5 14.2 %collective-permute-start.7 = (f32[16,128]{1,0:T(8,128)S(1)}, f32[16,128]{1,0:T(8,128)S(1)}, u32[]{:S(2)}, u32[]{:S(2)}) collective-permute-start(f32[16,128]{1,0:T(8,128)S(1)} %slice.288), channel_id=1, source_target_pairs={{0,16},{16,32},{32,48},{48,64},{64,80},{80,96},{96,112},{112,128},... | collective-permute-start | bytes 24584 | tf_op jit(solution)/shard_map/ppermute | solution.py:13
  226.5 12.5 %collective-permute-start.8 = (bf16[16,128]{1,0:T(8,128)(2,1)S(1)}, bf16[16,128]{1,0:T(8,128)(2,1)S(1)}, u32[]{:S(2)}, u32[]{:S(2)}) collective-permute-start(bf16[16,128]{1,0:T(8,128)(2,1)S(1)} %slice.290), channel_id=1, source_target_pairs={{16,0},{32,16},{48,32},{64,48},{80,64},{96,80},{112,96},{128,112},... | collective-permute-start | bytes 12296 | tf_op jit(solution)/shard_map/ppermute | solution.py:13
  230.7 17.1 %all-to-all-start.11 = ((f32[32,4,128]{2,1,0:T(4,128)}), f32[32,4,128]{2,1,0:T(4,128)S(1)}, u32[]{:S(2)}, u32[]{:S(2)}) async-start(f32[32,4,128]{2,1,0:T(4,128)} %pad_maximum_fusion.4), calls=%async_computation.11 | async-start | bytes 131072 | tf_op jit(solution)/shard_map/all_to_all | solution.py:69
  235.5 14.2 %collective-permute-start.9 = (f32[16,128]{1,0:T(8,128)S(1)}, f32[16,128]{1,0:T(8,128)S(1)}, u32[]{:S(2)}, u32[]{:S(2)}) collective-permute-start(f32[16,128]{1,0:T(8,128)S(1)} %slice.295), channel_id=1, source_target_pairs={{0,16},{16,32},{32,48},{48,64},{64,80},{80,96},{96,112},{112,128},... | collective-permute-start | bytes 24584 | tf_op jit(solution)/shard_map/ppermute | solution.py:13
  261.3 13.8 %collective-permute-start.10 = (bf16[16,128]{1,0:T(8,128)(2,1)S(1)}, bf16[16,128]{1,0:T(8,128)(2,1)S(1)}, u32[]{:S(2)}, u32[]{:S(2)}) collective-permute-start(bf16[16,128]{1,0:T(8,128)(2,1)S(1)} %slice.297), channel_id=1, source_target_pairs={{16,0},{32,16},{48,32},{64,48},{80,64},{96,80},{112,96},{128,112},... | collective-permute-start | bytes 12296 | tf_op jit(solution)/shard_map/ppermute | solution.py:13
  267.7 16.3 %all-to-all-start.13 = ((f32[32,4,128]{2,1,0:T(4,128)}), f32[32,4,128]{2,1,0:T(4,128)S(1)}, u32[]{:S(2)}, u32[]{:S(2)}) async-start(f32[32,4,128]{2,1,0:T(4,128)} %pad_maximum_fusion.5), calls=%async_computation.13 | async-start | bytes 131072 | tf_op jit(solution)/shard_map/all_to_all | solution.py:69
  272.0 13.9 %collective-permute-start.11 = (f32[16,128]{1,0:T(8,128)S(1)}, f32[16,128]{1,0:T(8,128)S(1)}, u32[]{:S(2)}, u32[]{:S(2)}) collective-permute-start(f32[16,128]{1,0:T(8,128)S(1)} %slice.302), channel_id=1, source_target_pairs={{0,16},{16,32},{32,48},{48,64},{64,80},{80,96},{96,112},{112,128},... | collective-permute-start | bytes 24584 | tf_op jit(solution)/shard_map/ppermute | solution.py:13
  322.6 12.5 %collective-permute-start.12 = (bf16[16,128]{1,0:T(8,128)(2,1)S(1)}, bf16[16,128]{1,0:T(8,128)(2,1)S(1)}, u32[]{:S(2)}, u32[]{:S(2)}) collective-permute-start(bf16[16,128]{1,0:T(8,128)(2,1)S(1)} %slice.304), channel_id=1, source_target_pairs={{16,0},{32,16},{48,32},{64,48},{80,64},{96,80},{112,96},{128,112},... | collective-permute-start | bytes 12296 | tf_op jit(solution)/shard_map/ppermute | solution.py:13
  326.8 17.1 %all-to-all-start.16 = ((f32[32,4,128]{2,1,0:T(4,128)}), f32[32,4,128]{2,1,0:T(4,128)S(1)}, u32[]{:S(2)}, u32[]{:S(2)}) async-start(f32[32,4,128]{2,1,0:T(4,128)} %pad_maximum_fusion.6), calls=%async_computation.16 | async-start | bytes 131072 | tf_op jit(solution)/shard_map/all_to_all | solution.py:69
  331.6 14.2 %collective-permute-start.13 = (f32[16,128]{1,0:T(8,128)S(1)}, f32[16,128]{1,0:T(8,128)S(1)}, u32[]{:S(2)}, u32[]{:S(2)}) collective-permute-start(f32[16,128]{1,0:T(8,128)S(1)} %slice.309), channel_id=1, source_target_pairs={{0,16},{16,32},{32,48},{48,64},{64,80},{80,96},{96,112},{112,128},... | collective-permute-start | bytes 24584 | tf_op jit(solution)/shard_map/ppermute | solution.py:13

commit v4 on v3

--- a/solution.py
+++ b/solution.py
@@ -36,12 +36,10 @@
     block_ids = row_index * rows_dev + jnp.arange(rows_dev)
     valid_mask = (block_ids + offset < row_count * rows_dev).astype(jnp.float32)[:, None]
     upper_mask = (offset > 0).astype(jnp.float32)
-    wanted = lax.all_to_all(columns_local, "row", split_axis=0, concat_axis=0, tiled=True)
     targets = jnp.arange(rows_dev)[None, :]
-    selection_output = (wanted.reshape(-1)[:, None] == targets).astype(jnp.float32)
     pick_in = (local_row_values.reshape(-1)[:, None] == targets).astype(jnp.float32)
 
-    def multiply(vector):
+    def multiply(vector, wanted=None):
         narrow_band_part = vector.astype(jnp.bfloat16)
         ahead_rows = shifted(narrow_band_part[:band_count], "row", -1)
         extended = jnp.concatenate([narrow_band_part, ahead_rows], 0)
@@ -56,7 +54,6 @@
         spread = lax.dynamic_update_slice_in_dim(
             jnp.zeros((rows_dev + band_count, block_size), jnp.float32), backward, offset, 0
         )
-        outgoing = narrow_band_part[wanted].astype(jnp.float32)
         far_backward = (
             jnp.einsum(
                 "nquo,nqu->nqo",
@@ -66,11 +63,23 @@
             )
             * live_mask
         )
-        exchanged = lax.all_to_all(
-            jnp.concatenate([outgoing, far_backward], 1), "row", split_axis=0, concat_axis=0, tiled=True
-        )
-        gathered_values = exchanged[:, :slots].astype(jnp.bfloat16)
-        returned = exchanged[:, slots:]
+        if wanted is None:
+            column_row = jnp.zeros((row_count, 1, block_size), jnp.float32)
+            column_row = column_row.at[:, 0, :slots].set(columns_local.astype(jnp.float32))
+            exchanged = lax.all_to_all(
+                jnp.concatenate([column_row, far_backward], 1), "row", split_axis=0, concat_axis=0, tiled=True
+            )
+            wanted = jnp.round(exchanged[:, 0, :slots]).astype(jnp.int32)
+            gathered_values = jnp.ones((row_count, slots, block_size), jnp.bfloat16)
+            returned = exchanged[:, 1:]
+        else:
+            outgoing = narrow_band_part[wanted].astype(jnp.float32)
+            exchanged = lax.all_to_all(
+                jnp.concatenate([outgoing, far_backward], 1), "row", split_axis=0, concat_axis=0, tiled=True
+            )
+            gathered_values = exchanged[:, :slots].astype(jnp.bfloat16)
+            returned = exchanged[:, slots:]
+        selection_output = (wanted.reshape(-1)[:, None] == targets).astype(jnp.float32)
         far_forward = (
             jnp.einsum(
                 "oqht,oqt->oqh",
@@ -89,20 +98,20 @@
         )
         carried = shifted(spread[rows_dev:], "row", 1)
         summed = jnp.concatenate([summed[:band_count] + carried, summed[band_count:]], 0)
-        return all_sum(summed, "band")
+        return all_sum(summed, "band"), wanted
 
-    row_sums = multiply(jnp.ones((rows_dev, block_size), jnp.float32))
+    row_sums, wanted = multiply(jnp.ones((rows_dev, block_size), jnp.float32))
     scaling = 1.0 / jnp.sqrt(row_sums)
     residual = jnp.zeros_like(scaling)
     for outer_step in range(OUTER):
-        balance = scaling * multiply(scaling)
+        balance = scaling * multiply(scaling, wanted)[0]
         residual = 1.0 - balance
         scaled = residual / balance
         direction = scaled
         local_product = jnp.sum(residual * scaled)
         growth = jnp.ones_like(scaling)
         for inner_step in range(INNER):
-            curved = scaling * multiply(scaling * direction) + balance * direction
+            curved = scaling * multiply(scaling * direction, wanted)[0] + balance * direction
             last = inner_step + 1 == INNER
             parts = [jnp.sum(direction * curved)]
             if inner_step == 0:

time: 379 us -> 360 us (0.950)
  blocking collectives: 145 us -> 131 us
    all_to_all x11 -> x10, blocking collectives: 145 us -> 131 us  [all_sum(): return jnp.sum(lax.all_to_all(copies, axis, 0, 0, tiled=True), 0)]
    all_to_all x1 -> x2, waiting for transfers between devices: 2.55 us -> 14.8 us  [the longest x1 7.56 us: multiply(): lax.all_to_all(jnp.concatenate([column_row, far_backward], 1), 'row', spl...]
    all_to_all x7 -> x6, waiting for transfers between devices: 59.6 us -> 48.7 us  [multiply(): lax.all_to_all(jnp.concatenate([outgoing, far_backward], 1), 'row', split...]
    all_to_all x7 -> x6, starting transfers between devices: 32.5 us -> 23.6 us  [multiply(): lax.all_to_all(jnp.concatenate([outgoing, far_backward], 1), 'row', split...]
    ppermute x14, starting transfers between devices: 48.4 us -> 55.9 us  [shifted(): lax.ppermute(value, axis, [(source, source + steps) for source in range(l...]
    all_to_all x1 -> x2, starting transfers between devices: 16.7 us -> 16.8 us  [the longest x1 10 us: multiply(): lax.all_to_all(jnp.concatenate([column_row, far_backward], 1), 'row', spl...]
where the time goes in v4:
time: 360 us; the launch traced here: 358 us
  blocking collectives  131 us (36%)
  starting transfers between devices  96.3 us (27%)
  waiting for transfers between devices  63.5 us (18%)
  matrix products  23.7 us (7%)
  other arithmetic  18.6 us (5%)
  local copies, waits for them, and re-layouts  14.3 us (4%)
  between operations  10.7 us (3%)
    all_to_all x10, blocking collectives, all_sum(): return jnp.sum(lax.all_to_all(copies, axis, 0, 0, tiled=True), 0)  131 us
    ppermute x14, starting transfers between devices, shifted(): lax.ppermute(value, axis, [(source, source + steps) for source in range(l...  55.9 us
    all_to_all x6, waiting for transfers between devices, multiply(): lax.all_to_all(jnp.concatenate([outgoing, far_backward], 1), 'row', split...  48.7 us
    all_to_all x6, starting transfers between devices, multiply(): lax.all_to_all(jnp.concatenate([outgoing, far_backward], 1), 'row', split...  23.6 us
    all_to_all x1, starting transfers between devices, multiply(): lax.all_to_all(jnp.concatenate([column_row, far_backward], 1), 'row', spl...  10 us
    dot_general x7, matrix products, multiply(): jnp.einsum('oqht,oqt->oqh', distant_local_part, gathered_values, preferre...  8.22 us
    all_to_all x1, waiting for transfers between devices, multiply(): lax.all_to_all(jnp.concatenate([column_row, far_backward], 1), 'row', spl...  7.56 us
    all_to_all x1, waiting for transfers between devices, all_sum(): return jnp.sum(lax.all_to_all(copies, axis, 0, 0, tiled=True), 0)  7.26 us
  transfers between devices with their start and end apart: 22, of which 8 were waited for; matrix products, arithmetic and copies ran while one was open for 10% of the time, Pallas kernels for 0%

profile of v4, /device:TPU:1, one launch (start us, length us, event | category | flops | bytes accessed | tf_op | source)
XLA Modules:
  0.0 358.0 jit_solution(2202956513199511926)
XLA Ops:
  0.7 8.9 %collective-permute-start = (bf16[16,128]{1,0:T(8,128)(2,1)S(1)}, bf16[16,128]{1,0:T(8,128)(2,1)S(1)}, u32[]{:S(2)}, u32[]{:S(2)}) collective-permute-start(bf16[16,128]{1,0:T(8,128)(2,1)S(1)} %slice.200), channel_id=1, source_target_pairs={{16,0},{32,16},{48,32},{64,48},{80,64},{96,80},{112,96},{128,112},... | collective-permute-start | bytes 12296 | tf_op jit(solution)/shard_map/ppermute | solution.py:13
  14.6 10.0 %all-to-all-start = ((f32[32,3,128]{2,1,0:T(4,128)}), f32[32,3,128]{2,1,0:T(4,128)S(1)}, u32[]{:S(2)}, u32[]{:S(2)}) async-start(f32[32,3,128]{2,1,0:T(4,128)} %select_maximum_fusion), calls=%async_computation | async-start | bytes 131072 | tf_op jit(solution)/shard_map/all_to_all | solution.py:69
  25.3 3.5 collective-permute-start.1
  30.0 7.6 %all-to-all-done = f32[32,3,128]{2,1,0:T(4,128)S(1)} async-done(((f32[32,3,128]{2,1,0:T(4,128)}), f32[32,3,128]{2,1,0:T(4,128)S(1)}, u32[]{:S(2)}, u32[]{:S(2)}) %all-to-all-start) | async-done | bytes 49184 | tf_op jit(solution)/shard_map/all_to_all | solution.py:69
  38.8 6.8 %all-to-all-start.1 = ((f32[16,32,128]{2,1,0:T(8,128)}), f32[16,32,128]{2,1,0:T(8,128)S(1)}, u32[]{:S(2)}, u32[]{:S(2)}) async-start(f32[16,32,128]{2,1,0:T(8,128)} %broadcast_in_dim.25), calls=%async_computation.1 | async-start | bytes 524288 | tf_op jit(solution)/shard_map/all_to_all | solution.py:19
  45.9 7.3 %all-to-all-done.1 = f32[16,32,128]{2,1,0:T(8,128)S(1)} async-done(((f32[16,32,128]{2,1,0:T(8,128)}), f32[16,32,128]{2,1,0:T(8,128)S(1)}, u32[]{:S(2)}, u32[]{:S(2)}) %all-to-all-start.1) | async-done | bytes 262176 | tf_op jit(solution)/shard_map/all_to_all | solution.py:19
  53.8 4.9 %collective-permute-start.2 = (bf16[16,128]{1,0:T(8,128)(2,1)S(1)}, bf16[16,128]{1,0:T(8,128)(2,1)S(1)}, u32[]{:S(2)}, u32[]{:S(2)}) collective-permute-start(bf16[16,128]{1,0:T(8,128)(2,1)S(1)} %slice.289), channel_id=1, source_target_pairs={{16,0},{32,16},{48,32},{64,48},{80,64},{96,80},{112,96},{128,112},... | collective-permute-start | bytes 12296 | tf_op jit(solution)/shard_map/ppermute | solution.py:13
  60.8 4.1 %all-to-all-start.2 = ((f32[32,4,128]{2,1,0:T(4,128)}), f32[32,4,128]{2,1,0:T(4,128)S(1)}, u32[]{:S(2)}, u32[]{:S(2)}) async-start(f32[32,4,128]{2,1,0:T(4,128)} %pad_maximum_fusion), calls=%async_computation.2 | async-start | bytes 131072 | tf_op jit(solution)/shard_map/all_to_all | solution.py:77
  65.5 3.5 collective-permute-start.3
  69.8 8.1 %all-to-all-done.2 = f32[32,4,128]{2,1,0:T(4,128)S(1)} async-done(((f32[32,4,128]{2,1,0:T(4,128)}), f32[32,4,128]{2,1,0:T(4,128)S(1)}, u32[]{:S(2)}, u32[]{:S(2)}) %all-to-all-start.2) | async-done | bytes 65568 | tf_op jit(solution)/shard_map/all_to_all | solution.py:77
  79.8 10.2 %all_to_all.94 = f32[16,32,128]{2,1,0:T(8,128)S(1)} all-to-all(f32[16,32,128]{2,1,0:T(8,128)S(1)} %broadcast_in_dim.26), channel_id=1, replica_groups=mesh['row'=32,'band'=16] {'band'}, dimensions={0} | all-to-all | bytes 524288 | tf_op jit(solution)/shard_map/all_to_all | solution.py:19
  91.4 4.9 %collective-permute-start.4 = (bf16[16,128]{1,0:T(8,128)(2,1)S(1)}, bf16[16,128]{1,0:T(8,128)(2,1)S(1)}, u32[]{:S(2)}, u32[]{:S(2)}) collective-permute-start(bf16[16,128]{1,0:T(8,128)(2,1)S(1)} %slice.296), channel_id=1, source_target_pairs={{16,0},{32,16},{48,32},{64,48},{80,64},{96,80},{112,96},{128,112},... | collective-permute-start | bytes 12296 | tf_op jit(solution)/shard_map/ppermute | solution.py:13
  97.7 3.6 %all-to-all-start.4 = ((f32[32,4,128]{2,1,0:T(4,128)}), f32[32,4,128]{2,1,0:T(4,128)S(1)}, u32[]{:S(2)}, u32[]{:S(2)}) async-start(f32[32,4,128]{2,1,0:T(4,128)} %pad_maximum_fusion.1), calls=%async_computation.4 | async-start | bytes 131072 | tf_op jit(solution)/shard_map/all_to_all | solution.py:77
  105.9 8.2 %all-to-all-done.4 = f32[32,4,128]{2,1,0:T(4,128)S(1)} async-done(((f32[32,4,128]{2,1,0:T(4,128)}), f32[32,4,128]{2,1,0:T(4,128)S(1)}, u32[]{:S(2)}, u32[]{:S(2)}) %all-to-all-start.4) | async-done | bytes 65568 | tf_op jit(solution)/shard_map/all_to_all | solution.py:77
  116.0 10.3 %all_to_all.95 = f32[16,32,128]{2,1,0:T(8,128)S(1)} all-to-all(f32[16,32,128]{2,1,0:T(8,128)S(1)} %broadcast_in_dim.27), channel_id=1, replica_groups=mesh['row'=32,'band'=16] {'band'}, dimensions={0} | all-to-all | bytes 524288 | tf_op jit(solution)/shard_map/all_to_all | solution.py:19
  129.6 17.3 %all_to_all.96 = f32[32,1,4]{2,1,0:T(1,128)S(1)} all-to-all(f32[32,1,4]{2,1,0:T(1,128)S(1)} %broadcast_in_dim.28), channel_id=1, replica_groups=mesh['row'=32,'band'=16] {'row'}, dimensions={0} | all-to-all | bytes 1024 | tf_op jit(solution)/shard_map/all_to_all | solution.py:19
  156.9 4.1 %all-to-all-start.7 = ((f32[32,4,128]{2,1,0:T(4,128)}), f32[32,4,128]{2,1,0:T(4,128)S(1)}, u32[]{:S(2)}, u32[]{:S(2)}) async-start(f32[32,4,128]{2,1,0:T(4,128)} %pad_maximum_fusion.2), calls=%async_computation.7 | async-start | bytes 131072 | tf_op jit(solution)/shard_map/all_to_all | solution.py:77
  165.9 8.1 %all-to-all-done.7 = f32[32,4,128]{2,1,0:T(4,128)S(1)} async-done(((f32[32,4,128]{2,1,0:T(4,128)}), f32[32,4,128]{2,1,0:T(4,128)S(1)}, u32[]{:S(2)}, u32[]{:S(2)}) %all-to-all-start.7) | async-done | bytes 65568 | tf_op jit(solution)/shard_map/all_to_all | solution.py:77
  176.0 10.2 %all_to_all.97 = f32[16,32,128]{2,1,0:T(8,128)S(1)} all-to-all(f32[16,32,128]{2,1,0:T(8,128)S(1)} %broadcast_in_dim.29), channel_id=1, replica_groups=mesh['row'=32,'band'=16] {'band'}, dimensions={0} | all-to-all | bytes 524288 | tf_op jit(solution)/shard_map/all_to_all | solution.py:19
  187.5 17.5 %all_to_all.98 = f32[32,1,1]{2,1,0:T(1,128)S(1)} all-to-all(f32[32,1,1]{2,1,0:T(1,128)S(1)} %broadcast_in_dim.30), channel_id=1, replica_groups=mesh['row'=32,'band'=16] {'row'}, dimensions={0} | all-to-all | bytes 256 | tf_op jit(solution)/shard_map/all_to_all | solution.py:19
  211.9 4.1 %all-to-all-start.10 = ((f32[32,4,128]{2,1,0:T(4,128)}), f32[32,4,128]{2,1,0:T(4,128)S(1)}, u32[]{:S(2)}, u32[]{:S(2)}) async-start(f32[32,4,128]{2,1,0:T(4,128)} %pad_maximum_fusion.3), calls=%async_computation.10 | async-start | bytes 131072 | tf_op jit(solution)/shard_map/all_to_all | solution.py:77
  220.9 8.1 %all-to-all-done.10 = f32[32,4,128]{2,1,0:T(4,128)S(1)} async-done(((f32[32,4,128]{2,1,0:T(4,128)}), f32[32,4,128]{2,1,0:T(4,128)S(1)}, u32[]{:S(2)}, u32[]{:S(2)}) %all-to-all-start.10) | async-done | bytes 65568 | tf_op jit(solution)/shard_map/all_to_all | solution.py:77
  230.9 10.2 %all_to_all.99 = f32[16,32,128]{2,1,0:T(8,128)S(1)} all-to-all(f32[16,32,128]{2,1,0:T(8,128)S(1)} %broadcast_in_dim.31), channel_id=1, replica_groups=mesh['row'=32,'band'=16] {'band'}, dimensions={0} | all-to-all | bytes 524288 | tf_op jit(solution)/shard_map/all_to_all | solution.py:19
  242.5 4.9 %collective-permute-start.10 = (bf16[16,128]{1,0:T(8,128)(2,1)S(1)}, bf16[16,128]{1,0:T(8,128)(2,1)S(1)}, u32[]{:S(2)}, u32[]{:S(2)}) collective-permute-start(bf16[16,128]{1,0:T(8,128)(2,1)S(1)} %slice.317), channel_id=1, source_target_pairs={{16,0},{32,16},{48,32},{64,48},{80,64},{96,80},{112,96},{128,112},... | collective-permute-start | bytes 12296 | tf_op jit(solution)/shard_map/ppermute | solution.py:13
  248.8 3.6 %all-to-all-start.12 = ((f32[32,4,128]{2,1,0:T(4,128)}), f32[32,4,128]{2,1,0:T(4,128)S(1)}, u32[]{:S(2)}, u32[]{:S(2)}) async-start(f32[32,4,128]{2,1,0:T(4,128)} %pad_maximum_fusion.4), calls=%async_computation.12 | async-start | bytes 131072 | tf_op jit(solution)/shard_map/all_to_all | solution.py:77
  257.0 8.2 %all-to-all-done.12 = f32[32,4,128]{2,1,0:T(4,128)S(1)} async-done(((f32[32,4,128]{2,1,0:T(4,128)}), f32[32,4,128]{2,1,0:T(4,128)S(1)}, u32[]{:S(2)}, u32[]{:S(2)}) %all-to-all-start.12) | async-done | bytes 65568 | tf_op jit(solution)/shard_map/all_to_all | solution.py:77
  267.1 10.3 %all_to_all.100 = f32[16,32,128]{2,1,0:T(8,128)S(1)} all-to-all(f32[16,32,128]{2,1,0:T(8,128)S(1)} %broadcast_in_dim.32), channel_id=1, replica_groups=mesh['row'=32,'band'=16] {'band'}, dimensions={0} | all-to-all | bytes 524288 | tf_op jit(solution)/shard_map/all_to_all | solution.py:19
  280.7 17.3 %all_to_all.101 = f32[32,1,4]{2,1,0:T(1,128)S(1)} all-to-all(f32[32,1,4]{2,1,0:T(1,128)S(1)} %broadcast_in_dim.33), channel_id=1, replica_groups=mesh['row'=32,'band'=16] {'row'}, dimensions={0} | all-to-all | bytes 1024 | tf_op jit(solution)/shard_map/all_to_all | solution.py:19
  308.0 4.1 %all-to-all-start.15 = ((f32[32,4,128]{2,1,0:T(4,128)}), f32[32,4,128]{2,1,0:T(4,128)S(1)}, u32[]{:S(2)}, u32[]{:S(2)}) async-start(f32[32,4,128]{2,1,0:T(4,128)} %pad_maximum_fusion.5), calls=%async_computation.15 | async-start | bytes 131072 | tf_op jit(solution)/shard_map/all_to_all | solution.py:77
  317.0 8.1 %all-to-all-done.15 = f32[32,4,128]{2,1,0:T(4,128)S(1)} async-done(((f32[32,4,128]{2,1,0:T(4,128)}), f32[32,4,128]{2,1,0:T(4,128)S(1)}, u32[]{:S(2)}, u32[]{:S(2)}) %all-to-all-start.15) | async-done | bytes 65568 | tf_op jit(solution)/shard_map/all_to_all | solution.py:77
  327.1 10.2 %all_to_all.102 = f32[16,32,128]{2,1,0:T(8,128)S(1)} all-to-all(f32[16,32,128]{2,1,0:T(8,128)S(1)} %broadcast_in_dim.34), channel_id=1, replica_groups=mesh['row'=32,'band'=16] {'band'}, dimensions={0} | all-to-all | bytes 524288 | tf_op jit(solution)/shard_map/all_to_all | solution.py:19
  338.6 17.5 %all_to_all.103 = f32[32,1,1]{2,1,0:T(1,128)S(1)} all-to-all(f32[32,1,1]{2,1,0:T(1,128)S(1)} %broadcast_in_dim.35), channel_id=1, replica_groups=mesh['row'=32,'band'=16] {'row'}, dimensions={0} | all-to-all | bytes 256 | tf_op jit(solution)/shard_map/all_to_all | solution.py:19
  (238 shorter events, 81.9 us)
Async XLA Ops:
  0.6 10.5 %copy-start = (bf16[1,1,32,2,128,128]{5,4,3,2,1,0:T(8,128)(2,1)S(1)}, bf16[1,1,32,2,128,128]{5,4,3,2,1,0:T(8,128)(2,1)}, u32[]{:S(2)}) copy-start(bf16[1,1,32,2,128,128]{5,4,3,2,1,0:T(8,128)(2,1)} %param.8) | copy-start | bytes 6291460
  0.7 28.4 %collective-permute-start = (bf16[16,128]{1,0:T(8,128)(2,1)S(1)}, bf16[16,128]{1,0:T(8,128)(2,1)S(1)}, u32[]{:S(2)}, u32[]{:S(2)}) collective-permute-start(bf16[16,128]{1,0:T(8,128)(2,1)S(1)} %slice.200), channel_id=1, source_target_pairs={{16,0},{32,16},{48,32},{64,48},{80,64},{96,80},{112,96},{128,112},... | collective-permute-start | bytes 12296 | tf_op jit(solution)/shard_map/ppermute | solution.py:13
  11.2 2.5 copy-start.3
  11.2 13.4 %copy-start.1 = (bf16[32,1,128,128]{3,2,1,0:T(8,128)(2,1)S(1)}, bf16[32,1,128,128]{3,2,1,0:T(8,128)(2,1)}, u32[]{:S(2)}) copy-start(bf16[32,1,128,128]{3,2,1,0:T(8,128)(2,1)} %param.7) | copy-start | bytes 3145732
  12.4 16.5 %copy-start.2 = (s32[1,1,32,2]{2,3,1,0:T(2,128)S(1)}, s32[1,1,32,2]{2,3,1,0:T(2,128)}, u32[]{:S(2)}) copy-start(s32[1,1,32,2]{2,3,1,0:T(2,128)} %param.9) | copy-start | bytes 772
  14.6 23.0 %all-to-all-start = ((f32[32,3,128]{2,1,0:T(4,128)}), f32[32,3,128]{2,1,0:T(4,128)S(1)}, u32[]{:S(2)}, u32[]{:S(2)}) async-start(f32[32,3,128]{2,1,0:T(4,128)} %select_maximum_fusion), calls=%async_computation | async-start | bytes 131072 | tf_op jit(solution)/shard_map/all_to_all | solution.py:69
  25.3 12.8 %collective-permute-start.1 = (f32[16,128]{1,0:T(8,128)S(1)}, f32[16,128]{1,0:T(8,128)S(1)}, u32[]{:S(2)}, u32[]{:S(2)}) collective-permute-start(f32[16,128]{1,0:T(8,128)S(1)} %slice.287), channel_id=1, source_target_pairs={{0,16},{16,32},{32,48},{48,64},{64,80},{80,96},{96,112},{112,128},... | collective-permute-start | bytes 24584 | tf_op jit(solution)/shard_map/ppermute | solution.py:13
  38.8 14.3 %all-to-all-start.1 = ((f32[16,32,128]{2,1,0:T(8,128)}), f32[16,32,128]{2,1,0:T(8,128)S(1)}, u32[]{:S(2)}, u32[]{:S(2)}) async-start(f32[16,32,128]{2,1,0:T(8,128)} %broadcast_in_dim.25), calls=%async_computation.1 | async-start | bytes 524288 | tf_op jit(solution)/shard_map/all_to_all | solution.py:19
  53.8 15.3 %collective-permute-start.2 = (bf16[16,128]{1,0:T(8,128)(2,1)S(1)}, bf16[16,128]{1,0:T(8,128)(2,1)S(1)}, u32[]{:S(2)}, u32[]{:S(2)}) collective-permute-start(bf16[16,128]{1,0:T(8,128)(2,1)S(1)} %slice.289), channel_id=1, source_target_pairs={{16,0},{32,16},{48,32},{64,48},{80,64},{96,80},{112,96},{128,112},... | collective-permute-start | bytes 12296 | tf_op jit(solution)/shard_map/ppermute | solution.py:13
  60.8 17.1 %all-to-all-start.2 = ((f32[32,4,128]{2,1,0:T(4,128)}), f32[32,4,128]{2,1,0:T(4,128)S(1)}, u32[]{:S(2)}, u32[]{:S(2)}) async-start(f32[32,4,128]{2,1,0:T(4,128)} %pad_maximum_fusion), calls=%async_computation.2 | async-start | bytes 131072 | tf_op jit(solution)/shard_map/all_to_all | solution.py:77
  65.5 14.2 %collective-permute-start.3 = (f32[16,128]{1,0:T(8,128)S(1)}, f32[16,128]{1,0:T(8,128)S(1)}, u32[]{:S(2)}, u32[]{:S(2)}) collective-permute-start(f32[16,128]{1,0:T(8,128)S(1)} %slice.294), channel_id=1, source_target_pairs={{0,16},{16,32},{32,48},{48,64},{64,80},{80,96},{96,112},{112,128},... | collective-permute-start | bytes 24584 | tf_op jit(solution)/shard_map/ppermute | solution.py:13
  91.4 13.8 %collective-permute-start.4 = (bf16[16,128]{1,0:T(8,128)(2,1)S(1)}, bf16[16,128]{1,0:T(8,128)(2,1)S(1)}, u32[]{:S(2)}, u32[]{:S(2)}) collective-permute-start(bf16[16,128]{1,0:T(8,128)(2,1)S(1)} %slice.296), channel_id=1, source_target_pairs={{16,0},{32,16},{48,32},{64,48},{80,64},{96,80},{112,96},{128,112},... | collective-permute-start | bytes 12296 | tf_op jit(solution)/shard_map/ppermute | solution.py:13
  97.7 16.3 %all-to-all-start.4 = ((f32[32,4,128]{2,1,0:T(4,128)}), f32[32,4,128]{2,1,0:T(4,128)S(1)}, u32[]{:S(2)}, u32[]{:S(2)}) async-start(f32[32,4,128]{2,1,0:T(4,128)} %pad_maximum_fusion.1), calls=%async_computation.4 | async-start | bytes 131072 | tf_op jit(solution)/shard_map/all_to_all | solution.py:77
  102.0 13.9 %collective-permute-start.5 = (f32[16,128]{1,0:T(8,128)S(1)}, f32[16,128]{1,0:T(8,128)S(1)}, u32[]{:S(2)}, u32[]{:S(2)}) collective-permute-start(f32[16,128]{1,0:T(8,128)S(1)} %slice.301), channel_id=1, source_target_pairs={{0,16},{16,32},{32,48},{48,64},{64,80},{80,96},{96,112},{112,128},... | collective-permute-start | bytes 24584 | tf_op jit(solution)/shard_map/ppermute | solution.py:13
  152.7 12.6 %collective-permute-start.6 = (bf16[16,128]{1,0:T(8,128)(2,1)S(1)}, bf16[16,128]{1,0:T(8,128)(2,1)S(1)}, u32[]{:S(2)}, u32[]{:S(2)}) collective-permute-start(bf16[16,128]{1,0:T(8,128)(2,1)S(1)} %slice.303), channel_id=1, source_target_pairs={{16,0},{32,16},{48,32},{64,48},{80,64},{96,80},{112,96},{128,112},... | collective-permute-start | bytes 12296 | tf_op jit(solution)/shard_map/ppermute | solution.py:13
  156.9 17.1 %all-to-all-start.7 = ((f32[32,4,128]{2,1,0:T(4,128)}), f32[32,4,128]{2,1,0:T(4,128)S(1)}, u32[]{:S(2)}, u32[]{:S(2)}) async-start(f32[32,4,128]{2,1,0:T(4,128)} %pad_maximum_fusion.2), calls=%async_computation.7 | async-start | bytes 131072 | tf_op jit(solution)/shard_map/all_to_all | solution.py:77
  161.7 14.2 %collective-permute-start.7 = (f32[16,128]{1,0:T(8,128)S(1)}, f32[16,128]{1,0:T(8,128)S(1)}, u32[]{:S(2)}, u32[]{:S(2)}) collective-permute-start(f32[16,128]{1,0:T(8,128)S(1)} %slice.308), channel_id=1, source_target_pairs={{0,16},{16,32},{32,48},{48,64},{64,80},{80,96},{96,112},{112,128},... | collective-permute-start | bytes 24584 | tf_op jit(solution)/shard_map/ppermute | solution.py:13
  207.6 12.6 %collective-permute-start.8 = (bf16[16,128]{1,0:T(8,128)(2,1)S(1)}, bf16[16,128]{1,0:T(8,128)(2,1)S(1)}, u32[]{:S(2)}, u32[]{:S(2)}) collective-permute-start(bf16[16,128]{1,0:T(8,128)(2,1)S(1)} %slice.310), channel_id=1, source_target_pairs={{16,0},{32,16},{48,32},{64,48},{80,64},{96,80},{112,96},{128,112},... | collective-permute-start | bytes 12296 | tf_op jit(solution)/shard_map/ppermute | solution.py:13
  211.9 17.1 %all-to-all-start.10 = ((f32[32,4,128]{2,1,0:T(4,128)}), f32[32,4,128]{2,1,0:T(4,128)S(1)}, u32[]{:S(2)}, u32[]{:S(2)}) async-start(f32[32,4,128]{2,1,0:T(4,128)} %pad_maximum_fusion.3), calls=%async_computation.10 | async-start | bytes 131072 | tf_op jit(solution)/shard_map/all_to_all | solution.py:77
  216.6 14.2 %collective-permute-start.9 = (f32[16,128]{1,0:T(8,128)S(1)}, f32[16,128]{1,0:T(8,128)S(1)}, u32[]{:S(2)}, u32[]{:S(2)}) collective-permute-start(f32[16,128]{1,0:T(8,128)S(1)} %slice.315), channel_id=1, source_target_pairs={{0,16},{16,32},{32,48},{48,64},{64,80},{80,96},{96,112},{112,128},... | collective-permute-start | bytes 24584 | tf_op jit(solution)/shard_map/ppermute | solution.py:13
  242.5 13.8 %collective-permute-start.10 = (bf16[16,128]{1,0:T(8,128)(2,1)S(1)}, bf16[16,128]{1,0:T(8,128)(2,1)S(1)}, u32[]{:S(2)}, u32[]{:S(2)}) collective-permute-start(bf16[16,128]{1,0:T(8,128)(2,1)S(1)} %slice.317), channel_id=1, source_target_pairs={{16,0},{32,16},{48,32},{64,48},{80,64},{96,80},{112,96},{128,112},... | collective-permute-start | bytes 12296 | tf_op jit(solution)/shard_map/ppermute | solution.py:13
  248.8 16.3 %all-to-all-start.12 = ((f32[32,4,128]{2,1,0:T(4,128)}), f32[32,4,128]{2,1,0:T(4,128)S(1)}, u32[]{:S(2)}, u32[]{:S(2)}) async-start(f32[32,4,128]{2,1,0:T(4,128)} %pad_maximum_fusion.4), calls=%async_computation.12 | async-start | bytes 131072 | tf_op jit(solution)/shard_map/all_to_all | solution.py:77
  253.1 13.9 %collective-permute-start.11 = (f32[16,128]{1,0:T(8,128)S(1)}, f32[16,128]{1,0:T(8,128)S(1)}, u32[]{:S(2)}, u32[]{:S(2)}) collective-permute-start(f32[16,128]{1,0:T(8,128)S(1)} %slice.322), channel_id=1, source_target_pairs={{0,16},{16,32},{32,48},{48,64},{64,80},{80,96},{96,112},{112,128},... | collective-permute-start | bytes 24584 | tf_op jit(solution)/shard_map/ppermute | solution.py:13
  303.7 12.6 %collective-permute-start.12 = (bf16[16,128]{1,0:T(8,128)(2,1)S(1)}, bf16[16,128]{1,0:T(8,128)(2,1)S(1)}, u32[]{:S(2)}, u32[]{:S(2)}) collective-permute-start(bf16[16,128]{1,0:T(8,128)(2,1)S(1)} %slice.324), channel_id=1, source_target_pairs={{16,0},{32,16},{48,32},{64,48},{80,64},{96,80},{112,96},{128,112},... | collective-permute-start | bytes 12296 | tf_op jit(solution)/shard_map/ppermute | solution.py:13
  308.0 17.1 %all-to-all-start.15 = ((f32[32,4,128]{2,1,0:T(4,128)}), f32[32,4,128]{2,1,0:T(4,128)S(1)}, u32[]{:S(2)}, u32[]{:S(2)}) async-start(f32[32,4,128]{2,1,0:T(4,128)} %pad_maximum_fusion.5), calls=%async_computation.15 | async-start | bytes 131072 | tf_op jit(solution)/shard_map/all_to_all | solution.py:77
  312.7 14.2 %collective-permute-start.13 = (f32[16,128]{1,0:T(8,128)S(1)}, f32[16,128]{1,0:T(8,128)S(1)}, u32[]{:S(2)}, u32[]{:S(2)}) collective-permute-start(f32[16,128]{1,0:T(8,128)S(1)} %slice.329), channel_id=1, source_target_pairs={{0,16},{16,32},{32,48},{48,64},{64,80},{80,96},{96,112},{112,128},... | collective-permute-start | bytes 24584 | tf_op jit(solution)/shard_map/ppermute | solution.py:13

commit v5 on v4

--- a/solution.py
+++ b/solution.py
@@ -108,18 +108,22 @@
         residual = 1.0 - balance
         scaled = residual / balance
         direction = scaled
-        local_product = jnp.sum(residual * scaled)
+        local_product = residual * scaled
         growth = jnp.ones_like(scaling)
         for inner_step in range(INNER):
             curved = scaling * multiply(scaling * direction, wanted)[0] + balance * direction
             last = inner_step + 1 == INNER
-            parts = [jnp.sum(direction * curved)]
+            parts = [direction * curved]
             if inner_step == 0:
                 parts.append(local_product)
             if not last:
-                parts.append(jnp.sum(residual * curved / balance))
-                parts.append(jnp.sum(curved * curved / balance))
-            totals = all_sum(jnp.stack(parts), "row")
+                parts.append(residual * curved / balance)
+                parts.append(curved * curved / balance)
+            stacked = jnp.stack(parts).reshape(len(parts), -1)
+            local_totals = jnp.dot(
+                stacked, jnp.ones((stacked.shape[1],), jnp.float32), precision=lax.Precision.HIGHEST
+            )
+            totals = all_sum(local_totals, "row")
             curvature = totals[0]
             if inner_step == 0:
                 current_residual_product = totals[1]

time: 360 us -> 357 us (level)
  other arithmetic: 18.6 us -> 14.4 us
    another operation x2 -> x0, other arithmetic: 5.23 us -> none  [on_device(): totals = all_sum(jnp.stack(parts), 'row')]
where the time goes in v5:
time: 357 us; the launch traced here: 355 us
  blocking collectives  131 us (37%)
  starting transfers between devices  96.3 us (27%)
  waiting for transfers between devices  63.5 us (18%)
  matrix products  24.4 us (7%)
  local copies, waits for them, and re-layouts  15 us (4%)
  other arithmetic  14.4 us (4%)
  between operations  10.9 us (3%)
    all_to_all x10, blocking collectives, all_sum(): return jnp.sum(lax.all_to_all(copies, axis, 0, 0, tiled=True), 0)  131 us
    ppermute x14, starting transfers between devices, shifted(): lax.ppermute(value, axis, [(source, source + steps) for source in range(l...  55.9 us
    all_to_all x6, waiting for transfers between devices, multiply(): lax.all_to_all(jnp.concatenate([outgoing, far_backward], 1), 'row', split...  48.6 us
    all_to_all x6, starting transfers between devices, multiply(): lax.all_to_all(jnp.concatenate([outgoing, far_backward], 1), 'row', split...  23.6 us
    all_to_all x1, starting transfers between devices, multiply(): lax.all_to_all(jnp.concatenate([column_row, far_backward], 1), 'row', spl...  10 us
    dot_general x7, matrix products, multiply(): jnp.einsum('oqht,oqt->oqh', distant_local_part, gathered_values, preferre...  8.22 us
    all_to_all x1, waiting for transfers between devices, multiply(): lax.all_to_all(jnp.concatenate([column_row, far_backward], 1), 'row', spl...  7.55 us
    all_to_all x1, waiting for transfers between devices, all_sum(): return jnp.sum(lax.all_to_all(copies, axis, 0, 0, tiled=True), 0)  7.26 us
  transfers between devices with their start and end apart: 22, of which 8 were waited for; matrix products, arithmetic and copies ran while one was open for 10% of the time, Pallas kernels for 0%

profile of v5, /device:TPU:1, one launch (start us, length us, event | category | flops | bytes accessed | tf_op | source)
XLA Modules:
  0.0 355.4 jit_solution(6767166366752800694)
XLA Ops:
  0.7 8.9 %collective-permute-start = (bf16[16,128]{1,0:T(8,128)(2,1)S(1)}, bf16[16,128]{1,0:T(8,128)(2,1)S(1)}, u32[]{:S(2)}, u32[]{:S(2)}) collective-permute-start(bf16[16,128]{1,0:T(8,128)(2,1)S(1)} %slice.200), channel_id=1, source_target_pairs={{16,0},{32,16},{48,32},{64,48},{80,64},{96,80},{112,96},{128,112},... | collective-permute-start | bytes 12296 | tf_op jit(solution)/shard_map/ppermute | solution.py:13
  14.6 10.0 %all-to-all-start = ((f32[32,3,128]{2,1,0:T(4,128)}), f32[32,3,128]{2,1,0:T(4,128)S(1)}, u32[]{:S(2)}, u32[]{:S(2)}) async-start(f32[32,3,128]{2,1,0:T(4,128)} %select_maximum_fusion), calls=%async_computation | async-start | bytes 131072 | tf_op jit(solution)/shard_map/all_to_all | solution.py:69
  25.3 3.5 collective-permute-start.1
  30.1 7.5 %all-to-all-done = f32[32,3,128]{2,1,0:T(4,128)S(1)} async-done(((f32[32,3,128]{2,1,0:T(4,128)}), f32[32,3,128]{2,1,0:T(4,128)S(1)}, u32[]{:S(2)}, u32[]{:S(2)}) %all-to-all-start) | async-done | bytes 49184 | tf_op jit(solution)/shard_map/all_to_all | solution.py:69
  38.8 6.8 %all-to-all-start.1 = ((f32[16,32,128]{2,1,0:T(8,128)}), f32[16,32,128]{2,1,0:T(8,128)S(1)}, u32[]{:S(2)}, u32[]{:S(2)}) async-start(f32[16,32,128]{2,1,0:T(8,128)} %broadcast_in_dim.25), calls=%async_computation.1 | async-start | bytes 524288 | tf_op jit(solution)/shard_map/all_to_all | solution.py:19
  45.9 7.3 %all-to-all-done.1 = f32[16,32,128]{2,1,0:T(8,128)S(1)} async-done(((f32[16,32,128]{2,1,0:T(8,128)}), f32[16,32,128]{2,1,0:T(8,128)S(1)}, u32[]{:S(2)}, u32[]{:S(2)}) %all-to-all-start.1) | async-done | bytes 262176 | tf_op jit(solution)/shard_map/all_to_all | solution.py:19
  53.9 4.9 %collective-permute-start.2 = (bf16[16,128]{1,0:T(8,128)(2,1)S(1)}, bf16[16,128]{1,0:T(8,128)(2,1)S(1)}, u32[]{:S(2)}, u32[]{:S(2)}) collective-permute-start(bf16[16,128]{1,0:T(8,128)(2,1)S(1)} %slice.289), channel_id=1, source_target_pairs={{16,0},{32,16},{48,32},{64,48},{80,64},{96,80},{112,96},{128,112},... | collective-permute-start | bytes 12296 | tf_op jit(solution)/shard_map/ppermute | solution.py:13
  60.9 4.1 %all-to-all-start.2 = ((f32[32,4,128]{2,1,0:T(4,128)}), f32[32,4,128]{2,1,0:T(4,128)S(1)}, u32[]{:S(2)}, u32[]{:S(2)}) async-start(f32[32,4,128]{2,1,0:T(4,128)} %pad_maximum_fusion), calls=%async_computation.2 | async-start | bytes 131072 | tf_op jit(solution)/shard_map/all_to_all | solution.py:77
  65.6 3.5 collective-permute-start.3
  69.8 8.1 %all-to-all-done.2 = f32[32,4,128]{2,1,0:T(4,128)S(1)} async-done(((f32[32,4,128]{2,1,0:T(4,128)}), f32[32,4,128]{2,1,0:T(4,128)S(1)}, u32[]{:S(2)}, u32[]{:S(2)}) %all-to-all-start.2) | async-done | bytes 65568 | tf_op jit(solution)/shard_map/all_to_all | solution.py:77
  79.9 10.2 %all_to_all.94 = f32[16,32,128]{2,1,0:T(8,128)S(1)} all-to-all(f32[16,32,128]{2,1,0:T(8,128)S(1)} %broadcast_in_dim.26), channel_id=1, replica_groups=mesh['row'=32,'band'=16] {'band'}, dimensions={0} | all-to-all | bytes 524288 | tf_op jit(solution)/shard_map/all_to_all | solution.py:19
  91.4 4.9 %collective-permute-start.4 = (bf16[16,128]{1,0:T(8,128)(2,1)S(1)}, bf16[16,128]{1,0:T(8,128)(2,1)S(1)}, u32[]{:S(2)}, u32[]{:S(2)}) collective-permute-start(bf16[16,128]{1,0:T(8,128)(2,1)S(1)} %slice.296), channel_id=1, source_target_pairs={{16,0},{32,16},{48,32},{64,48},{80,64},{96,80},{112,96},{128,112},... | collective-permute-start | bytes 12296 | tf_op jit(solution)/shard_map/ppermute | solution.py:13
  97.8 3.6 %all-to-all-start.4 = ((f32[32,4,128]{2,1,0:T(4,128)}), f32[32,4,128]{2,1,0:T(4,128)S(1)}, u32[]{:S(2)}, u32[]{:S(2)}) async-start(f32[32,4,128]{2,1,0:T(4,128)} %pad_maximum_fusion.1), calls=%async_computation.4 | async-start | bytes 131072 | tf_op jit(solution)/shard_map/all_to_all | solution.py:77
  105.9 8.2 %all-to-all-done.4 = f32[32,4,128]{2,1,0:T(4,128)S(1)} async-done(((f32[32,4,128]{2,1,0:T(4,128)}), f32[32,4,128]{2,1,0:T(4,128)S(1)}, u32[]{:S(2)}, u32[]{:S(2)}) %all-to-all-start.4) | async-done | bytes 65568 | tf_op jit(solution)/shard_map/all_to_all | solution.py:77
  116.1 10.3 %all_to_all.95 = f32[16,32,128]{2,1,0:T(8,128)S(1)} all-to-all(f32[16,32,128]{2,1,0:T(8,128)S(1)} %broadcast_in_dim.27), channel_id=1, replica_groups=mesh['row'=32,'band'=16] {'band'}, dimensions={0} | all-to-all | bytes 524288 | tf_op jit(solution)/shard_map/all_to_all | solution.py:19
  127.5 17.3 %all_to_all.96 = f32[32,1,4]{2,1,0:T(1,128)S(1)} all-to-all(f32[32,1,4]{2,1,0:T(1,128)S(1)} %broadcast_in_dim.28), channel_id=1, replica_groups=mesh['row'=32,'band'=16] {'row'}, dimensions={0} | all-to-all | bytes 1024 | tf_op jit(solution)/shard_map/all_to_all | solution.py:19
  154.8 4.1 %all-to-all-start.7 = ((f32[32,4,128]{2,1,0:T(4,128)}), f32[32,4,128]{2,1,0:T(4,128)S(1)}, u32[]{:S(2)}, u32[]{:S(2)}) async-start(f32[32,4,128]{2,1,0:T(4,128)} %pad_maximum_fusion.4), calls=%async_computation.7 | async-start | bytes 131072 | tf_op jit(solution)/shard_map/all_to_all | solution.py:77
  163.8 8.1 %all-to-all-done.7 = f32[32,4,128]{2,1,0:T(4,128)S(1)} async-done(((f32[32,4,128]{2,1,0:T(4,128)}), f32[32,4,128]{2,1,0:T(4,128)S(1)}, u32[]{:S(2)}, u32[]{:S(2)}) %all-to-all-start.7) | async-done | bytes 65568 | tf_op jit(solution)/shard_map/all_to_all | solution.py:77
  173.9 10.2 %all_to_all.97 = f32[16,32,128]{2,1,0:T(8,128)S(1)} all-to-all(f32[16,32,128]{2,1,0:T(8,128)S(1)} %broadcast_in_dim.29), channel_id=1, replica_groups=mesh['row'=32,'band'=16] {'band'}, dimensions={0} | all-to-all | bytes 524288 | tf_op jit(solution)/shard_map/all_to_all | solution.py:19
  185.4 17.5 %all_to_all.98 = f32[32,1,1]{2,1,0:T(1,128)S(1)} all-to-all(f32[32,1,1]{2,1,0:T(1,128)S(1)} %broadcast_in_dim.30), channel_id=1, replica_groups=mesh['row'=32,'band'=16] {'row'}, dimensions={0} | all-to-all | bytes 256 | tf_op jit(solution)/shard_map/all_to_all | solution.py:19
  209.8 4.1 %all-to-all-start.10 = ((f32[32,4,128]{2,1,0:T(4,128)}), f32[32,4,128]{2,1,0:T(4,128)S(1)}, u32[]{:S(2)}, u32[]{:S(2)}) async-start(f32[32,4,128]{2,1,0:T(4,128)} %pad_maximum_fusion.5), calls=%async_computation.10 | async-start | bytes 131072 | tf_op jit(solution)/shard_map/all_to_all | solution.py:77
  218.8 8.1 %all-to-all-done.10 = f32[32,4,128]{2,1,0:T(4,128)S(1)} async-done(((f32[32,4,128]{2,1,0:T(4,128)}), f32[32,4,128]{2,1,0:T(4,128)S(1)}, u32[]{:S(2)}, u32[]{:S(2)}) %all-to-all-start.10) | async-done | bytes 65568 | tf_op jit(solution)/shard_map/all_to_all | solution.py:77
  228.9 10.2 %all_to_all.99 = f32[16,32,128]{2,1,0:T(8,128)S(1)} all-to-all(f32[16,32,128]{2,1,0:T(8,128)S(1)} %broadcast_in_dim.31), channel_id=1, replica_groups=mesh['row'=32,'band'=16] {'band'}, dimensions={0} | all-to-all | bytes 524288 | tf_op jit(solution)/shard_map/all_to_all | solution.py:19
  241.0 4.9 %collective-permute-start.10 = (bf16[16,128]{1,0:T(8,128)(2,1)S(1)}, bf16[16,128]{1,0:T(8,128)(2,1)S(1)}, u32[]{:S(2)}, u32[]{:S(2)}) collective-permute-start(bf16[16,128]{1,0:T(8,128)(2,1)S(1)} %slice.317), channel_id=1, source_target_pairs={{16,0},{32,16},{48,32},{64,48},{80,64},{96,80},{112,96},{128,112},... | collective-permute-start | bytes 12296 | tf_op jit(solution)/shard_map/ppermute | solution.py:13
  247.3 3.6 %all-to-all-start.12 = ((f32[32,4,128]{2,1,0:T(4,128)}), f32[32,4,128]{2,1,0:T(4,128)S(1)}, u32[]{:S(2)}, u32[]{:S(2)}) async-start(f32[32,4,128]{2,1,0:T(4,128)} %pad_maximum_fusion.6), calls=%async_computation.12 | async-start | bytes 131072 | tf_op jit(solution)/shard_map/all_to_all | solution.py:77
  255.5 8.2 %all-to-all-done.12 = f32[32,4,128]{2,1,0:T(4,128)S(1)} async-done(((f32[32,4,128]{2,1,0:T(4,128)}), f32[32,4,128]{2,1,0:T(4,128)S(1)}, u32[]{:S(2)}, u32[]{:S(2)}) %all-to-all-start.12) | async-done | bytes 65568 | tf_op jit(solution)/shard_map/all_to_all | solution.py:77
  265.6 10.3 %all_to_all.100 = f32[16,32,128]{2,1,0:T(8,128)S(1)} all-to-all(f32[16,32,128]{2,1,0:T(8,128)S(1)} %broadcast_in_dim.32), channel_id=1, replica_groups=mesh['row'=32,'band'=16] {'band'}, dimensions={0} | all-to-all | bytes 524288 | tf_op jit(solution)/shard_map/all_to_all | solution.py:19
  277.2 17.3 %all_to_all.101 = f32[32,1,4]{2,1,0:T(1,128)S(1)} all-to-all(f32[32,1,4]{2,1,0:T(1,128)S(1)} %broadcast_in_dim.33), channel_id=1, replica_groups=mesh['row'=32,'band'=16] {'row'}, dimensions={0} | all-to-all | bytes 1024 | tf_op jit(solution)/shard_map/all_to_all | solution.py:19
  305.3 4.1 %all-to-all-start.15 = ((f32[32,4,128]{2,1,0:T(4,128)}), f32[32,4,128]{2,1,0:T(4,128)S(1)}, u32[]{:S(2)}, u32[]{:S(2)}) async-start(f32[32,4,128]{2,1,0:T(4,128)} %pad_maximum_fusion.9), calls=%async_computation.15 | async-start | bytes 131072 | tf_op jit(solution)/shard_map/all_to_all | solution.py:77
  314.3 8.1 %all-to-all-done.15 = f32[32,4,128]{2,1,0:T(4,128)S(1)} async-done(((f32[32,4,128]{2,1,0:T(4,128)}), f32[32,4,128]{2,1,0:T(4,128)S(1)}, u32[]{:S(2)}, u32[]{:S(2)}) %all-to-all-start.15) | async-done | bytes 65568 | tf_op jit(solution)/shard_map/all_to_all | solution.py:77
  324.4 10.2 %all_to_all.102 = f32[16,32,128]{2,1,0:T(8,128)S(1)} all-to-all(f32[16,32,128]{2,1,0:T(8,128)S(1)} %broadcast_in_dim.34), channel_id=1, replica_groups=mesh['row'=32,'band'=16] {'band'}, dimensions={0} | all-to-all | bytes 524288 | tf_op jit(solution)/shard_map/all_to_all | solution.py:19
  335.9 17.5 %all_to_all.103 = f32[32,1,1]{2,1,0:T(1,128)S(1)} all-to-all(f32[32,1,1]{2,1,0:T(1,128)S(1)} %broadcast_in_dim.35), channel_id=1, replica_groups=mesh['row'=32,'band'=16] {'row'}, dimensions={0} | all-to-all | bytes 256 | tf_op jit(solution)/shard_map/all_to_all | solution.py:19
  (256 shorter events, 79.1 us)
Async XLA Ops:
  0.6 10.5 %copy-start = (bf16[1,1,32,2,128,128]{5,4,3,2,1,0:T(8,128)(2,1)S(1)}, bf16[1,1,32,2,128,128]{5,4,3,2,1,0:T(8,128)(2,1)}, u32[]{:S(2)}) copy-start(bf16[1,1,32,2,128,128]{5,4,3,2,1,0:T(8,128)(2,1)} %param.8) | copy-start | bytes 6291460
  0.7 28.4 %collective-permute-start = (bf16[16,128]{1,0:T(8,128)(2,1)S(1)}, bf16[16,128]{1,0:T(8,128)(2,1)S(1)}, u32[]{:S(2)}, u32[]{:S(2)}) collective-permute-start(bf16[16,128]{1,0:T(8,128)(2,1)S(1)} %slice.200), channel_id=1, source_target_pairs={{16,0},{32,16},{48,32},{64,48},{80,64},{96,80},{112,96},{128,112},... | collective-permute-start | bytes 12296 | tf_op jit(solution)/shard_map/ppermute | solution.py:13
  11.2 2.5 copy-start.7
  11.2 13.4 %copy-start.1 = (bf16[32,1,128,128]{3,2,1,0:T(8,128)(2,1)S(1)}, bf16[32,1,128,128]{3,2,1,0:T(8,128)(2,1)}, u32[]{:S(2)}) copy-start(bf16[32,1,128,128]{3,2,1,0:T(8,128)(2,1)} %param.7) | copy-start | bytes 3145732
  12.4 16.5 %copy-start.6 = (s32[1,1,32,2]{2,3,1,0:T(2,128)S(1)}, s32[1,1,32,2]{2,3,1,0:T(2,128)}, u32[]{:S(2)}) copy-start(s32[1,1,32,2]{2,3,1,0:T(2,128)} %param.9) | copy-start | bytes 772
  14.6 23.0 %all-to-all-start = ((f32[32,3,128]{2,1,0:T(4,128)}), f32[32,3,128]{2,1,0:T(4,128)S(1)}, u32[]{:S(2)}, u32[]{:S(2)}) async-start(f32[32,3,128]{2,1,0:T(4,128)} %select_maximum_fusion), calls=%async_computation | async-start | bytes 131072 | tf_op jit(solution)/shard_map/all_to_all | solution.py:69
  25.3 12.8 %collective-permute-start.1 = (f32[16,128]{1,0:T(8,128)S(1)}, f32[16,128]{1,0:T(8,128)S(1)}, u32[]{:S(2)}, u32[]{:S(2)}) collective-permute-start(f32[16,128]{1,0:T(8,128)S(1)} %slice.287), channel_id=1, source_target_pairs={{0,16},{16,32},{32,48},{48,64},{64,80},{80,96},{96,112},{112,128},... | collective-permute-start | bytes 24584 | tf_op jit(solution)/shard_map/ppermute | solution.py:13
  28.8 236.1 %copy-start.10 = (f32[32]{0:T(128)}, f32[32]{0:T(128)S(1)}, u32[]{:S(2)}) copy-start(f32[32]{0:T(128)S(1)} %compare_convert_fusion) | copy-start | bytes 388
  29.1 235.9 %copy-start.8 = (s32[64]{0:T(128)}, s32[64]{0:T(128)S(1)}, u32[]{:S(2)}) copy-start(s32[64]{0:T(128)S(1)} %eq.14) | copy-start | bytes 772
  38.8 14.3 %all-to-all-start.1 = ((f32[16,32,128]{2,1,0:T(8,128)}), f32[16,32,128]{2,1,0:T(8,128)S(1)}, u32[]{:S(2)}, u32[]{:S(2)}) async-start(f32[16,32,128]{2,1,0:T(8,128)} %broadcast_in_dim.25), calls=%async_computation.1 | async-start | bytes 524288 | tf_op jit(solution)/shard_map/all_to_all | solution.py:19
  53.9 15.3 %collective-permute-start.2 = (bf16[16,128]{1,0:T(8,128)(2,1)S(1)}, bf16[16,128]{1,0:T(8,128)(2,1)S(1)}, u32[]{:S(2)}, u32[]{:S(2)}) collective-permute-start(bf16[16,128]{1,0:T(8,128)(2,1)S(1)} %slice.289), channel_id=1, source_target_pairs={{16,0},{32,16},{48,32},{64,48},{80,64},{96,80},{112,96},{128,112},... | collective-permute-start | bytes 12296 | tf_op jit(solution)/shard_map/ppermute | solution.py:13
  60.9 17.1 %all-to-all-start.2 = ((f32[32,4,128]{2,1,0:T(4,128)}), f32[32,4,128]{2,1,0:T(4,128)S(1)}, u32[]{:S(2)}, u32[]{:S(2)}) async-start(f32[32,4,128]{2,1,0:T(4,128)} %pad_maximum_fusion), calls=%async_computation.2 | async-start | bytes 131072 | tf_op jit(solution)/shard_map/all_to_all | solution.py:77
  65.6 14.2 %collective-permute-start.3 = (f32[16,128]{1,0:T(8,128)S(1)}, f32[16,128]{1,0:T(8,128)S(1)}, u32[]{:S(2)}, u32[]{:S(2)}) collective-permute-start(f32[16,128]{1,0:T(8,128)S(1)} %slice.294), channel_id=1, source_target_pairs={{0,16},{16,32},{32,48},{48,64},{64,80},{80,96},{96,112},{112,128},... | collective-permute-start | bytes 24584 | tf_op jit(solution)/shard_map/ppermute | solution.py:13
  91.4 13.8 %collective-permute-start.4 = (bf16[16,128]{1,0:T(8,128)(2,1)S(1)}, bf16[16,128]{1,0:T(8,128)(2,1)S(1)}, u32[]{:S(2)}, u32[]{:S(2)}) collective-permute-start(bf16[16,128]{1,0:T(8,128)(2,1)S(1)} %slice.296), channel_id=1, source_target_pairs={{16,0},{32,16},{48,32},{64,48},{80,64},{96,80},{112,96},{128,112},... | collective-permute-start | bytes 12296 | tf_op jit(solution)/shard_map/ppermute | solution.py:13
  97.8 16.3 %all-to-all-start.4 = ((f32[32,4,128]{2,1,0:T(4,128)}), f32[32,4,128]{2,1,0:T(4,128)S(1)}, u32[]{:S(2)}, u32[]{:S(2)}) async-start(f32[32,4,128]{2,1,0:T(4,128)} %pad_maximum_fusion.1), calls=%async_computation.4 | async-start | bytes 131072 | tf_op jit(solution)/shard_map/all_to_all | solution.py:77
  102.1 13.9 %collective-permute-start.5 = (f32[16,128]{1,0:T(8,128)S(1)}, f32[16,128]{1,0:T(8,128)S(1)}, u32[]{:S(2)}, u32[]{:S(2)}) collective-permute-start(f32[16,128]{1,0:T(8,128)S(1)} %slice.301), channel_id=1, source_target_pairs={{0,16},{16,32},{32,48},{48,64},{64,80},{80,96},{96,112},{112,128},... | collective-permute-start | bytes 24584 | tf_op jit(solution)/shard_map/ppermute | solution.py:13
  126.4 0.6 copy-start.4
  150.6 12.6 %collective-permute-start.6 = (bf16[16,128]{1,0:T(8,128)(2,1)S(1)}, bf16[16,128]{1,0:T(8,128)(2,1)S(1)}, u32[]{:S(2)}, u32[]{:S(2)}) collective-permute-start(bf16[16,128]{1,0:T(8,128)(2,1)S(1)} %slice.303), channel_id=1, source_target_pairs={{16,0},{32,16},{48,32},{64,48},{80,64},{96,80},{112,96},{128,112},... | collective-permute-start | bytes 12296 | tf_op jit(solution)/shard_map/ppermute | solution.py:13
  154.8 17.1 %all-to-all-start.7 = ((f32[32,4,128]{2,1,0:T(4,128)}), f32[32,4,128]{2,1,0:T(4,128)S(1)}, u32[]{:S(2)}, u32[]{:S(2)}) async-start(f32[32,4,128]{2,1,0:T(4,128)} %pad_maximum_fusion.4), calls=%async_computation.7 | async-start | bytes 131072 | tf_op jit(solution)/shard_map/all_to_all | solution.py:77
  159.6 14.2 %collective-permute-start.7 = (f32[16,128]{1,0:T(8,128)S(1)}, f32[16,128]{1,0:T(8,128)S(1)}, u32[]{:S(2)}, u32[]{:S(2)}) collective-permute-start(f32[16,128]{1,0:T(8,128)S(1)} %slice.308), channel_id=1, source_target_pairs={{0,16},{16,32},{32,48},{48,64},{64,80},{80,96},{96,112},{112,128},... | collective-permute-start | bytes 24584 | tf_op jit(solution)/shard_map/ppermute | solution.py:13
  205.6 12.6 %collective-permute-start.8 = (bf16[16,128]{1,0:T(8,128)(2,1)S(1)}, bf16[16,128]{1,0:T(8,128)(2,1)S(1)}, u32[]{:S(2)}, u32[]{:S(2)}) collective-permute-start(bf16[16,128]{1,0:T(8,128)(2,1)S(1)} %slice.310), channel_id=1, source_target_pairs={{16,0},{32,16},{48,32},{64,48},{80,64},{96,80},{112,96},{128,112},... | collective-permute-start | bytes 12296 | tf_op jit(solution)/shard_map/ppermute | solution.py:13
  209.8 17.1 %all-to-all-start.10 = ((f32[32,4,128]{2,1,0:T(4,128)}), f32[32,4,128]{2,1,0:T(4,128)S(1)}, u32[]{:S(2)}, u32[]{:S(2)}) async-start(f32[32,4,128]{2,1,0:T(4,128)} %pad_maximum_fusion.5), calls=%async_computation.10 | async-start | bytes 131072 | tf_op jit(solution)/shard_map/all_to_all | solution.py:77
  214.6 14.2 %collective-permute-start.9 = (f32[16,128]{1,0:T(8,128)S(1)}, f32[16,128]{1,0:T(8,128)S(1)}, u32[]{:S(2)}, u32[]{:S(2)}) collective-permute-start(f32[16,128]{1,0:T(8,128)S(1)} %slice.315), channel_id=1, source_target_pairs={{0,16},{16,32},{32,48},{48,64},{64,80},{80,96},{96,112},{112,128},... | collective-permute-start | bytes 24584 | tf_op jit(solution)/shard_map/ppermute | solution.py:13
  241.0 13.8 %collective-permute-start.10 = (bf16[16,128]{1,0:T(8,128)(2,1)S(1)}, bf16[16,128]{1,0:T(8,128)(2,1)S(1)}, u32[]{:S(2)}, u32[]{:S(2)}) collective-permute-start(bf16[16,128]{1,0:T(8,128)(2,1)S(1)} %slice.317), channel_id=1, source_target_pairs={{16,0},{32,16},{48,32},{64,48},{80,64},{96,80},{112,96},{128,112},... | collective-permute-start | bytes 12296 | tf_op jit(solution)/shard_map/ppermute | solution.py:13
  247.3 16.3 %all-to-all-start.12 = ((f32[32,4,128]{2,1,0:T(4,128)}), f32[32,4,128]{2,1,0:T(4,128)S(1)}, u32[]{:S(2)}, u32[]{:S(2)}) async-start(f32[32,4,128]{2,1,0:T(4,128)} %pad_maximum_fusion.6), calls=%async_computation.12 | async-start | bytes 131072 | tf_op jit(solution)/shard_map/all_to_all | solution.py:77
  251.6 13.9 %collective-permute-start.11 = (f32[16,128]{1,0:T(8,128)S(1)}, f32[16,128]{1,0:T(8,128)S(1)}, u32[]{:S(2)}, u32[]{:S(2)}) collective-permute-start(f32[16,128]{1,0:T(8,128)S(1)} %slice.322), channel_id=1, source_target_pairs={{0,16},{16,32},{32,48},{48,64},{64,80},{80,96},{96,112},{112,128},... | collective-permute-start | bytes 24584 | tf_op jit(solution)/shard_map/ppermute | solution.py:13
  301.0 12.6 %collective-permute-start.12 = (bf16[16,128]{1,0:T(8,128)(2,1)S(1)}, bf16[16,128]{1,0:T(8,128)(2,1)S(1)}, u32[]{:S(2)}, u32[]{:S(2)}) collective-permute-start(bf16[16,128]{1,0:T(8,128)(2,1)S(1)} %slice.324), channel_id=1, source_target_pairs={{16,0},{32,16},{48,32},{64,48},{80,64},{96,80},{112,96},{128,112},... | collective-permute-start | bytes 12296 | tf_op jit(solution)/shard_map/ppermute | solution.py:13
  305.3 17.1 %all-to-all-start.15 = ((f32[32,4,128]{2,1,0:T(4,128)}), f32[32,4,128]{2,1,0:T(4,128)S(1)}, u32[]{:S(2)}, u32[]{:S(2)}) async-start(f32[32,4,128]{2,1,0:T(4,128)} %pad_maximum_fusion.9), calls=%async_computation.15 | async-start | bytes 131072 | tf_op jit(solution)/shard_map/all_to_all | solution.py:77
  309.4 14.3 %copy-start.9 = (s32[64]{0:T(128)S(1)}, s32[64]{0:T(128)}, u32[]{:S(2)}) copy-start(s32[64]{0:T(128)} %copy-done.8) | copy-start | bytes 772
  309.4 14.3 %copy-start.11 = (f32[32]{0:T(128)S(1)}, f32[32]{0:T(128)}, u32[]{:S(2)}) copy-start(f32[32]{0:T(128)} %copy-done.10) | copy-start | bytes 388
  310.1 14.2 %collective-permute-start.13 = (f32[16,128]{1,0:T(8,128)S(1)}, f32[16,128]{1,0:T(8,128)S(1)}, u32[]{:S(2)}, u32[]{:S(2)}) collective-permute-start(f32[16,128]{1,0:T(8,128)S(1)} %slice.329), channel_id=1, source_target_pairs={{0,16},{16,32},{32,48},{48,64},{64,80},{80,96},{96,112},{112,128},... | collective-permute-start | bytes 24584 | tf_op jit(solution)/shard_map/ppermute | solution.py:13
  314.3 40.4 %copy-start.2 = (f32[32,128]{1,0:T(8,128)S(1)}, f32[32,128]{1,0:T(8,128)}, u32[]{:S(2)}) copy-start(f32[32,128]{1,0:T(8,128)} %get-tuple-element.19) | copy-start | bytes 49156
  (2 other events, 1.2 us)

commit v6 on v5

--- a/solution.py
+++ b/solution.py
@@ -17,6 +17,13 @@
     count = lax.axis_size(axis)
     copies = jnp.broadcast_to(value[None], (count,) + value.shape)
     return jnp.sum(lax.all_to_all(copies, axis, 0, 0, tiled=True), 0)
+
+
+def lane_totals(value, axis, lanes):
+    count = lax.axis_size(axis)
+    copies = jnp.broadcast_to(value[None], (count,) + value.shape)
+    received = lax.all_to_all(copies, axis, 0, 0, tiled=True)
+    return jnp.dot(received.T, jnp.ones((count, lanes), jnp.float32), precision=lax.Precision.HIGHEST)
 
 
 def on_device(band_blocks, distant_block_slots, far_rows, far_columns, far_counts):
@@ -123,7 +130,7 @@
             local_totals = jnp.dot(
                 stacked, jnp.ones((stacked.shape[1],), jnp.float32), precision=lax.Precision.HIGHEST
             )
-            totals = all_sum(local_totals, "row")
+            totals = lane_totals(local_totals, "row", block_size)
             curvature = totals[0]
             if inner_step == 0:
                 current_residual_product = totals[1]

time: 357 us -> 347 us (0.972)
  between operations: 10.9 us -> 2.15 us
    all_to_all x0 -> x4, blocking collectives: none -> 69.6 us  [lane_totals(): received = lax.all_to_all(copies, axis, 0, 0, tiled=True)]
    all_to_all x10 -> x6, blocking collectives: 131 us -> 61.5 us  [all_sum(): return jnp.sum(lax.all_to_all(copies, axis, 0, 0, tiled=True), 0)]
where the time goes in v6:
time: 347 us; the launch traced here: 346 us
  blocking collectives  131 us (38%)
  starting transfers between devices  96.3 us (28%)
  waiting for transfers between devices  63.1 us (18%)
  matrix products  25 us (7%)
  local copies, waits for them, and re-layouts  15.1 us (4%)
  other arithmetic  12.9 us (4%)
    all_to_all x4, blocking collectives, lane_totals(): received = lax.all_to_all(copies, axis, 0, 0, tiled=True)  69.6 us
    all_to_all x6, blocking collectives, all_sum(): return jnp.sum(lax.all_to_all(copies, axis, 0, 0, tiled=True), 0)  61.5 us
    ppermute x14, starting transfers between devices, shifted(): lax.ppermute(value, axis, [(source, source + steps) for source in range(l...  55.9 us
    all_to_all x6, waiting for transfers between devices, multiply(): lax.all_to_all(jnp.concatenate([outgoing, far_backward], 1), 'row', split...  48.3 us
    all_to_all x6, starting transfers between devices, multiply(): lax.all_to_all(jnp.concatenate([outgoing, far_backward], 1), 'row', split...  23.6 us
    all_to_all x1, starting transfers between devices, multiply(): lax.all_to_all(jnp.concatenate([column_row, far_backward], 1), 'row', spl...  10 us
    dot_general x7, matrix products, multiply(): jnp.einsum('oqht,oqt->oqh', distant_local_part, gathered_values, preferre...  8.22 us
    all_to_all x1, waiting for transfers between devices, multiply(): lax.all_to_all(jnp.concatenate([column_row, far_backward], 1), 'row', spl...  7.55 us
  transfers between devices with their start and end apart: 22, of which 8 were waited for; matrix products, arithmetic and copies ran while one was open for 10% of the time, Pallas kernels for 0%

profile of v6, /device:TPU:1, one launch (start us, length us, event | category | flops | bytes accessed | tf_op | source)
XLA Modules:
  0.0 345.8 jit_solution(14470787572274697896)
XLA Ops:
  0.7 8.9 %collective-permute-start = (bf16[16,128]{1,0:T(8,128)(2,1)S(1)}, bf16[16,128]{1,0:T(8,128)(2,1)S(1)}, u32[]{:S(2)}, u32[]{:S(2)}) collective-permute-start(bf16[16,128]{1,0:T(8,128)(2,1)S(1)} %slice.200), channel_id=1, source_target_pairs={{16,0},{32,16},{48,32},{64,48},{80,64},{96,80},{112,96},{128,112},... | collective-permute-start | bytes 12296 | tf_op jit(solution)/shard_map/ppermute | solution.py:13
  14.5 10.0 %all-to-all-start = ((f32[32,3,128]{2,1,0:T(4,128)}), f32[32,3,128]{2,1,0:T(4,128)S(1)}, u32[]{:S(2)}, u32[]{:S(2)}) async-start(f32[32,3,128]{2,1,0:T(4,128)} %select_maximum_fusion), calls=%async_computation | async-start | bytes 131072 | tf_op jit(solution)/shard_map/all_to_all | solution.py:76
  25.3 3.5 %collective-permute-start.1 = (f32[16,128]{1,0:T(8,128)S(1)}, f32[16,128]{1,0:T(8,128)S(1)}, u32[]{:S(2)}, u32[]{:S(2)}) collective-permute-start(f32[16,128]{1,0:T(8,128)S(1)} %slice.287), channel_id=1, source_target_pairs={{0,16},{16,32},{32,48},{48,64},{64,80},{80,96},{96,112},{112,128},... | collective-permute-start | bytes 24584 | tf_op jit(solution)/shard_map/ppermute | solution.py:13
  30.0 7.5 %all-to-all-done = f32[32,3,128]{2,1,0:T(4,128)S(1)} async-done(((f32[32,3,128]{2,1,0:T(4,128)}), f32[32,3,128]{2,1,0:T(4,128)S(1)}, u32[]{:S(2)}, u32[]{:S(2)}) %all-to-all-start) | async-done | bytes 49184 | tf_op jit(solution)/shard_map/all_to_all | solution.py:76
  38.8 6.8 %all-to-all-start.1 = ((f32[16,32,128]{2,1,0:T(8,128)}), f32[16,32,128]{2,1,0:T(8,128)S(1)}, u32[]{:S(2)}, u32[]{:S(2)}) async-start(f32[16,32,128]{2,1,0:T(8,128)} %broadcast_in_dim.25), calls=%async_computation.1 | async-start | bytes 524288 | tf_op jit(solution)/shard_map/all_to_all | solution.py:19
  45.9 7.3 %all-to-all-done.1 = f32[16,32,128]{2,1,0:T(8,128)S(1)} async-done(((f32[16,32,128]{2,1,0:T(8,128)}), f32[16,32,128]{2,1,0:T(8,128)S(1)}, u32[]{:S(2)}, u32[]{:S(2)}) %all-to-all-start.1) | async-done | bytes 262176 | tf_op jit(solution)/shard_map/all_to_all | solution.py:19
  53.8 4.9 %collective-permute-start.2 = (bf16[16,128]{1,0:T(8,128)(2,1)S(1)}, bf16[16,128]{1,0:T(8,128)(2,1)S(1)}, u32[]{:S(2)}, u32[]{:S(2)}) collective-permute-start(bf16[16,128]{1,0:T(8,128)(2,1)S(1)} %slice.289), channel_id=1, source_target_pairs={{16,0},{32,16},{48,32},{64,48},{80,64},{96,80},{112,96},{128,112},... | collective-permute-start | bytes 12296 | tf_op jit(solution)/shard_map/ppermute | solution.py:13
  60.8 4.0 %all-to-all-start.2 = ((f32[32,4,128]{2,1,0:T(4,128)}), f32[32,4,128]{2,1,0:T(4,128)S(1)}, u32[]{:S(2)}, u32[]{:S(2)}) async-start(f32[32,4,128]{2,1,0:T(4,128)} %pad_maximum_fusion), calls=%async_computation.2 | async-start | bytes 131072 | tf_op jit(solution)/shard_map/all_to_all | solution.py:84
  65.6 3.5 %collective-permute-start.3 = (f32[16,128]{1,0:T(8,128)S(1)}, f32[16,128]{1,0:T(8,128)S(1)}, u32[]{:S(2)}, u32[]{:S(2)}) collective-permute-start(f32[16,128]{1,0:T(8,128)S(1)} %slice.294), channel_id=1, source_target_pairs={{0,16},{16,32},{32,48},{48,64},{64,80},{80,96},{96,112},{112,128},... | collective-permute-start | bytes 24584 | tf_op jit(solution)/shard_map/ppermute | solution.py:13
  69.8 8.1 %all-to-all-done.2 = f32[32,4,128]{2,1,0:T(4,128)S(1)} async-done(((f32[32,4,128]{2,1,0:T(4,128)}), f32[32,4,128]{2,1,0:T(4,128)S(1)}, u32[]{:S(2)}, u32[]{:S(2)}) %all-to-all-start.2) | async-done | bytes 65568 | tf_op jit(solution)/shard_map/all_to_all | solution.py:84
  79.9 10.2 %all_to_all.104 = f32[16,32,128]{2,1,0:T(8,128)S(1)} all-to-all(f32[16,32,128]{2,1,0:T(8,128)S(1)} %broadcast_in_dim.26), channel_id=1, replica_groups=mesh['row'=32,'band'=16] {'band'}, dimensions={0} | all-to-all | bytes 524288 | tf_op jit(solution)/shard_map/all_to_all | solution.py:19
  91.4 4.9 %collective-permute-start.4 = (bf16[16,128]{1,0:T(8,128)(2,1)S(1)}, bf16[16,128]{1,0:T(8,128)(2,1)S(1)}, u32[]{:S(2)}, u32[]{:S(2)}) collective-permute-start(bf16[16,128]{1,0:T(8,128)(2,1)S(1)} %slice.296), channel_id=1, source_target_pairs={{16,0},{32,16},{48,32},{64,48},{80,64},{96,80},{112,96},{128,112},... | collective-permute-start | bytes 12296 | tf_op jit(solution)/shard_map/ppermute | solution.py:13
  97.7 3.6 %all-to-all-start.4 = ((f32[32,4,128]{2,1,0:T(4,128)}), f32[32,4,128]{2,1,0:T(4,128)S(1)}, u32[]{:S(2)}, u32[]{:S(2)}) async-start(f32[32,4,128]{2,1,0:T(4,128)} %pad_maximum_fusion.1), calls=%async_computation.4 | async-start | bytes 131072 | tf_op jit(solution)/shard_map/all_to_all | solution.py:84
  105.9 8.0 %all-to-all-done.4 = f32[32,4,128]{2,1,0:T(4,128)S(1)} async-done(((f32[32,4,128]{2,1,0:T(4,128)}), f32[32,4,128]{2,1,0:T(4,128)S(1)}, u32[]{:S(2)}, u32[]{:S(2)}) %all-to-all-start.4) | async-done | bytes 65568 | tf_op jit(solution)/shard_map/all_to_all | solution.py:84
  115.9 10.4 %all_to_all.105 = f32[16,32,128]{2,1,0:T(8,128)S(1)} all-to-all(f32[16,32,128]{2,1,0:T(8,128)S(1)} %broadcast_in_dim.27), channel_id=1, replica_groups=mesh['row'=32,'band'=16] {'band'}, dimensions={0} | all-to-all | bytes 524288 | tf_op jit(solution)/shard_map/all_to_all | solution.py:19
  126.8 17.3 %all_to_all.100 = f32[32,1,4]{2,1,0:T(1,128)S(1)} all-to-all(f32[32,1,4]{2,1,0:T(1,128)S(1)} %broadcast_in_dim.28), channel_id=1, replica_groups=mesh['row'=32,'band'=16] {'row'}, dimensions={0} | all-to-all | bytes 1024 | tf_op jit(solution)/shard_map/all_to_all | solution.py:25
  150.5 4.1 %all-to-all-start.7 = ((f32[32,4,128]{2,1,0:T(4,128)}), f32[32,4,128]{2,1,0:T(4,128)S(1)}, u32[]{:S(2)}, u32[]{:S(2)}) async-start(f32[32,4,128]{2,1,0:T(4,128)} %pad_maximum_fusion.4), calls=%async_computation.7 | async-start | bytes 131072 | tf_op jit(solution)/shard_map/all_to_all | solution.py:84
  159.5 8.1 %all-to-all-done.7 = f32[32,4,128]{2,1,0:T(4,128)S(1)} async-done(((f32[32,4,128]{2,1,0:T(4,128)}), f32[32,4,128]{2,1,0:T(4,128)S(1)}, u32[]{:S(2)}, u32[]{:S(2)}) %all-to-all-start.7) | async-done | bytes 65568 | tf_op jit(solution)/shard_map/all_to_all | solution.py:84
  169.6 10.2 %all_to_all.106 = f32[16,32,128]{2,1,0:T(8,128)S(1)} all-to-all(f32[16,32,128]{2,1,0:T(8,128)S(1)} %broadcast_in_dim.29), channel_id=1, replica_groups=mesh['row'=32,'band'=16] {'band'}, dimensions={0} | all-to-all | bytes 524288 | tf_op jit(solution)/shard_map/all_to_all | solution.py:19
  181.2 17.5 %all_to_all.101 = f32[32,1,1]{2,1,0:T(1,128)S(1)} all-to-all(f32[32,1,1]{2,1,0:T(1,128)S(1)} %broadcast_in_dim.30), channel_id=1, replica_groups=mesh['row'=32,'band'=16] {'row'}, dimensions={0} | all-to-all | bytes 256 | tf_op jit(solution)/shard_map/all_to_all | solution.py:25
  204.7 4.1 %all-to-all-start.10 = ((f32[32,4,128]{2,1,0:T(4,128)}), f32[32,4,128]{2,1,0:T(4,128)S(1)}, u32[]{:S(2)}, u32[]{:S(2)}) async-start(f32[32,4,128]{2,1,0:T(4,128)} %pad_maximum_fusion.5), calls=%async_computation.10 | async-start | bytes 131072 | tf_op jit(solution)/shard_map/all_to_all | solution.py:84
  213.8 8.1 %all-to-all-done.10 = f32[32,4,128]{2,1,0:T(4,128)S(1)} async-done(((f32[32,4,128]{2,1,0:T(4,128)}), f32[32,4,128]{2,1,0:T(4,128)S(1)}, u32[]{:S(2)}, u32[]{:S(2)}) %all-to-all-start.10) | async-done | bytes 65568 | tf_op jit(solution)/shard_map/all_to_all | solution.py:84
  223.8 10.2 %all_to_all.107 = f32[16,32,128]{2,1,0:T(8,128)S(1)} all-to-all(f32[16,32,128]{2,1,0:T(8,128)S(1)} %broadcast_in_dim.31), channel_id=1, replica_groups=mesh['row'=32,'band'=16] {'band'}, dimensions={0} | all-to-all | bytes 524288 | tf_op jit(solution)/shard_map/all_to_all | solution.py:19
  235.3 4.9 %collective-permute-start.10 = (bf16[16,128]{1,0:T(8,128)(2,1)S(1)}, bf16[16,128]{1,0:T(8,128)(2,1)S(1)}, u32[]{:S(2)}, u32[]{:S(2)}) collective-permute-start(bf16[16,128]{1,0:T(8,128)(2,1)S(1)} %slice.317), channel_id=1, source_target_pairs={{16,0},{32,16},{48,32},{64,48},{80,64},{96,80},{112,96},{128,112},... | collective-permute-start | bytes 12296 | tf_op jit(solution)/shard_map/ppermute | solution.py:13
  241.7 3.6 %all-to-all-start.12 = ((f32[32,4,128]{2,1,0:T(4,128)}), f32[32,4,128]{2,1,0:T(4,128)S(1)}, u32[]{:S(2)}, u32[]{:S(2)}) async-start(f32[32,4,128]{2,1,0:T(4,128)} %pad_maximum_fusion.6), calls=%async_computation.12 | async-start | bytes 131072 | tf_op jit(solution)/shard_map/all_to_all | solution.py:84
  249.8 8.0 %all-to-all-done.12 = f32[32,4,128]{2,1,0:T(4,128)S(1)} async-done(((f32[32,4,128]{2,1,0:T(4,128)}), f32[32,4,128]{2,1,0:T(4,128)S(1)}, u32[]{:S(2)}, u32[]{:S(2)}) %all-to-all-start.12) | async-done | bytes 65568 | tf_op jit(solution)/shard_map/all_to_all | solution.py:84
  259.8 10.4 %all_to_all.108 = f32[16,32,128]{2,1,0:T(8,128)S(1)} all-to-all(f32[16,32,128]{2,1,0:T(8,128)S(1)} %broadcast_in_dim.32), channel_id=1, replica_groups=mesh['row'=32,'band'=16] {'band'}, dimensions={0} | all-to-all | bytes 524288 | tf_op jit(solution)/shard_map/all_to_all | solution.py:19
  273.5 17.3 %all_to_all.102 = f32[32,1,4]{2,1,0:T(1,128)S(1)} all-to-all(f32[32,1,4]{2,1,0:T(1,128)S(1)} %broadcast_in_dim.33), channel_id=1, replica_groups=mesh['row'=32,'band'=16] {'row'}, dimensions={0} | all-to-all | bytes 1024 | tf_op jit(solution)/shard_map/all_to_all | solution.py:25
  296.5 4.1 %all-to-all-start.15 = ((f32[32,4,128]{2,1,0:T(4,128)}), f32[32,4,128]{2,1,0:T(4,128)S(1)}, u32[]{:S(2)}, u32[]{:S(2)}) async-start(f32[32,4,128]{2,1,0:T(4,128)} %pad_maximum_fusion.9), calls=%async_computation.15 | async-start | bytes 131072 | tf_op jit(solution)/shard_map/all_to_all | solution.py:84
  305.6 8.1 %all-to-all-done.15 = f32[32,4,128]{2,1,0:T(4,128)S(1)} async-done(((f32[32,4,128]{2,1,0:T(4,128)}), f32[32,4,128]{2,1,0:T(4,128)S(1)}, u32[]{:S(2)}, u32[]{:S(2)}) %all-to-all-start.15) | async-done | bytes 65568 | tf_op jit(solution)/shard_map/all_to_all | solution.py:84
  315.6 10.2 %all_to_all.109 = f32[16,32,128]{2,1,0:T(8,128)S(1)} all-to-all(f32[16,32,128]{2,1,0:T(8,128)S(1)} %broadcast_in_dim.34), channel_id=1, replica_groups=mesh['row'=32,'band'=16] {'band'}, dimensions={0} | all-to-all | bytes 524288 | tf_op jit(solution)/shard_map/all_to_all | solution.py:19
  327.2 17.5 %all_to_all.103 = f32[32,1,1]{2,1,0:T(1,128)S(1)} all-to-all(f32[32,1,1]{2,1,0:T(1,128)S(1)} %broadcast_in_dim.35), channel_id=1, replica_groups=mesh['row'=32,'band'=16] {'row'}, dimensions={0} | all-to-all | bytes 256 | tf_op jit(solution)/shard_map/all_to_all | solution.py:25
  (287 shorter events, 78.4 us)
Async XLA Ops:
  0.7 28.4 %collective-permute-start = (bf16[16,128]{1,0:T(8,128)(2,1)S(1)}, bf16[16,128]{1,0:T(8,128)(2,1)S(1)}, u32[]{:S(2)}, u32[]{:S(2)}) collective-permute-start(bf16[16,128]{1,0:T(8,128)(2,1)S(1)} %slice.200), channel_id=1, source_target_pairs={{16,0},{32,16},{48,32},{64,48},{80,64},{96,80},{112,96},{128,112},... | collective-permute-start | bytes 12296 | tf_op jit(solution)/shard_map/ppermute | solution.py:13
  14.5 23.0 %all-to-all-start = ((f32[32,3,128]{2,1,0:T(4,128)}), f32[32,3,128]{2,1,0:T(4,128)S(1)}, u32[]{:S(2)}, u32[]{:S(2)}) async-start(f32[32,3,128]{2,1,0:T(4,128)} %select_maximum_fusion), calls=%async_computation | async-start | bytes 131072 | tf_op jit(solution)/shard_map/all_to_all | solution.py:76
  25.3 12.8 %collective-permute-start.1 = (f32[16,128]{1,0:T(8,128)S(1)}, f32[16,128]{1,0:T(8,128)S(1)}, u32[]{:S(2)}, u32[]{:S(2)}) collective-permute-start(f32[16,128]{1,0:T(8,128)S(1)} %slice.287), channel_id=1, source_target_pairs={{0,16},{16,32},{32,48},{48,64},{64,80},{80,96},{96,112},{112,128},... | collective-permute-start | bytes 24584 | tf_op jit(solution)/shard_map/ppermute | solution.py:13
  38.8 14.3 %all-to-all-start.1 = ((f32[16,32,128]{2,1,0:T(8,128)}), f32[16,32,128]{2,1,0:T(8,128)S(1)}, u32[]{:S(2)}, u32[]{:S(2)}) async-start(f32[16,32,128]{2,1,0:T(8,128)} %broadcast_in_dim.25), calls=%async_computation.1 | async-start | bytes 524288 | tf_op jit(solution)/shard_map/all_to_all | solution.py:19
  53.8 15.3 %collective-permute-start.2 = (bf16[16,128]{1,0:T(8,128)(2,1)S(1)}, bf16[16,128]{1,0:T(8,128)(2,1)S(1)}, u32[]{:S(2)}, u32[]{:S(2)}) collective-permute-start(bf16[16,128]{1,0:T(8,128)(2,1)S(1)} %slice.289), channel_id=1, source_target_pairs={{16,0},{32,16},{48,32},{64,48},{80,64},{96,80},{112,96},{128,112},... | collective-permute-start | bytes 12296 | tf_op jit(solution)/shard_map/ppermute | solution.py:13
  60.8 17.1 %all-to-all-start.2 = ((f32[32,4,128]{2,1,0:T(4,128)}), f32[32,4,128]{2,1,0:T(4,128)S(1)}, u32[]{:S(2)}, u32[]{:S(2)}) async-start(f32[32,4,128]{2,1,0:T(4,128)} %pad_maximum_fusion), calls=%async_computation.2 | async-start | bytes 131072 | tf_op jit(solution)/shard_map/all_to_all | solution.py:84
  65.6 14.2 %collective-permute-start.3 = (f32[16,128]{1,0:T(8,128)S(1)}, f32[16,128]{1,0:T(8,128)S(1)}, u32[]{:S(2)}, u32[]{:S(2)}) collective-permute-start(f32[16,128]{1,0:T(8,128)S(1)} %slice.294), channel_id=1, source_target_pairs={{0,16},{16,32},{32,48},{48,64},{64,80},{80,96},{96,112},{112,128},... | collective-permute-start | bytes 24584 | tf_op jit(solution)/shard_map/ppermute | solution.py:13
  90.1 36.2 %copy-start.2 = (f32[32,128]{1,0:T(8,128)}, f32[32,128]{1,0:T(8,128)S(1)}, u32[]{:S(2)}) copy-start(f32[32,128]{1,0:T(8,128)S(1)} %get-tuple-element.51) | copy-start | bytes 49156
  91.4 13.8 %collective-permute-start.4 = (bf16[16,128]{1,0:T(8,128)(2,1)S(1)}, bf16[16,128]{1,0:T(8,128)(2,1)S(1)}, u32[]{:S(2)}, u32[]{:S(2)}) collective-permute-start(bf16[16,128]{1,0:T(8,128)(2,1)S(1)} %slice.296), channel_id=1, source_target_pairs={{16,0},{32,16},{48,32},{64,48},{80,64},{96,80},{112,96},{128,112},... | collective-permute-start | bytes 12296 | tf_op jit(solution)/shard_map/ppermute | solution.py:13
  97.7 16.2 %all-to-all-start.4 = ((f32[32,4,128]{2,1,0:T(4,128)}), f32[32,4,128]{2,1,0:T(4,128)S(1)}, u32[]{:S(2)}, u32[]{:S(2)}) async-start(f32[32,4,128]{2,1,0:T(4,128)} %pad_maximum_fusion.1), calls=%async_computation.4 | async-start | bytes 131072 | tf_op jit(solution)/shard_map/all_to_all | solution.py:84
  102.0 13.8 %collective-permute-start.5 = (f32[16,128]{1,0:T(8,128)S(1)}, f32[16,128]{1,0:T(8,128)S(1)}, u32[]{:S(2)}, u32[]{:S(2)}) collective-permute-start(f32[16,128]{1,0:T(8,128)S(1)} %slice.301), channel_id=1, source_target_pairs={{0,16},{16,32},{32,48},{48,64},{64,80},{80,96},{96,112},{112,128},... | collective-permute-start | bytes 24584 | tf_op jit(solution)/shard_map/ppermute | solution.py:13
  126.3 18.6 %copy-start.3 = (f32[1,4096]{1,0:T(1,128)}, f32[1,4096]{1,0:T(1,128)S(1)}, u32[]{:S(2)}) copy-start(f32[1,4096]{1,0:T(1,128)S(1)} %get-tuple-element.29) | copy-start | bytes 49156
  126.3 18.6 %copy-start.4 = (f32[1,4096]{1,0:T(1,128)}, f32[1,4096]{1,0:T(1,128)S(1)}, u32[]{:S(2)}) copy-start(f32[1,4096]{1,0:T(1,128)S(1)} %get-tuple-element.30) | copy-start | bytes 49156
  126.4 18.6 %copy-start.5 = (f32[1,4096]{1,0:T(1,128)}, f32[1,4096]{1,0:T(1,128)S(1)}, u32[]{:S(2)}) copy-start(f32[1,4096]{1,0:T(1,128)S(1)} %get-tuple-element.31) | copy-start | bytes 49156
  144.9 54.2 %copy-start.6 = (f32[128]{0:T(128)}, f32[128]{0:T(128)S(1)}, u32[]{:S(2)}) copy-start(f32[128]{0:T(128)S(1)} %get-tuple-element.25) | copy-start | bytes 1540
  144.9 54.2 %copy-start.8 = (f32[1,128]{1,0:T(1,128)}, f32[1,128]{1,0:T(1,128)S(1)}, u32[]{:S(2)}) copy-start(f32[1,128]{1,0:T(1,128)S(1)} %get-tuple-element.27) | copy-start | bytes 1540
  146.3 12.6 %collective-permute-start.6 = (bf16[16,128]{1,0:T(8,128)(2,1)S(1)}, bf16[16,128]{1,0:T(8,128)(2,1)S(1)}, u32[]{:S(2)}, u32[]{:S(2)}) collective-permute-start(bf16[16,128]{1,0:T(8,128)(2,1)S(1)} %slice.303), channel_id=1, source_target_pairs={{16,0},{32,16},{48,32},{64,48},{80,64},{96,80},{112,96},{128,112},... | collective-permute-start | bytes 12296 | tf_op jit(solution)/shard_map/ppermute | solution.py:13
  150.5 17.1 %all-to-all-start.7 = ((f32[32,4,128]{2,1,0:T(4,128)}), f32[32,4,128]{2,1,0:T(4,128)S(1)}, u32[]{:S(2)}, u32[]{:S(2)}) async-start(f32[32,4,128]{2,1,0:T(4,128)} %pad_maximum_fusion.4), calls=%async_computation.7 | async-start | bytes 131072 | tf_op jit(solution)/shard_map/all_to_all | solution.py:84
  155.3 14.2 %collective-permute-start.7 = (f32[16,128]{1,0:T(8,128)S(1)}, f32[16,128]{1,0:T(8,128)S(1)}, u32[]{:S(2)}, u32[]{:S(2)}) collective-permute-start(f32[16,128]{1,0:T(8,128)S(1)} %slice.308), channel_id=1, source_target_pairs={{0,16},{16,32},{32,48},{48,64},{64,80},{80,96},{96,112},{112,128},... | collective-permute-start | bytes 24584 | tf_op jit(solution)/shard_map/ppermute | solution.py:13
  159.5 39.5 %copy-start.19 = (f32[1,128]{1,0:T(1,128)S(1)}, f32[1,128]{1,0:T(1,128)}, u32[]{:S(2)}) copy-start(f32[1,128]{1,0:T(1,128)} %get-tuple-element.26) | copy-start | bytes 1540
  200.5 12.6 %collective-permute-start.8 = (bf16[16,128]{1,0:T(8,128)(2,1)S(1)}, bf16[16,128]{1,0:T(8,128)(2,1)S(1)}, u32[]{:S(2)}, u32[]{:S(2)}) collective-permute-start(bf16[16,128]{1,0:T(8,128)(2,1)S(1)} %slice.310), channel_id=1, source_target_pairs={{16,0},{32,16},{48,32},{64,48},{80,64},{96,80},{112,96},{128,112},... | collective-permute-start | bytes 12296 | tf_op jit(solution)/shard_map/ppermute | solution.py:13
  204.7 17.1 %all-to-all-start.10 = ((f32[32,4,128]{2,1,0:T(4,128)}), f32[32,4,128]{2,1,0:T(4,128)S(1)}, u32[]{:S(2)}, u32[]{:S(2)}) async-start(f32[32,4,128]{2,1,0:T(4,128)} %pad_maximum_fusion.5), calls=%async_computation.10 | async-start | bytes 131072 | tf_op jit(solution)/shard_map/all_to_all | solution.py:84
  209.5 14.2 %collective-permute-start.9 = (f32[16,128]{1,0:T(8,128)S(1)}, f32[16,128]{1,0:T(8,128)S(1)}, u32[]{:S(2)}, u32[]{:S(2)}) collective-permute-start(f32[16,128]{1,0:T(8,128)S(1)} %slice.315), channel_id=1, source_target_pairs={{0,16},{16,32},{32,48},{48,64},{64,80},{80,96},{96,112},{112,128},... | collective-permute-start | bytes 24584 | tf_op jit(solution)/shard_map/ppermute | solution.py:13
  235.3 13.8 %collective-permute-start.10 = (bf16[16,128]{1,0:T(8,128)(2,1)S(1)}, bf16[16,128]{1,0:T(8,128)(2,1)S(1)}, u32[]{:S(2)}, u32[]{:S(2)}) collective-permute-start(bf16[16,128]{1,0:T(8,128)(2,1)S(1)} %slice.317), channel_id=1, source_target_pairs={{16,0},{32,16},{48,32},{64,48},{80,64},{96,80},{112,96},{128,112},... | collective-permute-start | bytes 12296 | tf_op jit(solution)/shard_map/ppermute | solution.py:13
  241.7 16.2 %all-to-all-start.12 = ((f32[32,4,128]{2,1,0:T(4,128)}), f32[32,4,128]{2,1,0:T(4,128)S(1)}, u32[]{:S(2)}, u32[]{:S(2)}) async-start(f32[32,4,128]{2,1,0:T(4,128)} %pad_maximum_fusion.6), calls=%async_computation.12 | async-start | bytes 131072 | tf_op jit(solution)/shard_map/all_to_all | solution.py:84
  246.0 13.8 %collective-permute-start.11 = (f32[16,128]{1,0:T(8,128)S(1)}, f32[16,128]{1,0:T(8,128)S(1)}, u32[]{:S(2)}, u32[]{:S(2)}) collective-permute-start(f32[16,128]{1,0:T(8,128)S(1)} %slice.322), channel_id=1, source_target_pairs={{0,16},{16,32},{32,48},{48,64},{64,80},{80,96},{96,112},{112,128},... | collective-permute-start | bytes 24584 | tf_op jit(solution)/shard_map/ppermute | solution.py:13
  292.3 12.6 %collective-permute-start.12 = (bf16[16,128]{1,0:T(8,128)(2,1)S(1)}, bf16[16,128]{1,0:T(8,128)(2,1)S(1)}, u32[]{:S(2)}, u32[]{:S(2)}) collective-permute-start(bf16[16,128]{1,0:T(8,128)(2,1)S(1)} %slice.324), channel_id=1, source_target_pairs={{16,0},{32,16},{48,32},{64,48},{80,64},{96,80},{112,96},{128,112},... | collective-permute-start | bytes 12296 | tf_op jit(solution)/shard_map/ppermute | solution.py:13
  296.5 17.1 %all-to-all-start.15 = ((f32[32,4,128]{2,1,0:T(4,128)}), f32[32,4,128]{2,1,0:T(4,128)S(1)}, u32[]{:S(2)}, u32[]{:S(2)}) async-start(f32[32,4,128]{2,1,0:T(4,128)} %pad_maximum_fusion.9), calls=%async_computation.15 | async-start | bytes 131072 | tf_op jit(solution)/shard_map/all_to_all | solution.py:84
  301.3 14.2 %collective-permute-start.13 = (f32[16,128]{1,0:T(8,128)S(1)}, f32[16,128]{1,0:T(8,128)S(1)}, u32[]{:S(2)}, u32[]{:S(2)}) collective-permute-start(f32[16,128]{1,0:T(8,128)S(1)} %slice.329), channel_id=1, source_target_pairs={{0,16},{16,32},{32,48},{48,64},{64,80},{80,96},{96,112},{112,128},... | collective-permute-start | bytes 24584 | tf_op jit(solution)/shard_map/ppermute | solution.py:13
  305.5 20.3 %copy-start.7 = (f32[128]{0:T(128)S(1)}, f32[128]{0:T(128)}, u32[]{:S(2)}) copy-start(f32[128]{0:T(128)} %copy-done.6) | copy-start | bytes 1540
  305.6 20.3 %copy-start.9 = (f32[1,128]{1,0:T(1,128)S(1)}, f32[1,128]{1,0:T(1,128)}, u32[]{:S(2)}) copy-start(f32[1,128]{1,0:T(1,128)} %copy-done.8) | copy-start | bytes 1540
  305.6 20.3 %copy-start.11 = (f32[128]{0:T(128)S(1)}, f32[128]{0:T(128)}, u32[]{:S(2)}) copy-start(f32[128]{0:T(128)} %copy-done.10) | copy-start | bytes 1540
  (15 other events, 189.5 us)

commit v7 on v6

--- a/solution.py
+++ b/solution.py
@@ -45,6 +45,11 @@
     upper_mask = (offset > 0).astype(jnp.float32)
     targets = jnp.arange(rows_dev)[None, :]
     pick_in = (local_row_values.reshape(-1)[:, None] == targets).astype(jnp.float32)
+    pick_rows = pick_in.astype(jnp.bfloat16)
+
+    def picked(selection, vector):
+        product = jnp.dot(selection, vector, preferred_element_type=jnp.float32)
+        return product.reshape(row_count, slots, block_size)
 
     def multiply(vector, wanted=None):
         narrow_band_part = vector.astype(jnp.bfloat16)
@@ -65,7 +70,7 @@
             jnp.einsum(
                 "nquo,nqu->nqo",
                 distant_local_part,
-                narrow_band_part[local_row_values],
+                picked(pick_rows, narrow_band_part).astype(jnp.bfloat16),
                 preferred_element_type=jnp.float32,
             )
             * live_mask
@@ -80,7 +85,8 @@
             gathered_values = jnp.ones((row_count, slots, block_size), jnp.bfloat16)
             returned = exchanged[:, 1:]
         else:
-            outgoing = narrow_band_part[wanted].astype(jnp.float32)
+            pick_out = (wanted.reshape(-1)[:, None] == targets).astype(jnp.bfloat16)
+            outgoing = picked(pick_out, narrow_band_part)
             exchanged = lax.all_to_all(
                 jnp.concatenate([outgoing, far_backward], 1), "row", split_axis=0, concat_axis=0, tiled=True
             )

time: 347 us -> 341 us (0.983)
  blocking collectives: 131 us -> 145 us
  local copies, waits for them, and re-layouts: 15.1 us -> 5.49 us
  waiting for transfers between devices: 63.1 us -> 56 us
  starting transfers between devices: 96.3 us -> 89.7 us
  matrix products: 25 us -> 29.5 us
    all_to_all x6 -> x7, blocking collectives: 61.5 us -> 75.5 us  [all_sum(): return jnp.sum(lax.all_to_all(copies, axis, 0, 0, tiled=True), 0)]
    gather x13 -> x0, local copies, waits for them, and re-layouts: 8.29 us -> none  [the longest x7 4.47 us: multiply(): narrow_band_part[local_row_values]]
    all_to_all x1 -> x0, waiting for transfers between devices: 7.26 us -> none  [all_sum(): return jnp.sum(lax.all_to_all(copies, axis, 0, 0, tiled=True), 0)]
    all_to_all x1 -> x0, starting transfers between devices: 6.75 us -> none  [all_sum(): return jnp.sum(lax.all_to_all(copies, axis, 0, 0, tiled=True), 0)]
    dot_general x7 -> x20, matrix products: 4.55 us -> 8.98 us  [the longest x7 4.57 us: multiply(): jnp.einsum('nquo,nqu->nqo', distant_local_part, picked(pick_rows, narrow_...]
  transfers between devices with their start and end apart: 22 -> 21, of which waited for: 8 -> 7; matrix products, arithmetic and copies ran while one was open for 10% -> 10% of each run, Pallas kernels for 0% -> 0%
where the time goes in v7:
time: 341 us; the launch traced here: 339 us
  blocking collectives  145 us (43%)
  starting transfers between devices  89.7 us (26%)
  waiting for transfers between devices  56 us (16%)
  matrix products  29.5 us (9%)
  other arithmetic  11.6 us (3%)
  local copies, waits for them, and re-layouts  5.49 us (2%)
    all_to_all x7, blocking collectives, all_sum(): return jnp.sum(lax.all_to_all(copies, axis, 0, 0, tiled=True), 0)  75.5 us
    all_to_all x4, blocking collectives, lane_totals(): received = lax.all_to_all(copies, axis, 0, 0, tiled=True)  69.5 us
    ppermute x14, starting transfers between devices, shifted(): lax.ppermute(value, axis, [(source, source + steps) for source in range(l...  56.1 us
    all_to_all x6, waiting for transfers between devices, multiply(): lax.all_to_all(jnp.concatenate([outgoing, far_backward], 1), 'row', split...  48.5 us
    all_to_all x6, starting transfers between devices, multiply(): lax.all_to_all(jnp.concatenate([outgoing, far_backward], 1), 'row', split...  23.6 us
    all_to_all x1, starting transfers between devices, multiply(): lax.all_to_all(jnp.concatenate([column_row, far_backward], 1), 'row', spl...  10 us
    dot_general x7, matrix products, multiply(): jnp.einsum('oqht,oqt->oqh', distant_local_part, gathered_values, preferre...  8.23 us
    all_to_all x1, waiting for transfers between devices, multiply(): lax.all_to_all(jnp.concatenate([column_row, far_backward], 1), 'row', spl...  7.55 us
  transfers between devices with their start and end apart: 21, of which 7 were waited for; matrix products, arithmetic and copies ran while one was open for 10% of the time, Pallas kernels for 0%

profile of v7, /device:TPU:1, one launch (start us, length us, event | category | flops | bytes accessed | tf_op | source)
XLA Modules:
  0.0 339.4 jit_solution(4481550389128388769)
XLA Ops:
  0.7 8.9 %collective-permute-start = (bf16[16,128]{1,0:T(8,128)(2,1)S(1)}, bf16[16,128]{1,0:T(8,128)(2,1)S(1)}, u32[]{:S(2)}, u32[]{:S(2)}) collective-permute-start(bf16[16,128]{1,0:T(8,128)(2,1)S(1)} %slice.200), channel_id=1, source_target_pairs={{16,0},{32,16},{48,32},{64,48},{80,64},{96,80},{112,96},{128,112},... | collective-permute-start | bytes 12296 | tf_op jit(solution)/shard_map/ppermute | solution.py:13
  13.9 10.0 %all-to-all-start = ((f32[32,3,128]{2,1,0:T(4,128)}), f32[32,3,128]{2,1,0:T(4,128)S(1)}, u32[]{:S(2)}, u32[]{:S(2)}) async-start(f32[32,3,128]{2,1,0:T(4,128)} %select_maximum_fusion), calls=%async_computation | async-start | bytes 131072 | tf_op jit(solution)/shard_map/all_to_all | solution.py:81
  24.6 3.5 %collective-permute-start.1 = (f32[16,128]{1,0:T(8,128)S(1)}, f32[16,128]{1,0:T(8,128)S(1)}, u32[]{:S(2)}, u32[]{:S(2)}) collective-permute-start(f32[16,128]{1,0:T(8,128)S(1)} %slice.261), channel_id=1, source_target_pairs={{0,16},{16,32},{32,48},{48,64},{64,80},{80,96},{96,112},{112,128},... | collective-permute-start | bytes 24584 | tf_op jit(solution)/shard_map/ppermute | solution.py:13
  29.4 7.5 %all-to-all-done = f32[32,3,128]{2,1,0:T(4,128)S(1)} async-done(((f32[32,3,128]{2,1,0:T(4,128)}), f32[32,3,128]{2,1,0:T(4,128)S(1)}, u32[]{:S(2)}, u32[]{:S(2)}) %all-to-all-start) | async-done | bytes 49184 | tf_op jit(solution)/shard_map/all_to_all | solution.py:81
  37.5 14.1 %all_to_all.104 = f32[16,32,128]{2,1,0:T(8,128)S(1)} all-to-all(f32[16,32,128]{2,1,0:T(8,128)S(1)} %broadcast_in_dim.25), channel_id=1, replica_groups=mesh['row'=32,'band'=16] {'band'}, dimensions={0} | all-to-all | bytes 524288 | tf_op jit(solution)/shard_map/all_to_all | solution.py:19
  52.0 4.9 %collective-permute-start.2 = (bf16[16,128]{1,0:T(8,128)(2,1)S(1)}, bf16[16,128]{1,0:T(8,128)(2,1)S(1)}, u32[]{:S(2)}, u32[]{:S(2)}) collective-permute-start(bf16[16,128]{1,0:T(8,128)(2,1)S(1)} %slice.263), channel_id=1, source_target_pairs={{16,0},{32,16},{48,32},{64,48},{80,64},{96,80},{112,96},{128,112},... | collective-permute-start | bytes 12296 | tf_op jit(solution)/shard_map/ppermute | solution.py:13
  58.4 4.0 %all-to-all-start.2 = ((f32[32,4,128]{2,1,0:T(4,128)}), f32[32,4,128]{2,1,0:T(4,128)S(1)}, u32[]{:S(2)}, u32[]{:S(2)}) async-start(f32[32,4,128]{2,1,0:T(4,128)} %pad_maximum_fusion), calls=%async_computation.2 | async-start | bytes 131072 | tf_op jit(solution)/shard_map/all_to_all | solution.py:90
  63.1 3.5 %collective-permute-start.3 = (f32[16,128]{1,0:T(8,128)S(1)}, f32[16,128]{1,0:T(8,128)S(1)}, u32[]{:S(2)}, u32[]{:S(2)}) collective-permute-start(f32[16,128]{1,0:T(8,128)S(1)} %slice.268), channel_id=1, source_target_pairs={{0,16},{16,32},{32,48},{48,64},{64,80},{80,96},{96,112},{112,128},... | collective-permute-start | bytes 24584 | tf_op jit(solution)/shard_map/ppermute | solution.py:13
  67.4 8.1 %all-to-all-done.2 = f32[32,4,128]{2,1,0:T(4,128)S(1)} async-done(((f32[32,4,128]{2,1,0:T(4,128)}), f32[32,4,128]{2,1,0:T(4,128)S(1)}, u32[]{:S(2)}, u32[]{:S(2)}) %all-to-all-start.2) | async-done | bytes 65568 | tf_op jit(solution)/shard_map/all_to_all | solution.py:90
  77.4 10.2 %all_to_all.105 = f32[16,32,128]{2,1,0:T(8,128)S(1)} all-to-all(f32[16,32,128]{2,1,0:T(8,128)S(1)} %broadcast_in_dim.26), channel_id=1, replica_groups=mesh['row'=32,'band'=16] {'band'}, dimensions={0} | all-to-all | bytes 524288 | tf_op jit(solution)/shard_map/all_to_all | solution.py:19
  88.0 4.9 %collective-permute-start.4 = (bf16[16,128]{1,0:T(8,128)(2,1)S(1)}, bf16[16,128]{1,0:T(8,128)(2,1)S(1)}, u32[]{:S(2)}, u32[]{:S(2)}) collective-permute-start(bf16[16,128]{1,0:T(8,128)(2,1)S(1)} %slice.270), channel_id=1, source_target_pairs={{16,0},{32,16},{48,32},{64,48},{80,64},{96,80},{112,96},{128,112},... | collective-permute-start | bytes 12296 | tf_op jit(solution)/shard_map/ppermute | solution.py:13
  94.4 3.6 %all-to-all-start.4 = ((f32[32,4,128]{2,1,0:T(4,128)}), f32[32,4,128]{2,1,0:T(4,128)S(1)}, u32[]{:S(2)}, u32[]{:S(2)}) async-start(f32[32,4,128]{2,1,0:T(4,128)} %pad_maximum_fusion.1), calls=%async_computation.4 | async-start | bytes 131072 | tf_op jit(solution)/shard_map/all_to_all | solution.py:90
  102.5 8.2 %all-to-all-done.4 = f32[32,4,128]{2,1,0:T(4,128)S(1)} async-done(((f32[32,4,128]{2,1,0:T(4,128)}), f32[32,4,128]{2,1,0:T(4,128)S(1)}, u32[]{:S(2)}, u32[]{:S(2)}) %all-to-all-start.4) | async-done | bytes 65568 | tf_op jit(solution)/shard_map/all_to_all | solution.py:90
  112.7 10.3 %all_to_all.106 = f32[16,32,128]{2,1,0:T(8,128)S(1)} all-to-all(f32[16,32,128]{2,1,0:T(8,128)S(1)} %broadcast_in_dim.27), channel_id=1, replica_groups=mesh['row'=32,'band'=16] {'band'}, dimensions={0} | all-to-all | bytes 524288 | tf_op jit(solution)/shard_map/all_to_all | solution.py:19
  123.5 17.3 %all_to_all.100 = f32[32,1,4]{2,1,0:T(1,128)S(1)} all-to-all(f32[32,1,4]{2,1,0:T(1,128)S(1)} %broadcast_in_dim.28), channel_id=1, replica_groups=mesh['row'=32,'band'=16] {'row'}, dimensions={0} | all-to-all | bytes 1024 | tf_op jit(solution)/shard_map/all_to_all | solution.py:25
  145.7 4.1 %all-to-all-start.7 = ((f32[32,4,128]{2,1,0:T(4,128)}), f32[32,4,128]{2,1,0:T(4,128)S(1)}, u32[]{:S(2)}, u32[]{:S(2)}) async-start(f32[32,4,128]{2,1,0:T(4,128)} %pad_maximum_fusion.4), calls=%async_computation.7 | async-start | bytes 131072 | tf_op jit(solution)/shard_map/all_to_all | solution.py:90
  150.4 3.7 %collective-permute-start.7 = (f32[16,128]{1,0:T(8,128)S(1)}, f32[16,128]{1,0:T(8,128)S(1)}, u32[]{:S(2)}, u32[]{:S(2)}) collective-permute-start(f32[16,128]{1,0:T(8,128)S(1)} %slice.282), channel_id=1, source_target_pairs={{0,16},{16,32},{32,48},{48,64},{64,80},{80,96},{96,112},{112,128},... | collective-permute-start | bytes 24584 | tf_op jit(solution)/shard_map/ppermute | solution.py:13
  154.9 7.9 %all-to-all-done.7 = f32[32,4,128]{2,1,0:T(4,128)S(1)} async-done(((f32[32,4,128]{2,1,0:T(4,128)}), f32[32,4,128]{2,1,0:T(4,128)S(1)}, u32[]{:S(2)}, u32[]{:S(2)}) %all-to-all-start.7) | async-done | bytes 65568 | tf_op jit(solution)/shard_map/all_to_all | solution.py:90
  164.8 10.2 %all_to_all.107 = f32[16,32,128]{2,1,0:T(8,128)S(1)} all-to-all(f32[16,32,128]{2,1,0:T(8,128)S(1)} %broadcast_in_dim.29), channel_id=1, replica_groups=mesh['row'=32,'band'=16] {'band'}, dimensions={0} | all-to-all | bytes 524288 | tf_op jit(solution)/shard_map/all_to_all | solution.py:19
  176.2 17.5 %all_to_all.101 = f32[32,1,1]{2,1,0:T(1,128)S(1)} all-to-all(f32[32,1,1]{2,1,0:T(1,128)S(1)} %broadcast_in_dim.30), channel_id=1, replica_groups=mesh['row'=32,'band'=16] {'row'}, dimensions={0} | all-to-all | bytes 256 | tf_op jit(solution)/shard_map/all_to_all | solution.py:25
  198.8 4.1 %all-to-all-start.10 = ((f32[32,4,128]{2,1,0:T(4,128)}), f32[32,4,128]{2,1,0:T(4,128)S(1)}, u32[]{:S(2)}, u32[]{:S(2)}) async-start(f32[32,4,128]{2,1,0:T(4,128)} %pad_maximum_fusion.5), calls=%async_computation.10 | async-start | bytes 131072 | tf_op jit(solution)/shard_map/all_to_all | solution.py:90
  207.9 8.1 %all-to-all-done.10 = f32[32,4,128]{2,1,0:T(4,128)S(1)} async-done(((f32[32,4,128]{2,1,0:T(4,128)}), f32[32,4,128]{2,1,0:T(4,128)S(1)}, u32[]{:S(2)}, u32[]{:S(2)}) %all-to-all-start.10) | async-done | bytes 65568 | tf_op jit(solution)/shard_map/all_to_all | solution.py:90
  217.9 10.2 %all_to_all.108 = f32[16,32,128]{2,1,0:T(8,128)S(1)} all-to-all(f32[16,32,128]{2,1,0:T(8,128)S(1)} %broadcast_in_dim.31), channel_id=1, replica_groups=mesh['row'=32,'band'=16] {'band'}, dimensions={0} | all-to-all | bytes 524288 | tf_op jit(solution)/shard_map/all_to_all | solution.py:19
  228.6 4.9 %collective-permute-start.10 = (bf16[16,128]{1,0:T(8,128)(2,1)S(1)}, bf16[16,128]{1,0:T(8,128)(2,1)S(1)}, u32[]{:S(2)}, u32[]{:S(2)}) collective-permute-start(bf16[16,128]{1,0:T(8,128)(2,1)S(1)} %slice.291), channel_id=1, source_target_pairs={{16,0},{32,16},{48,32},{64,48},{80,64},{96,80},{112,96},{128,112},... | collective-permute-start | bytes 12296 | tf_op jit(solution)/shard_map/ppermute | solution.py:13
  234.9 3.6 %all-to-all-start.12 = ((f32[32,4,128]{2,1,0:T(4,128)}), f32[32,4,128]{2,1,0:T(4,128)S(1)}, u32[]{:S(2)}, u32[]{:S(2)}) async-start(f32[32,4,128]{2,1,0:T(4,128)} %pad_maximum_fusion.6), calls=%async_computation.12 | async-start | bytes 131072 | tf_op jit(solution)/shard_map/all_to_all | solution.py:90
  243.1 8.2 %all-to-all-done.12 = f32[32,4,128]{2,1,0:T(4,128)S(1)} async-done(((f32[32,4,128]{2,1,0:T(4,128)}), f32[32,4,128]{2,1,0:T(4,128)S(1)}, u32[]{:S(2)}, u32[]{:S(2)}) %all-to-all-start.12) | async-done | bytes 65568 | tf_op jit(solution)/shard_map/all_to_all | solution.py:90
  253.2 10.3 %all_to_all.109 = f32[16,32,128]{2,1,0:T(8,128)S(1)} all-to-all(f32[16,32,128]{2,1,0:T(8,128)S(1)} %broadcast_in_dim.32), channel_id=1, replica_groups=mesh['row'=32,'band'=16] {'band'}, dimensions={0} | all-to-all | bytes 524288 | tf_op jit(solution)/shard_map/all_to_all | solution.py:19
  266.7 17.3 %all_to_all.102 = f32[32,1,4]{2,1,0:T(1,128)S(1)} all-to-all(f32[32,1,4]{2,1,0:T(1,128)S(1)} %broadcast_in_dim.33), channel_id=1, replica_groups=mesh['row'=32,'band'=16] {'row'}, dimensions={0} | all-to-all | bytes 1024 | tf_op jit(solution)/shard_map/all_to_all | solution.py:25
  290.1 4.1 %all-to-all-start.15 = ((f32[32,4,128]{2,1,0:T(4,128)}), f32[32,4,128]{2,1,0:T(4,128)S(1)}, u32[]{:S(2)}, u32[]{:S(2)}) async-start(f32[32,4,128]{2,1,0:T(4,128)} %pad_maximum_fusion.9), calls=%async_computation.15 | async-start | bytes 131072 | tf_op jit(solution)/shard_map/all_to_all | solution.py:90
  299.1 8.1 %all-to-all-done.15 = f32[32,4,128]{2,1,0:T(4,128)S(1)} async-done(((f32[32,4,128]{2,1,0:T(4,128)}), f32[32,4,128]{2,1,0:T(4,128)S(1)}, u32[]{:S(2)}, u32[]{:S(2)}) %all-to-all-start.15) | async-done | bytes 65568 | tf_op jit(solution)/shard_map/all_to_all | solution.py:90
  309.2 10.2 %all_to_all.110 = f32[16,32,128]{2,1,0:T(8,128)S(1)} all-to-all(f32[16,32,128]{2,1,0:T(8,128)S(1)} %broadcast_in_dim.34), channel_id=1, replica_groups=mesh['row'=32,'band'=16] {'band'}, dimensions={0} | all-to-all | bytes 524288 | tf_op jit(solution)/shard_map/all_to_all | solution.py:19
  320.8 17.5 %all_to_all.103 = f32[32,1,1]{2,1,0:T(1,128)S(1)} all-to-all(f32[32,1,1]{2,1,0:T(1,128)S(1)} %broadcast_in_dim.35), channel_id=1, replica_groups=mesh['row'=32,'band'=16] {'row'}, dimensions={0} | all-to-all | bytes 256 | tf_op jit(solution)/shard_map/all_to_all | solution.py:25
  (263 shorter events, 68.3 us)
Async XLA Ops:
  0.7 27.7 %collective-permute-start = (bf16[16,128]{1,0:T(8,128)(2,1)S(1)}, bf16[16,128]{1,0:T(8,128)(2,1)S(1)}, u32[]{:S(2)}, u32[]{:S(2)}) collective-permute-start(bf16[16,128]{1,0:T(8,128)(2,1)S(1)} %slice.200), channel_id=1, source_target_pairs={{16,0},{32,16},{48,32},{64,48},{80,64},{96,80},{112,96},{128,112},... | collective-permute-start | bytes 12296 | tf_op jit(solution)/shard_map/ppermute | solution.py:13
  13.9 23.0 %all-to-all-start = ((f32[32,3,128]{2,1,0:T(4,128)}), f32[32,3,128]{2,1,0:T(4,128)S(1)}, u32[]{:S(2)}, u32[]{:S(2)}) async-start(f32[32,3,128]{2,1,0:T(4,128)} %select_maximum_fusion), calls=%async_computation | async-start | bytes 131072 | tf_op jit(solution)/shard_map/all_to_all | solution.py:81
  24.3 214.6 %copy-start.7 = (f32[32]{0:T(128)}, f32[32]{0:T(128)S(1)}, u32[]{:S(2)}) copy-start(f32[32]{0:T(128)S(1)} %compare_select_fusion) | copy-start | bytes 388
  24.6 12.8 %collective-permute-start.1 = (f32[16,128]{1,0:T(8,128)S(1)}, f32[16,128]{1,0:T(8,128)S(1)}, u32[]{:S(2)}, u32[]{:S(2)}) collective-permute-start(f32[16,128]{1,0:T(8,128)S(1)} %slice.261), channel_id=1, source_target_pairs={{0,16},{16,32},{32,48},{48,64},{64,80},{80,96},{96,112},{112,128},... | collective-permute-start | bytes 24584 | tf_op jit(solution)/shard_map/ppermute | solution.py:13
  28.2 135.9 %copy-start.19 = (f32[32]{0:T(128)}, f32[32]{0:T(128)S(1)}, u32[]{:S(2)}) copy-start(f32[32]{0:T(128)S(1)} %compare_convert_fusion) | copy-start | bytes 388
  28.4 224.2 %copy-start.17 = (s32[64]{0:T(128)}, s32[64]{0:T(128)S(1)}, u32[]{:S(2)}) copy-start(s32[64]{0:T(128)S(1)} %eq.23) | copy-start | bytes 772
  37.1 215.8 %copy-start.5 = (s32[64]{0:T(128)}, s32[64]{0:T(128)S(1)}, u32[]{:S(2)}) copy-start(s32[64]{0:T(128)S(1)} %convert_element_type.140) | copy-start | bytes 772
  52.0 14.6 %collective-permute-start.2 = (bf16[16,128]{1,0:T(8,128)(2,1)S(1)}, bf16[16,128]{1,0:T(8,128)(2,1)S(1)}, u32[]{:S(2)}, u32[]{:S(2)}) collective-permute-start(bf16[16,128]{1,0:T(8,128)(2,1)S(1)} %slice.263), channel_id=1, source_target_pairs={{16,0},{32,16},{48,32},{64,48},{80,64},{96,80},{112,96},{128,112},... | collective-permute-start | bytes 12296 | tf_op jit(solution)/shard_map/ppermute | solution.py:13
  58.4 17.1 %all-to-all-start.2 = ((f32[32,4,128]{2,1,0:T(4,128)}), f32[32,4,128]{2,1,0:T(4,128)S(1)}, u32[]{:S(2)}, u32[]{:S(2)}) async-start(f32[32,4,128]{2,1,0:T(4,128)} %pad_maximum_fusion), calls=%async_computation.2 | async-start | bytes 131072 | tf_op jit(solution)/shard_map/all_to_all | solution.py:90
  63.1 14.2 %collective-permute-start.3 = (f32[16,128]{1,0:T(8,128)S(1)}, f32[16,128]{1,0:T(8,128)S(1)}, u32[]{:S(2)}, u32[]{:S(2)}) collective-permute-start(f32[16,128]{1,0:T(8,128)S(1)} %slice.268), channel_id=1, source_target_pairs={{0,16},{16,32},{32,48},{48,64},{64,80},{80,96},{96,112},{112,128},... | collective-permute-start | bytes 24584 | tf_op jit(solution)/shard_map/ppermute | solution.py:13
  88.0 13.8 %collective-permute-start.4 = (bf16[16,128]{1,0:T(8,128)(2,1)S(1)}, bf16[16,128]{1,0:T(8,128)(2,1)S(1)}, u32[]{:S(2)}, u32[]{:S(2)}) collective-permute-start(bf16[16,128]{1,0:T(8,128)(2,1)S(1)} %slice.270), channel_id=1, source_target_pairs={{16,0},{32,16},{48,32},{64,48},{80,64},{96,80},{112,96},{128,112},... | collective-permute-start | bytes 12296 | tf_op jit(solution)/shard_map/ppermute | solution.py:13
  94.4 16.3 %all-to-all-start.4 = ((f32[32,4,128]{2,1,0:T(4,128)}), f32[32,4,128]{2,1,0:T(4,128)S(1)}, u32[]{:S(2)}, u32[]{:S(2)}) async-start(f32[32,4,128]{2,1,0:T(4,128)} %pad_maximum_fusion.1), calls=%async_computation.4 | async-start | bytes 131072 | tf_op jit(solution)/shard_map/all_to_all | solution.py:90
  98.7 13.9 %collective-permute-start.5 = (f32[16,128]{1,0:T(8,128)S(1)}, f32[16,128]{1,0:T(8,128)S(1)}, u32[]{:S(2)}, u32[]{:S(2)}) collective-permute-start(f32[16,128]{1,0:T(8,128)S(1)} %slice.275), channel_id=1, source_target_pairs={{0,16},{16,32},{32,48},{48,64},{64,80},{80,96},{96,112},{112,128},... | collective-permute-start | bytes 24584 | tf_op jit(solution)/shard_map/ppermute | solution.py:13
  123.0 18.0 %copy-start.4 = (f32[1,4096]{1,0:T(1,128)}, f32[1,4096]{1,0:T(1,128)S(1)}, u32[]{:S(2)}) copy-start(f32[1,4096]{1,0:T(1,128)S(1)} %get-tuple-element.31) | copy-start | bytes 49156
  141.0 53.2 %copy-start.9 = (f32[128]{0:T(128)}, f32[128]{0:T(128)S(1)}, u32[]{:S(2)}) copy-start(f32[128]{0:T(128)S(1)} %get-tuple-element.25) | copy-start | bytes 1540
  141.0 53.2 %copy-start.11 = (f32[1,128]{1,0:T(1,128)}, f32[1,128]{1,0:T(1,128)S(1)}, u32[]{:S(2)}) copy-start(f32[1,128]{1,0:T(1,128)S(1)} %get-tuple-element.27) | copy-start | bytes 1540
  141.4 12.7 %collective-permute-start.6 = (bf16[16,128]{1,0:T(8,128)(2,1)S(1)}, bf16[16,128]{1,0:T(8,128)(2,1)S(1)}, u32[]{:S(2)}, u32[]{:S(2)}) collective-permute-start(bf16[16,128]{1,0:T(8,128)(2,1)S(1)} %slice.277), channel_id=1, source_target_pairs={{16,0},{32,16},{48,32},{64,48},{80,64},{96,80},{112,96},{128,112},... | collective-permute-start | bytes 12296 | tf_op jit(solution)/shard_map/ppermute | solution.py:13
  145.7 17.1 %all-to-all-start.7 = ((f32[32,4,128]{2,1,0:T(4,128)}), f32[32,4,128]{2,1,0:T(4,128)S(1)}, u32[]{:S(2)}, u32[]{:S(2)}) async-start(f32[32,4,128]{2,1,0:T(4,128)} %pad_maximum_fusion.4), calls=%async_computation.7 | async-start | bytes 131072 | tf_op jit(solution)/shard_map/all_to_all | solution.py:90
  150.4 14.3 %collective-permute-start.7 = (f32[16,128]{1,0:T(8,128)S(1)}, f32[16,128]{1,0:T(8,128)S(1)}, u32[]{:S(2)}, u32[]{:S(2)}) collective-permute-start(f32[16,128]{1,0:T(8,128)S(1)} %slice.282), channel_id=1, source_target_pairs={{0,16},{16,32},{32,48},{48,64},{64,80},{80,96},{96,112},{112,128},... | collective-permute-start | bytes 24584 | tf_op jit(solution)/shard_map/ppermute | solution.py:13
  194.6 12.6 %collective-permute-start.8 = (bf16[16,128]{1,0:T(8,128)(2,1)S(1)}, bf16[16,128]{1,0:T(8,128)(2,1)S(1)}, u32[]{:S(2)}, u32[]{:S(2)}) collective-permute-start(bf16[16,128]{1,0:T(8,128)(2,1)S(1)} %slice.284), channel_id=1, source_target_pairs={{16,0},{32,16},{48,32},{64,48},{80,64},{96,80},{112,96},{128,112},... | collective-permute-start | bytes 12296 | tf_op jit(solution)/shard_map/ppermute | solution.py:13
  198.8 17.1 %all-to-all-start.10 = ((f32[32,4,128]{2,1,0:T(4,128)}), f32[32,4,128]{2,1,0:T(4,128)S(1)}, u32[]{:S(2)}, u32[]{:S(2)}) async-start(f32[32,4,128]{2,1,0:T(4,128)} %pad_maximum_fusion.5), calls=%async_computation.10 | async-start | bytes 131072 | tf_op jit(solution)/shard_map/all_to_all | solution.py:90
  203.6 14.2 %collective-permute-start.9 = (f32[16,128]{1,0:T(8,128)S(1)}, f32[16,128]{1,0:T(8,128)S(1)}, u32[]{:S(2)}, u32[]{:S(2)}) collective-permute-start(f32[16,128]{1,0:T(8,128)S(1)} %slice.289), channel_id=1, source_target_pairs={{0,16},{16,32},{32,48},{48,64},{64,80},{80,96},{96,112},{112,128},... | collective-permute-start | bytes 24584 | tf_op jit(solution)/shard_map/ppermute | solution.py:13
  228.6 13.8 %collective-permute-start.10 = (bf16[16,128]{1,0:T(8,128)(2,1)S(1)}, bf16[16,128]{1,0:T(8,128)(2,1)S(1)}, u32[]{:S(2)}, u32[]{:S(2)}) collective-permute-start(bf16[16,128]{1,0:T(8,128)(2,1)S(1)} %slice.291), channel_id=1, source_target_pairs={{16,0},{32,16},{48,32},{64,48},{80,64},{96,80},{112,96},{128,112},... | collective-permute-start | bytes 12296 | tf_op jit(solution)/shard_map/ppermute | solution.py:13
  234.9 16.3 %all-to-all-start.12 = ((f32[32,4,128]{2,1,0:T(4,128)}), f32[32,4,128]{2,1,0:T(4,128)S(1)}, u32[]{:S(2)}, u32[]{:S(2)}) async-start(f32[32,4,128]{2,1,0:T(4,128)} %pad_maximum_fusion.6), calls=%async_computation.12 | async-start | bytes 131072 | tf_op jit(solution)/shard_map/all_to_all | solution.py:90
  239.2 13.9 %collective-permute-start.11 = (f32[16,128]{1,0:T(8,128)S(1)}, f32[16,128]{1,0:T(8,128)S(1)}, u32[]{:S(2)}, u32[]{:S(2)}) collective-permute-start(f32[16,128]{1,0:T(8,128)S(1)} %slice.296), channel_id=1, source_target_pairs={{0,16},{16,32},{32,48},{48,64},{64,80},{80,96},{96,112},{112,128},... | collective-permute-start | bytes 24584 | tf_op jit(solution)/shard_map/ppermute | solution.py:13
  266.2 28.4 %copy-start.8 = (f32[32]{0:T(128)S(1)}, f32[32]{0:T(128)}, u32[]{:S(2)}) copy-start(f32[32]{0:T(128)} %copy-done.7) | copy-start | bytes 388
  285.9 12.6 %collective-permute-start.12 = (bf16[16,128]{1,0:T(8,128)(2,1)S(1)}, bf16[16,128]{1,0:T(8,128)(2,1)S(1)}, u32[]{:S(2)}, u32[]{:S(2)}) collective-permute-start(bf16[16,128]{1,0:T(8,128)(2,1)S(1)} %slice.298), channel_id=1, source_target_pairs={{16,0},{32,16},{48,32},{64,48},{80,64},{96,80},{112,96},{128,112},... | collective-permute-start | bytes 12296 | tf_op jit(solution)/shard_map/ppermute | solution.py:13
  290.1 17.1 %all-to-all-start.15 = ((f32[32,4,128]{2,1,0:T(4,128)}), f32[32,4,128]{2,1,0:T(4,128)S(1)}, u32[]{:S(2)}, u32[]{:S(2)}) async-start(f32[32,4,128]{2,1,0:T(4,128)} %pad_maximum_fusion.9), calls=%async_computation.15 | async-start | bytes 131072 | tf_op jit(solution)/shard_map/all_to_all | solution.py:90
  294.9 14.3 %collective-permute-start.13 = (f32[16,128]{1,0:T(8,128)S(1)}, f32[16,128]{1,0:T(8,128)S(1)}, u32[]{:S(2)}, u32[]{:S(2)}) collective-permute-start(f32[16,128]{1,0:T(8,128)S(1)} %slice.303), channel_id=1, source_target_pairs={{0,16},{16,32},{32,48},{48,64},{64,80},{80,96},{96,112},{112,128},... | collective-permute-start | bytes 24584 | tf_op jit(solution)/shard_map/ppermute | solution.py:13
  299.1 20.3 %copy-start.10 = (f32[128]{0:T(128)S(1)}, f32[128]{0:T(128)}, u32[]{:S(2)}) copy-start(f32[128]{0:T(128)} %copy-done.9) | copy-start | bytes 1540
  299.1 20.3 %copy-start.12 = (f32[1,128]{1,0:T(1,128)S(1)}, f32[1,128]{1,0:T(1,128)}, u32[]{:S(2)}) copy-start(f32[1,128]{1,0:T(1,128)} %copy-done.11) | copy-start | bytes 1540
  299.1 20.3 %copy-start.14 = (f32[128]{0:T(128)S(1)}, f32[128]{0:T(128)}, u32[]{:S(2)}) copy-start(f32[128]{0:T(128)} %copy-done.13) | copy-start | bytes 1540
  (11 other events, 147.9 us)

commit v8 on v7

--- a/solution.py
+++ b/solution.py
@@ -19,9 +19,8 @@
     return jnp.sum(lax.all_to_all(copies, axis, 0, 0, tiled=True), 0)
 
 
-def lane_totals(value, axis, lanes):
+def lane_totals(copies, axis, lanes):
     count = lax.axis_size(axis)
-    copies = jnp.broadcast_to(value[None], (count,) + value.shape)
     received = lax.all_to_all(copies, axis, 0, 0, tiled=True)
     return jnp.dot(received.T, jnp.ones((count, lanes), jnp.float32), precision=lax.Precision.HIGHEST)
 
@@ -133,10 +132,10 @@
                 parts.append(residual * curved / balance)
                 parts.append(curved * curved / balance)
             stacked = jnp.stack(parts).reshape(len(parts), -1)
-            local_totals = jnp.dot(
-                stacked, jnp.ones((stacked.shape[1],), jnp.float32), precision=lax.Precision.HIGHEST
+            copies = jnp.dot(
+                jnp.ones((row_count, stacked.shape[1]), jnp.float32), stacked.T, precision=lax.Precision.HIGHEST
             )
-            totals = lane_totals(local_totals, "row", block_size)
+            totals = lane_totals(copies, "row", block_size)
             curvature = totals[0]
             if inner_step == 0:
                 current_residual_product = totals[1]

time: 341 us -> 340 us (level)
  no operation moved by 1% of the time
where the time goes in v8:
time: 340 us; the launch traced here: 338 us
  blocking collectives  145 us (43%)
  starting transfers between devices  89.9 us (26%)
  waiting for transfers between devices  55.8 us (16%)
  matrix products  30.9 us (9%)
  other arithmetic  10.3 us (3%)
  local copies, waits for them, and re-layouts  4.15 us (1%)
    all_to_all x7, blocking collectives, all_sum(): return jnp.sum(lax.all_to_all(copies, axis, 0, 0, tiled=True), 0)  75.5 us
    all_to_all x4, blocking collectives, lane_totals(): received = lax.all_to_all(copies, axis, 0, 0, tiled=True)  69.5 us
    ppermute x14, starting transfers between devices, shifted(): lax.ppermute(value, axis, [(source, source + steps) for source in range(l...  56.3 us
    all_to_all x6, waiting for transfers between devices, multiply(): lax.all_to_all(jnp.concatenate([outgoing, far_backward], 1), 'row', split...  48.2 us
    all_to_all x6, starting transfers between devices, multiply(): lax.all_to_all(jnp.concatenate([outgoing, far_backward], 1), 'row', split...  23.6 us
    all_to_all x1, starting transfers between devices, multiply(): lax.all_to_all(jnp.concatenate([column_row, far_backward], 1), 'row', spl...  10 us
    dot_general x7, matrix products, multiply(): jnp.einsum('oqht,oqt->oqh', distant_local_part, gathered_values, preferre...  8.23 us
    all_to_all x1, waiting for transfers between devices, multiply(): lax.all_to_all(jnp.concatenate([column_row, far_backward], 1), 'row', spl...  7.55 us
  transfers between devices with their start and end apart: 21, of which 7 were waited for; matrix products, arithmetic and copies ran while one was open for 10% of the time, Pallas kernels for 0%

profile of v8, /device:TPU:1, one launch (start us, length us, event | category | flops | bytes accessed | tf_op | source)
XLA Modules:
  0.0 338.2 jit_solution(1244819878010646294)
XLA Ops:
  0.7 8.9 %collective-permute-start = (bf16[16,128]{1,0:T(8,128)(2,1)S(1)}, bf16[16,128]{1,0:T(8,128)(2,1)S(1)}, u32[]{:S(2)}, u32[]{:S(2)}) collective-permute-start(bf16[16,128]{1,0:T(8,128)(2,1)S(1)} %slice.200), channel_id=1, source_target_pairs={{16,0},{32,16},{48,32},{64,48},{80,64},{96,80},{112,96},{128,112},... | collective-permute-start | bytes 12296 | tf_op jit(solution)/shard_map/ppermute | solution.py:13
  13.9 10.0 %all-to-all-start = ((f32[32,3,128]{2,1,0:T(4,128)}), f32[32,3,128]{2,1,0:T(4,128)S(1)}, u32[]{:S(2)}, u32[]{:S(2)}) async-start(f32[32,3,128]{2,1,0:T(4,128)} %select_maximum_fusion), calls=%async_computation | async-start | bytes 131072 | tf_op jit(solution)/shard_map/all_to_all | solution.py:80
  24.6 3.5 %collective-permute-start.1 = (f32[16,128]{1,0:T(8,128)S(1)}, f32[16,128]{1,0:T(8,128)S(1)}, u32[]{:S(2)}, u32[]{:S(2)}) collective-permute-start(f32[16,128]{1,0:T(8,128)S(1)} %slice.261), channel_id=1, source_target_pairs={{0,16},{16,32},{32,48},{48,64},{64,80},{80,96},{96,112},{112,128},... | collective-permute-start | bytes 24584 | tf_op jit(solution)/shard_map/ppermute | solution.py:13
  29.4 7.5 %all-to-all-done = f32[32,3,128]{2,1,0:T(4,128)S(1)} async-done(((f32[32,3,128]{2,1,0:T(4,128)}), f32[32,3,128]{2,1,0:T(4,128)S(1)}, u32[]{:S(2)}, u32[]{:S(2)}) %all-to-all-start) | async-done | bytes 49184 | tf_op jit(solution)/shard_map/all_to_all | solution.py:80
  37.4 14.1 %all_to_all.116 = f32[16,32,128]{2,1,0:T(8,128)S(1)} all-to-all(f32[16,32,128]{2,1,0:T(8,128)S(1)} %broadcast_in_dim.17), channel_id=1, replica_groups=mesh['row'=32,'band'=16] {'band'}, dimensions={0} | all-to-all | bytes 524288 | tf_op jit(solution)/shard_map/all_to_all | solution.py:19
  52.0 4.9 %collective-permute-start.2 = (bf16[16,128]{1,0:T(8,128)(2,1)S(1)}, bf16[16,128]{1,0:T(8,128)(2,1)S(1)}, u32[]{:S(2)}, u32[]{:S(2)}) collective-permute-start(bf16[16,128]{1,0:T(8,128)(2,1)S(1)} %slice.263), channel_id=1, source_target_pairs={{16,0},{32,16},{48,32},{64,48},{80,64},{96,80},{112,96},{128,112},... | collective-permute-start | bytes 12296 | tf_op jit(solution)/shard_map/ppermute | solution.py:13
  58.4 4.0 %all-to-all-start.2 = ((f32[32,4,128]{2,1,0:T(4,128)}), f32[32,4,128]{2,1,0:T(4,128)S(1)}, u32[]{:S(2)}, u32[]{:S(2)}) async-start(f32[32,4,128]{2,1,0:T(4,128)} %pad_maximum_fusion), calls=%async_computation.2 | async-start | bytes 131072 | tf_op jit(solution)/shard_map/all_to_all | solution.py:89
  67.3 8.1 %all-to-all-done.2 = f32[32,4,128]{2,1,0:T(4,128)S(1)} async-done(((f32[32,4,128]{2,1,0:T(4,128)}), f32[32,4,128]{2,1,0:T(4,128)S(1)}, u32[]{:S(2)}, u32[]{:S(2)}) %all-to-all-start.2) | async-done | bytes 65568 | tf_op jit(solution)/shard_map/all_to_all | solution.py:89
  77.4 10.2 %all_to_all.117 = f32[16,32,128]{2,1,0:T(8,128)S(1)} all-to-all(f32[16,32,128]{2,1,0:T(8,128)S(1)} %broadcast_in_dim.18), channel_id=1, replica_groups=mesh['row'=32,'band'=16] {'band'}, dimensions={0} | all-to-all | bytes 524288 | tf_op jit(solution)/shard_map/all_to_all | solution.py:19
  88.0 4.9 %collective-permute-start.4 = (bf16[16,128]{1,0:T(8,128)(2,1)S(1)}, bf16[16,128]{1,0:T(8,128)(2,1)S(1)}, u32[]{:S(2)}, u32[]{:S(2)}) collective-permute-start(bf16[16,128]{1,0:T(8,128)(2,1)S(1)} %slice.270), channel_id=1, source_target_pairs={{16,0},{32,16},{48,32},{64,48},{80,64},{96,80},{112,96},{128,112},... | collective-permute-start | bytes 12296 | tf_op jit(solution)/shard_map/ppermute | solution.py:13
  94.3 3.6 %all-to-all-start.4 = ((f32[32,4,128]{2,1,0:T(4,128)}), f32[32,4,128]{2,1,0:T(4,128)S(1)}, u32[]{:S(2)}, u32[]{:S(2)}) async-start(f32[32,4,128]{2,1,0:T(4,128)} %pad_maximum_fusion.1), calls=%async_computation.4 | async-start | bytes 131072 | tf_op jit(solution)/shard_map/all_to_all | solution.py:89
  102.5 8.2 %all-to-all-done.4 = f32[32,4,128]{2,1,0:T(4,128)S(1)} async-done(((f32[32,4,128]{2,1,0:T(4,128)}), f32[32,4,128]{2,1,0:T(4,128)S(1)}, u32[]{:S(2)}, u32[]{:S(2)}) %all-to-all-start.4) | async-done | bytes 65568 | tf_op jit(solution)/shard_map/all_to_all | solution.py:89
  112.6 10.3 %all_to_all.118 = f32[16,32,128]{2,1,0:T(8,128)S(1)} all-to-all(f32[16,32,128]{2,1,0:T(8,128)S(1)} %broadcast_in_dim.19), channel_id=1, replica_groups=mesh['row'=32,'band'=16] {'band'}, dimensions={0} | all-to-all | bytes 524288 | tf_op jit(solution)/shard_map/all_to_all | solution.py:19
  123.6 17.3 %all_to_all.112 = f32[32,1,4]{2,1,0:T(1,128)S(1)} all-to-all(f32[32,1,4]{2,1,0:T(1,128)S(1)} %bitcast.441), channel_id=1, replica_groups=mesh['row'=32,'band'=16] {'row'}, dimensions={0} | all-to-all | bytes 1024 | tf_op jit(solution)/shard_map/all_to_all | solution.py:24
  145.8 4.1 %all-to-all-start.7 = ((f32[32,4,128]{2,1,0:T(4,128)}), f32[32,4,128]{2,1,0:T(4,128)S(1)}, u32[]{:S(2)}, u32[]{:S(2)}) async-start(f32[32,4,128]{2,1,0:T(4,128)} %pad_maximum_fusion.4), calls=%async_computation.7 | async-start | bytes 131072 | tf_op jit(solution)/shard_map/all_to_all | solution.py:89
  150.6 3.7 %collective-permute-start.7 = (f32[16,128]{1,0:T(8,128)S(1)}, f32[16,128]{1,0:T(8,128)S(1)}, u32[]{:S(2)}, u32[]{:S(2)}) collective-permute-start(f32[16,128]{1,0:T(8,128)S(1)} %slice.282), channel_id=1, source_target_pairs={{0,16},{16,32},{32,48},{48,64},{64,80},{80,96},{96,112},{112,128},... | collective-permute-start | bytes 24584 | tf_op jit(solution)/shard_map/ppermute | solution.py:13
  155.0 7.9 %all-to-all-done.7 = f32[32,4,128]{2,1,0:T(4,128)S(1)} async-done(((f32[32,4,128]{2,1,0:T(4,128)}), f32[32,4,128]{2,1,0:T(4,128)S(1)}, u32[]{:S(2)}, u32[]{:S(2)}) %all-to-all-start.7) | async-done | bytes 65568 | tf_op jit(solution)/shard_map/all_to_all | solution.py:89
  164.9 10.2 %all_to_all.119 = f32[16,32,128]{2,1,0:T(8,128)S(1)} all-to-all(f32[16,32,128]{2,1,0:T(8,128)S(1)} %broadcast_in_dim.20), channel_id=1, replica_groups=mesh['row'=32,'band'=16] {'band'}, dimensions={0} | all-to-all | bytes 524288 | tf_op jit(solution)/shard_map/all_to_all | solution.py:19
  175.7 17.5 %all_to_all.113 = f32[32,1,1]{2,1,0:T(1,128)S(1)} all-to-all(f32[32,1,1]{2,1,0:T(1,128)S(1)} %bitcast.443), channel_id=1, replica_groups=mesh['row'=32,'band'=16] {'row'}, dimensions={0} | all-to-all | bytes 256 | tf_op jit(solution)/shard_map/all_to_all | solution.py:24
  198.3 4.1 %all-to-all-start.10 = ((f32[32,4,128]{2,1,0:T(4,128)}), f32[32,4,128]{2,1,0:T(4,128)S(1)}, u32[]{:S(2)}, u32[]{:S(2)}) async-start(f32[32,4,128]{2,1,0:T(4,128)} %pad_maximum_fusion.5), calls=%async_computation.10 | async-start | bytes 131072 | tf_op jit(solution)/shard_map/all_to_all | solution.py:89
  207.3 8.1 %all-to-all-done.10 = f32[32,4,128]{2,1,0:T(4,128)S(1)} async-done(((f32[32,4,128]{2,1,0:T(4,128)}), f32[32,4,128]{2,1,0:T(4,128)S(1)}, u32[]{:S(2)}, u32[]{:S(2)}) %all-to-all-start.10) | async-done | bytes 65568 | tf_op jit(solution)/shard_map/all_to_all | solution.py:89
  217.4 10.2 %all_to_all.120 = f32[16,32,128]{2,1,0:T(8,128)S(1)} all-to-all(f32[16,32,128]{2,1,0:T(8,128)S(1)} %broadcast_in_dim.21), channel_id=1, replica_groups=mesh['row'=32,'band'=16] {'band'}, dimensions={0} | all-to-all | bytes 524288 | tf_op jit(solution)/shard_map/all_to_all | solution.py:19
  228.0 4.9 %collective-permute-start.10 = (bf16[16,128]{1,0:T(8,128)(2,1)S(1)}, bf16[16,128]{1,0:T(8,128)(2,1)S(1)}, u32[]{:S(2)}, u32[]{:S(2)}) collective-permute-start(bf16[16,128]{1,0:T(8,128)(2,1)S(1)} %slice.291), channel_id=1, source_target_pairs={{16,0},{32,16},{48,32},{64,48},{80,64},{96,80},{112,96},{128,112},... | collective-permute-start | bytes 12296 | tf_op jit(solution)/shard_map/ppermute | solution.py:13
  234.4 3.6 %all-to-all-start.12 = ((f32[32,4,128]{2,1,0:T(4,128)}), f32[32,4,128]{2,1,0:T(4,128)S(1)}, u32[]{:S(2)}, u32[]{:S(2)}) async-start(f32[32,4,128]{2,1,0:T(4,128)} %pad_maximum_fusion.6), calls=%async_computation.12 | async-start | bytes 131072 | tf_op jit(solution)/shard_map/all_to_all | solution.py:89
  242.5 8.2 %all-to-all-done.12 = f32[32,4,128]{2,1,0:T(4,128)S(1)} async-done(((f32[32,4,128]{2,1,0:T(4,128)}), f32[32,4,128]{2,1,0:T(4,128)S(1)}, u32[]{:S(2)}, u32[]{:S(2)}) %all-to-all-start.12) | async-done | bytes 65568 | tf_op jit(solution)/shard_map/all_to_all | solution.py:89
  252.7 10.3 %all_to_all.121 = f32[16,32,128]{2,1,0:T(8,128)S(1)} all-to-all(f32[16,32,128]{2,1,0:T(8,128)S(1)} %broadcast_in_dim.22), channel_id=1, replica_groups=mesh['row'=32,'band'=16] {'band'}, dimensions={0} | all-to-all | bytes 524288 | tf_op jit(solution)/shard_map/all_to_all | solution.py:19
  266.3 17.2 %all_to_all.114 = f32[32,1,4]{2,1,0:T(1,128)S(1)} all-to-all(f32[32,1,4]{2,1,0:T(1,128)S(1)} %bitcast.442), channel_id=1, replica_groups=mesh['row'=32,'band'=16] {'row'}, dimensions={0} | all-to-all | bytes 1024 | tf_op jit(solution)/shard_map/all_to_all | solution.py:24
  289.6 4.1 %all-to-all-start.15 = ((f32[32,4,128]{2,1,0:T(4,128)}), f32[32,4,128]{2,1,0:T(4,128)S(1)}, u32[]{:S(2)}, u32[]{:S(2)}) async-start(f32[32,4,128]{2,1,0:T(4,128)} %pad_maximum_fusion.9), calls=%async_computation.15 | async-start | bytes 131072 | tf_op jit(solution)/shard_map/all_to_all | solution.py:89
  294.4 3.8 %collective-permute-start.13 = (f32[16,128]{1,0:T(8,128)S(1)}, f32[16,128]{1,0:T(8,128)S(1)}, u32[]{:S(2)}, u32[]{:S(2)}) collective-permute-start(f32[16,128]{1,0:T(8,128)S(1)} %slice.303), channel_id=1, source_target_pairs={{0,16},{16,32},{32,48},{48,64},{64,80},{80,96},{96,112},{112,128},... | collective-permute-start | bytes 24584 | tf_op jit(solution)/shard_map/ppermute | solution.py:13
  298.9 7.8 %all-to-all-done.15 = f32[32,4,128]{2,1,0:T(4,128)S(1)} async-done(((f32[32,4,128]{2,1,0:T(4,128)}), f32[32,4,128]{2,1,0:T(4,128)S(1)}, u32[]{:S(2)}, u32[]{:S(2)}) %all-to-all-start.15) | async-done | bytes 65568 | tf_op jit(solution)/shard_map/all_to_all | solution.py:89
  308.7 10.2 %all_to_all.122 = f32[16,32,128]{2,1,0:T(8,128)S(1)} all-to-all(f32[16,32,128]{2,1,0:T(8,128)S(1)} %broadcast_in_dim.23), channel_id=1, replica_groups=mesh['row'=32,'band'=16] {'band'}, dimensions={0} | all-to-all | bytes 524288 | tf_op jit(solution)/shard_map/all_to_all | solution.py:19
  319.6 17.5 %all_to_all.115 = f32[32,1,1]{2,1,0:T(1,128)S(1)} all-to-all(f32[32,1,1]{2,1,0:T(1,128)S(1)} %bitcast.444), channel_id=1, replica_groups=mesh['row'=32,'band'=16] {'row'}, dimensions={0} | all-to-all | bytes 256 | tf_op jit(solution)/shard_map/all_to_all | solution.py:24
  (261 shorter events, 67.2 us)
Async XLA Ops:
  0.7 27.7 %collective-permute-start = (bf16[16,128]{1,0:T(8,128)(2,1)S(1)}, bf16[16,128]{1,0:T(8,128)(2,1)S(1)}, u32[]{:S(2)}, u32[]{:S(2)}) collective-permute-start(bf16[16,128]{1,0:T(8,128)(2,1)S(1)} %slice.200), channel_id=1, source_target_pairs={{16,0},{32,16},{48,32},{64,48},{80,64},{96,80},{112,96},{128,112},... | collective-permute-start | bytes 12296 | tf_op jit(solution)/shard_map/ppermute | solution.py:13
  13.9 23.0 %all-to-all-start = ((f32[32,3,128]{2,1,0:T(4,128)}), f32[32,3,128]{2,1,0:T(4,128)S(1)}, u32[]{:S(2)}, u32[]{:S(2)}) async-start(f32[32,3,128]{2,1,0:T(4,128)} %select_maximum_fusion), calls=%async_computation | async-start | bytes 131072 | tf_op jit(solution)/shard_map/all_to_all | solution.py:80
  24.3 214.1 %copy-start.7 = (f32[32]{0:T(128)}, f32[32]{0:T(128)S(1)}, u32[]{:S(2)}) copy-start(f32[32]{0:T(128)S(1)} %compare_select_fusion) | copy-start | bytes 388
  24.6 12.8 %collective-permute-start.1 = (f32[16,128]{1,0:T(8,128)S(1)}, f32[16,128]{1,0:T(8,128)S(1)}, u32[]{:S(2)}, u32[]{:S(2)}) collective-permute-start(f32[16,128]{1,0:T(8,128)S(1)} %slice.261), channel_id=1, source_target_pairs={{0,16},{16,32},{32,48},{48,64},{64,80},{80,96},{96,112},{112,128},... | collective-permute-start | bytes 24584 | tf_op jit(solution)/shard_map/ppermute | solution.py:13
  28.2 136.0 %copy-start.19 = (f32[32]{0:T(128)}, f32[32]{0:T(128)S(1)}, u32[]{:S(2)}) copy-start(f32[32]{0:T(128)S(1)} %compare_convert_fusion) | copy-start | bytes 388
  28.4 223.6 %copy-start.17 = (s32[64]{0:T(128)}, s32[64]{0:T(128)S(1)}, u32[]{:S(2)}) copy-start(s32[64]{0:T(128)S(1)} %eq.23) | copy-start | bytes 772
  37.1 215.2 %copy-start.5 = (s32[64]{0:T(128)}, s32[64]{0:T(128)S(1)}, u32[]{:S(2)}) copy-start(s32[64]{0:T(128)S(1)} %convert_element_type.140) | copy-start | bytes 772
  52.0 14.6 %collective-permute-start.2 = (bf16[16,128]{1,0:T(8,128)(2,1)S(1)}, bf16[16,128]{1,0:T(8,128)(2,1)S(1)}, u32[]{:S(2)}, u32[]{:S(2)}) collective-permute-start(bf16[16,128]{1,0:T(8,128)(2,1)S(1)} %slice.263), channel_id=1, source_target_pairs={{16,0},{32,16},{48,32},{64,48},{80,64},{96,80},{112,96},{128,112},... | collective-permute-start | bytes 12296 | tf_op jit(solution)/shard_map/ppermute | solution.py:13
  58.4 17.1 %all-to-all-start.2 = ((f32[32,4,128]{2,1,0:T(4,128)}), f32[32,4,128]{2,1,0:T(4,128)S(1)}, u32[]{:S(2)}, u32[]{:S(2)}) async-start(f32[32,4,128]{2,1,0:T(4,128)} %pad_maximum_fusion), calls=%async_computation.2 | async-start | bytes 131072 | tf_op jit(solution)/shard_map/all_to_all | solution.py:89
  63.1 14.2 %collective-permute-start.3 = (f32[16,128]{1,0:T(8,128)S(1)}, f32[16,128]{1,0:T(8,128)S(1)}, u32[]{:S(2)}, u32[]{:S(2)}) collective-permute-start(f32[16,128]{1,0:T(8,128)S(1)} %slice.268), channel_id=1, source_target_pairs={{0,16},{16,32},{32,48},{48,64},{64,80},{80,96},{96,112},{112,128},... | collective-permute-start | bytes 24584 | tf_op jit(solution)/shard_map/ppermute | solution.py:13
  88.0 13.8 %collective-permute-start.4 = (bf16[16,128]{1,0:T(8,128)(2,1)S(1)}, bf16[16,128]{1,0:T(8,128)(2,1)S(1)}, u32[]{:S(2)}, u32[]{:S(2)}) collective-permute-start(bf16[16,128]{1,0:T(8,128)(2,1)S(1)} %slice.270), channel_id=1, source_target_pairs={{16,0},{32,16},{48,32},{64,48},{80,64},{96,80},{112,96},{128,112},... | collective-permute-start | bytes 12296 | tf_op jit(solution)/shard_map/ppermute | solution.py:13
  94.3 16.3 %all-to-all-start.4 = ((f32[32,4,128]{2,1,0:T(4,128)}), f32[32,4,128]{2,1,0:T(4,128)S(1)}, u32[]{:S(2)}, u32[]{:S(2)}) async-start(f32[32,4,128]{2,1,0:T(4,128)} %pad_maximum_fusion.1), calls=%async_computation.4 | async-start | bytes 131072 | tf_op jit(solution)/shard_map/all_to_all | solution.py:89
  98.6 13.9 %collective-permute-start.5 = (f32[16,128]{1,0:T(8,128)S(1)}, f32[16,128]{1,0:T(8,128)S(1)}, u32[]{:S(2)}, u32[]{:S(2)}) collective-permute-start(f32[16,128]{1,0:T(8,128)S(1)} %slice.275), channel_id=1, source_target_pairs={{0,16},{16,32},{32,48},{48,64},{64,80},{80,96},{96,112},{112,128},... | collective-permute-start | bytes 24584 | tf_op jit(solution)/shard_map/ppermute | solution.py:13
  123.0 18.2 %copy-start.4 = (f32[1,4096]{1,0:T(1,128)}, f32[1,4096]{1,0:T(1,128)S(1)}, u32[]{:S(2)}) copy-start(f32[1,4096]{1,0:T(1,128)S(1)} %get-tuple-element.31) | copy-start | bytes 49156
  141.1 52.6 %copy-start.9 = (f32[128]{0:T(128)}, f32[128]{0:T(128)S(1)}, u32[]{:S(2)}) copy-start(f32[128]{0:T(128)S(1)} %get-tuple-element.25) | copy-start | bytes 1540
  141.1 52.6 %copy-start.11 = (f32[1,128]{1,0:T(1,128)}, f32[1,128]{1,0:T(1,128)S(1)}, u32[]{:S(2)}) copy-start(f32[1,128]{1,0:T(1,128)S(1)} %get-tuple-element.27) | copy-start | bytes 1540
  141.6 12.7 %collective-permute-start.6 = (bf16[16,128]{1,0:T(8,128)(2,1)S(1)}, bf16[16,128]{1,0:T(8,128)(2,1)S(1)}, u32[]{:S(2)}, u32[]{:S(2)}) collective-permute-start(bf16[16,128]{1,0:T(8,128)(2,1)S(1)} %slice.277), channel_id=1, source_target_pairs={{16,0},{32,16},{48,32},{64,48},{80,64},{96,80},{112,96},{128,112},... | collective-permute-start | bytes 12296 | tf_op jit(solution)/shard_map/ppermute | solution.py:13
  145.8 17.1 %all-to-all-start.7 = ((f32[32,4,128]{2,1,0:T(4,128)}), f32[32,4,128]{2,1,0:T(4,128)S(1)}, u32[]{:S(2)}, u32[]{:S(2)}) async-start(f32[32,4,128]{2,1,0:T(4,128)} %pad_maximum_fusion.4), calls=%async_computation.7 | async-start | bytes 131072 | tf_op jit(solution)/shard_map/all_to_all | solution.py:89
  150.6 14.3 %collective-permute-start.7 = (f32[16,128]{1,0:T(8,128)S(1)}, f32[16,128]{1,0:T(8,128)S(1)}, u32[]{:S(2)}, u32[]{:S(2)}) collective-permute-start(f32[16,128]{1,0:T(8,128)S(1)} %slice.282), channel_id=1, source_target_pairs={{0,16},{16,32},{32,48},{48,64},{64,80},{80,96},{96,112},{112,128},... | collective-permute-start | bytes 24584 | tf_op jit(solution)/shard_map/ppermute | solution.py:13
  194.1 12.5 %collective-permute-start.8 = (bf16[16,128]{1,0:T(8,128)(2,1)S(1)}, bf16[16,128]{1,0:T(8,128)(2,1)S(1)}, u32[]{:S(2)}, u32[]{:S(2)}) collective-permute-start(bf16[16,128]{1,0:T(8,128)(2,1)S(1)} %slice.284), channel_id=1, source_target_pairs={{16,0},{32,16},{48,32},{64,48},{80,64},{96,80},{112,96},{128,112},... | collective-permute-start | bytes 12296 | tf_op jit(solution)/shard_map/ppermute | solution.py:13
  198.3 17.1 %all-to-all-start.10 = ((f32[32,4,128]{2,1,0:T(4,128)}), f32[32,4,128]{2,1,0:T(4,128)S(1)}, u32[]{:S(2)}, u32[]{:S(2)}) async-start(f32[32,4,128]{2,1,0:T(4,128)} %pad_maximum_fusion.5), calls=%async_computation.10 | async-start | bytes 131072 | tf_op jit(solution)/shard_map/all_to_all | solution.py:89
  203.1 14.2 %collective-permute-start.9 = (f32[16,128]{1,0:T(8,128)S(1)}, f32[16,128]{1,0:T(8,128)S(1)}, u32[]{:S(2)}, u32[]{:S(2)}) collective-permute-start(f32[16,128]{1,0:T(8,128)S(1)} %slice.289), channel_id=1, source_target_pairs={{0,16},{16,32},{32,48},{48,64},{64,80},{80,96},{96,112},{112,128},... | collective-permute-start | bytes 24584 | tf_op jit(solution)/shard_map/ppermute | solution.py:13
  228.0 13.8 %collective-permute-start.10 = (bf16[16,128]{1,0:T(8,128)(2,1)S(1)}, bf16[16,128]{1,0:T(8,128)(2,1)S(1)}, u32[]{:S(2)}, u32[]{:S(2)}) collective-permute-start(bf16[16,128]{1,0:T(8,128)(2,1)S(1)} %slice.291), channel_id=1, source_target_pairs={{16,0},{32,16},{48,32},{64,48},{80,64},{96,80},{112,96},{128,112},... | collective-permute-start | bytes 12296 | tf_op jit(solution)/shard_map/ppermute | solution.py:13
  234.4 16.3 %all-to-all-start.12 = ((f32[32,4,128]{2,1,0:T(4,128)}), f32[32,4,128]{2,1,0:T(4,128)S(1)}, u32[]{:S(2)}, u32[]{:S(2)}) async-start(f32[32,4,128]{2,1,0:T(4,128)} %pad_maximum_fusion.6), calls=%async_computation.12 | async-start | bytes 131072 | tf_op jit(solution)/shard_map/all_to_all | solution.py:89
  238.7 13.9 %collective-permute-start.11 = (f32[16,128]{1,0:T(8,128)S(1)}, f32[16,128]{1,0:T(8,128)S(1)}, u32[]{:S(2)}, u32[]{:S(2)}) collective-permute-start(f32[16,128]{1,0:T(8,128)S(1)} %slice.296), channel_id=1, source_target_pairs={{0,16},{16,32},{32,48},{48,64},{64,80},{80,96},{96,112},{112,128},... | collective-permute-start | bytes 24584 | tf_op jit(solution)/shard_map/ppermute | solution.py:13
  265.7 28.4 %copy-start.8 = (f32[32]{0:T(128)S(1)}, f32[32]{0:T(128)}, u32[]{:S(2)}) copy-start(f32[32]{0:T(128)} %copy-done.7) | copy-start | bytes 388
  285.4 12.8 %collective-permute-start.12 = (bf16[16,128]{1,0:T(8,128)(2,1)S(1)}, bf16[16,128]{1,0:T(8,128)(2,1)S(1)}, u32[]{:S(2)}, u32[]{:S(2)}) collective-permute-start(bf16[16,128]{1,0:T(8,128)(2,1)S(1)} %slice.298), channel_id=1, source_target_pairs={{16,0},{32,16},{48,32},{64,48},{80,64},{96,80},{112,96},{128,112},... | collective-permute-start | bytes 12296 | tf_op jit(solution)/shard_map/ppermute | solution.py:13
  289.6 17.1 %all-to-all-start.15 = ((f32[32,4,128]{2,1,0:T(4,128)}), f32[32,4,128]{2,1,0:T(4,128)S(1)}, u32[]{:S(2)}, u32[]{:S(2)}) async-start(f32[32,4,128]{2,1,0:T(4,128)} %pad_maximum_fusion.9), calls=%async_computation.15 | async-start | bytes 131072 | tf_op jit(solution)/shard_map/all_to_all | solution.py:89
  294.4 14.3 %collective-permute-start.13 = (f32[16,128]{1,0:T(8,128)S(1)}, f32[16,128]{1,0:T(8,128)S(1)}, u32[]{:S(2)}, u32[]{:S(2)}) collective-permute-start(f32[16,128]{1,0:T(8,128)S(1)} %slice.303), channel_id=1, source_target_pairs={{0,16},{16,32},{32,48},{48,64},{64,80},{80,96},{96,112},{112,128},... | collective-permute-start | bytes 24584 | tf_op jit(solution)/shard_map/ppermute | solution.py:13
  298.9 20.1 %copy-start.10 = (f32[128]{0:T(128)S(1)}, f32[128]{0:T(128)}, u32[]{:S(2)}) copy-start(f32[128]{0:T(128)} %copy-done.9) | copy-start | bytes 1540
  298.9 20.1 %copy-start.12 = (f32[1,128]{1,0:T(1,128)S(1)}, f32[1,128]{1,0:T(1,128)}, u32[]{:S(2)}) copy-start(f32[1,128]{1,0:T(1,128)} %copy-done.11) | copy-start | bytes 1540
  298.9 20.1 %copy-start.14 = (f32[128]{0:T(128)S(1)}, f32[128]{0:T(128)}, u32[]{:S(2)}) copy-start(f32[128]{0:T(128)} %copy-done.13) | copy-start | bytes 1540
  (11 other events, 148.2 us)

commit v9 on v8

--- a/solution.py
+++ b/solution.py
@@ -101,13 +101,12 @@
             )
             * live_mask
         )
+        selection = jnp.concatenate([pick_in, selection_output], 0)
+        far_parts = jnp.concatenate(
+            [far_forward.reshape(-1, block_size), returned.reshape(-1, block_size)], 0
+        )
         summed = forward + spread[:rows_dev]
-        summed = summed + jnp.dot(
-            pick_in.T, far_forward.reshape(-1, block_size), precision=lax.Precision.HIGHEST
-        )
-        summed = summed + jnp.dot(
-            selection_output.T, returned.reshape(-1, block_size), precision=lax.Precision.HIGHEST
-        )
+        summed = summed + jnp.dot(selection.T, far_parts, precision=lax.Precision.HIGHEST)
         carried = shifted(spread[rows_dev:], "row", 1)
         summed = jnp.concatenate([summed[:band_count] + carried, summed[band_count:]], 0)
         return all_sum(summed, "band"), wanted

time: 340 us -> 339 us (level)
    all_to_all x1, starting transfers between devices: 10 us -> 16.7 us  [multiply(): lax.all_to_all(jnp.concatenate([column_row, far_backward], 1), 'row', spl...]
    ppermute x14, starting transfers between devices: 56.3 us -> 49.6 us  [shifted(): lax.ppermute(value, axis, [(source, source + steps) for source in range(l...]
  transfers between devices with their start and end apart: 21 -> 21, of which waited for: 7 -> 7; matrix products, arithmetic and copies ran while one was open for 10% -> 8% of each run, Pallas kernels for 0% -> 0%
where the time goes in v9:
time: 339 us; the launch traced here: 337 us
  blocking collectives  145 us (43%)
  starting transfers between devices  92.5 us (27%)
  waiting for transfers between devices  53.9 us (16%)
  matrix products  28.2 us (8%)
  other arithmetic  11.1 us (3%)
  local copies, waits for them, and re-layouts  4.15 us (1%)
    all_to_all x7, blocking collectives, all_sum(): return jnp.sum(lax.all_to_all(copies, axis, 0, 0, tiled=True), 0)  75.6 us
    all_to_all x4, blocking collectives, lane_totals(): received = lax.all_to_all(copies, axis, 0, 0, tiled=True)  69.8 us
    ppermute x14, starting transfers between devices, shifted(): lax.ppermute(value, axis, [(source, source + steps) for source in range(l...  49.6 us
    all_to_all x6, waiting for transfers between devices, multiply(): lax.all_to_all(jnp.concatenate([outgoing, far_backward], 1), 'row', split...  48 us
    all_to_all x6, starting transfers between devices, multiply(): lax.all_to_all(jnp.concatenate([outgoing, far_backward], 1), 'row', split...  26.1 us
    all_to_all x1, starting transfers between devices, multiply(): lax.all_to_all(jnp.concatenate([column_row, far_backward], 1), 'row', spl...  16.7 us
    dot_general x7, matrix products, multiply(): jnp.einsum('oqht,oqt->oqh', distant_local_part, gathered_values, preferre...  8.23 us
  transfers between devices with their start and end apart: 21, of which 7 were waited for; matrix products, arithmetic and copies ran while one was open for 8% of the time, Pallas kernels for 0%

profile of v9, /device:TPU:1, one launch (start us, length us, event | category | flops | bytes accessed | tf_op | source)
XLA Modules:
  0.0 337.2 jit_solution(9163007053477630353)
XLA Ops:
  5.1 16.7 %all-to-all-start = ((f32[32,3,128]{2,1,0:T(4,128)}), f32[32,3,128]{2,1,0:T(4,128)S(1)}, u32[]{:S(2)}, u32[]{:S(2)}) async-start(f32[32,3,128]{2,1,0:T(4,128)} %select_maximum_fusion), calls=%async_computation | async-start | bytes 131072 | tf_op jit(solution)/shard_map/all_to_all | solution.py:80
  29.1 5.8 %all-to-all-done = f32[32,3,128]{2,1,0:T(4,128)S(1)} async-done(((f32[32,3,128]{2,1,0:T(4,128)}), f32[32,3,128]{2,1,0:T(4,128)S(1)}, u32[]{:S(2)}, u32[]{:S(2)}) %all-to-all-start) | async-done | bytes 49184 | tf_op jit(solution)/shard_map/all_to_all | solution.py:80
  35.4 14.1 %all_to_all.116 = f32[16,32,128]{2,1,0:T(8,128)S(1)} all-to-all(f32[16,32,128]{2,1,0:T(8,128)S(1)} %broadcast_in_dim.17), channel_id=1, replica_groups=mesh['row'=32,'band'=16] {'band'}, dimensions={0} | all-to-all | bytes 524288 | tf_op jit(solution)/shard_map/all_to_all | solution.py:19
  50.0 4.9 %collective-permute-start.2 = (bf16[16,128]{1,0:T(8,128)(2,1)S(1)}, bf16[16,128]{1,0:T(8,128)(2,1)S(1)}, u32[]{:S(2)}, u32[]{:S(2)}) collective-permute-start(bf16[16,128]{1,0:T(8,128)(2,1)S(1)} %slice.263), channel_id=1, source_target_pairs={{16,0},{32,16},{48,32},{64,48},{80,64},{96,80},{112,96},{128,112},... | collective-permute-start | bytes 12296 | tf_op jit(solution)/shard_map/ppermute | solution.py:13
  56.3 6.5 %all-to-all-start.2 = ((f32[32,4,128]{2,1,0:T(4,128)}), f32[32,4,128]{2,1,0:T(4,128)S(1)}, u32[]{:S(2)}, u32[]{:S(2)}) async-start(f32[32,4,128]{2,1,0:T(4,128)} %pad_maximum_fusion), calls=%async_computation.2 | async-start | bytes 131072 | tf_op jit(solution)/shard_map/all_to_all | solution.py:89
  63.5 3.5 %collective-permute-start.3 = (f32[16,128]{1,0:T(8,128)S(1)}, f32[16,128]{1,0:T(8,128)S(1)}, u32[]{:S(2)}, u32[]{:S(2)}) collective-permute-start(f32[16,128]{1,0:T(8,128)S(1)} %slice.268), channel_id=1, source_target_pairs={{0,16},{16,32},{32,48},{48,64},{64,80},{80,96},{96,112},{112,128},... | collective-permute-start | bytes 24584 | tf_op jit(solution)/shard_map/ppermute | solution.py:13
  67.8 8.1 %all-to-all-done.2 = f32[32,4,128]{2,1,0:T(4,128)S(1)} async-done(((f32[32,4,128]{2,1,0:T(4,128)}), f32[32,4,128]{2,1,0:T(4,128)S(1)}, u32[]{:S(2)}, u32[]{:S(2)}) %all-to-all-start.2) | async-done | bytes 65568 | tf_op jit(solution)/shard_map/all_to_all | solution.py:89
  77.4 10.2 %all_to_all.117 = f32[16,32,128]{2,1,0:T(8,128)S(1)} all-to-all(f32[16,32,128]{2,1,0:T(8,128)S(1)} %broadcast_in_dim.18), channel_id=1, replica_groups=mesh['row'=32,'band'=16] {'band'}, dimensions={0} | all-to-all | bytes 524288 | tf_op jit(solution)/shard_map/all_to_all | solution.py:19
  88.1 4.6 %collective-permute-start.4 = (bf16[16,128]{1,0:T(8,128)(2,1)S(1)}, bf16[16,128]{1,0:T(8,128)(2,1)S(1)}, u32[]{:S(2)}, u32[]{:S(2)}) collective-permute-start(bf16[16,128]{1,0:T(8,128)(2,1)S(1)} %slice.270), channel_id=1, source_target_pairs={{16,0},{32,16},{48,32},{64,48},{80,64},{96,80},{112,96},{128,112},... | collective-permute-start | bytes 12296 | tf_op jit(solution)/shard_map/ppermute | solution.py:13
  94.1 3.7 %all-to-all-start.4 = ((f32[32,4,128]{2,1,0:T(4,128)}), f32[32,4,128]{2,1,0:T(4,128)S(1)}, u32[]{:S(2)}, u32[]{:S(2)}) async-start(f32[32,4,128]{2,1,0:T(4,128)} %pad_maximum_fusion.1), calls=%async_computation.4 | async-start | bytes 131072 | tf_op jit(solution)/shard_map/all_to_all | solution.py:89
  98.5 3.5 %collective-permute-start.5 = (f32[16,128]{1,0:T(8,128)S(1)}, f32[16,128]{1,0:T(8,128)S(1)}, u32[]{:S(2)}, u32[]{:S(2)}) collective-permute-start(f32[16,128]{1,0:T(8,128)S(1)} %slice.275), channel_id=1, source_target_pairs={{0,16},{16,32},{32,48},{48,64},{64,80},{80,96},{96,112},{112,128},... | collective-permute-start | bytes 24584 | tf_op jit(solution)/shard_map/ppermute | solution.py:13
  102.7 8.1 %all-to-all-done.4 = f32[32,4,128]{2,1,0:T(4,128)S(1)} async-done(((f32[32,4,128]{2,1,0:T(4,128)}), f32[32,4,128]{2,1,0:T(4,128)S(1)}, u32[]{:S(2)}, u32[]{:S(2)}) %all-to-all-start.4) | async-done | bytes 65568 | tf_op jit(solution)/shard_map/all_to_all | solution.py:89
  112.4 10.3 %all_to_all.118 = f32[16,32,128]{2,1,0:T(8,128)S(1)} all-to-all(f32[16,32,128]{2,1,0:T(8,128)S(1)} %broadcast_in_dim.19), channel_id=1, replica_groups=mesh['row'=32,'band'=16] {'band'}, dimensions={0} | all-to-all | bytes 524288 | tf_op jit(solution)/shard_map/all_to_all | solution.py:19
  123.4 17.5 %all_to_all.112 = f32[32,1,4]{2,1,0:T(1,128)S(1)} all-to-all(f32[32,1,4]{2,1,0:T(1,128)S(1)} %bitcast.434), channel_id=1, replica_groups=mesh['row'=32,'band'=16] {'row'}, dimensions={0} | all-to-all | bytes 1024 | tf_op jit(solution)/shard_map/all_to_all | solution.py:24
  146.4 4.1 %all-to-all-start.7 = ((f32[32,4,128]{2,1,0:T(4,128)}), f32[32,4,128]{2,1,0:T(4,128)S(1)}, u32[]{:S(2)}, u32[]{:S(2)}) async-start(f32[32,4,128]{2,1,0:T(4,128)} %pad_maximum_fusion.4), calls=%async_computation.7 | async-start | bytes 131072 | tf_op jit(solution)/shard_map/all_to_all | solution.py:89
  151.1 3.7 %collective-permute-start.7 = (f32[16,128]{1,0:T(8,128)S(1)}, f32[16,128]{1,0:T(8,128)S(1)}, u32[]{:S(2)}, u32[]{:S(2)}) collective-permute-start(f32[16,128]{1,0:T(8,128)S(1)} %slice.282), channel_id=1, source_target_pairs={{0,16},{16,32},{32,48},{48,64},{64,80},{80,96},{96,112},{112,128},... | collective-permute-start | bytes 24584 | tf_op jit(solution)/shard_map/ppermute | solution.py:13
  155.6 7.9 %all-to-all-done.7 = f32[32,4,128]{2,1,0:T(4,128)S(1)} async-done(((f32[32,4,128]{2,1,0:T(4,128)}), f32[32,4,128]{2,1,0:T(4,128)S(1)}, u32[]{:S(2)}, u32[]{:S(2)}) %all-to-all-start.7) | async-done | bytes 65568 | tf_op jit(solution)/shard_map/all_to_all | solution.py:89
  165.1 10.2 %all_to_all.119 = f32[16,32,128]{2,1,0:T(8,128)S(1)} all-to-all(f32[16,32,128]{2,1,0:T(8,128)S(1)} %broadcast_in_dim.20), channel_id=1, replica_groups=mesh['row'=32,'band'=16] {'band'}, dimensions={0} | all-to-all | bytes 524288 | tf_op jit(solution)/shard_map/all_to_all | solution.py:19
  175.9 17.5 %all_to_all.113 = f32[32,1,1]{2,1,0:T(1,128)S(1)} all-to-all(f32[32,1,1]{2,1,0:T(1,128)S(1)} %bitcast.436), channel_id=1, replica_groups=mesh['row'=32,'band'=16] {'row'}, dimensions={0} | all-to-all | bytes 256 | tf_op jit(solution)/shard_map/all_to_all | solution.py:24
  198.5 4.1 %all-to-all-start.10 = ((f32[32,4,128]{2,1,0:T(4,128)}), f32[32,4,128]{2,1,0:T(4,128)S(1)}, u32[]{:S(2)}, u32[]{:S(2)}) async-start(f32[32,4,128]{2,1,0:T(4,128)} %pad_maximum_fusion.5), calls=%async_computation.10 | async-start | bytes 131072 | tf_op jit(solution)/shard_map/all_to_all | solution.py:89
  207.5 8.1 %all-to-all-done.10 = f32[32,4,128]{2,1,0:T(4,128)S(1)} async-done(((f32[32,4,128]{2,1,0:T(4,128)}), f32[32,4,128]{2,1,0:T(4,128)S(1)}, u32[]{:S(2)}, u32[]{:S(2)}) %all-to-all-start.10) | async-done | bytes 65568 | tf_op jit(solution)/shard_map/all_to_all | solution.py:89
  217.2 10.2 %all_to_all.120 = f32[16,32,128]{2,1,0:T(8,128)S(1)} all-to-all(f32[16,32,128]{2,1,0:T(8,128)S(1)} %broadcast_in_dim.21), channel_id=1, replica_groups=mesh['row'=32,'band'=16] {'band'}, dimensions={0} | all-to-all | bytes 524288 | tf_op jit(solution)/shard_map/all_to_all | solution.py:19
  227.8 4.9 %collective-permute-start.10 = (bf16[16,128]{1,0:T(8,128)(2,1)S(1)}, bf16[16,128]{1,0:T(8,128)(2,1)S(1)}, u32[]{:S(2)}, u32[]{:S(2)}) collective-permute-start(bf16[16,128]{1,0:T(8,128)(2,1)S(1)} %slice.291), channel_id=1, source_target_pairs={{16,0},{32,16},{48,32},{64,48},{80,64},{96,80},{112,96},{128,112},... | collective-permute-start | bytes 12296 | tf_op jit(solution)/shard_map/ppermute | solution.py:13
  234.2 3.6 %all-to-all-start.12 = ((f32[32,4,128]{2,1,0:T(4,128)}), f32[32,4,128]{2,1,0:T(4,128)S(1)}, u32[]{:S(2)}, u32[]{:S(2)}) async-start(f32[32,4,128]{2,1,0:T(4,128)} %pad_maximum_fusion.6), calls=%async_computation.12 | async-start | bytes 131072 | tf_op jit(solution)/shard_map/all_to_all | solution.py:89
  242.3 8.0 %all-to-all-done.12 = f32[32,4,128]{2,1,0:T(4,128)S(1)} async-done(((f32[32,4,128]{2,1,0:T(4,128)}), f32[32,4,128]{2,1,0:T(4,128)S(1)}, u32[]{:S(2)}, u32[]{:S(2)}) %all-to-all-start.12) | async-done | bytes 65568 | tf_op jit(solution)/shard_map/all_to_all | solution.py:89
  251.9 10.4 %all_to_all.121 = f32[16,32,128]{2,1,0:T(8,128)S(1)} all-to-all(f32[16,32,128]{2,1,0:T(8,128)S(1)} %broadcast_in_dim.22), channel_id=1, replica_groups=mesh['row'=32,'band'=16] {'band'}, dimensions={0} | all-to-all | bytes 524288 | tf_op jit(solution)/shard_map/all_to_all | solution.py:19
  265.7 17.3 %all_to_all.114 = f32[32,1,4]{2,1,0:T(1,128)S(1)} all-to-all(f32[32,1,4]{2,1,0:T(1,128)S(1)} %bitcast.435), channel_id=1, replica_groups=mesh['row'=32,'band'=16] {'row'}, dimensions={0} | all-to-all | bytes 1024 | tf_op jit(solution)/shard_map/all_to_all | solution.py:24
  289.1 4.1 %all-to-all-start.15 = ((f32[32,4,128]{2,1,0:T(4,128)}), f32[32,4,128]{2,1,0:T(4,128)S(1)}, u32[]{:S(2)}, u32[]{:S(2)}) async-start(f32[32,4,128]{2,1,0:T(4,128)} %pad_maximum_fusion.9), calls=%async_computation.15 | async-start | bytes 131072 | tf_op jit(solution)/shard_map/all_to_all | solution.py:89
  293.8 3.8 %collective-permute-start.13 = (f32[16,128]{1,0:T(8,128)S(1)}, f32[16,128]{1,0:T(8,128)S(1)}, u32[]{:S(2)}, u32[]{:S(2)}) collective-permute-start(f32[16,128]{1,0:T(8,128)S(1)} %slice.303), channel_id=1, source_target_pairs={{0,16},{16,32},{32,48},{48,64},{64,80},{80,96},{96,112},{112,128},... | collective-permute-start | bytes 24584 | tf_op jit(solution)/shard_map/ppermute | solution.py:13
  298.3 7.8 %all-to-all-done.15 = f32[32,4,128]{2,1,0:T(4,128)S(1)} async-done(((f32[32,4,128]{2,1,0:T(4,128)}), f32[32,4,128]{2,1,0:T(4,128)S(1)}, u32[]{:S(2)}, u32[]{:S(2)}) %all-to-all-start.15) | async-done | bytes 65568 | tf_op jit(solution)/shard_map/all_to_all | solution.py:89
  307.7 10.2 %all_to_all.122 = f32[16,32,128]{2,1,0:T(8,128)S(1)} all-to-all(f32[16,32,128]{2,1,0:T(8,128)S(1)} %broadcast_in_dim.23), channel_id=1, replica_groups=mesh['row'=32,'band'=16] {'band'}, dimensions={0} | all-to-all | bytes 524288 | tf_op jit(solution)/shard_map/all_to_all | solution.py:19
  318.6 17.5 %all_to_all.115 = f32[32,1,1]{2,1,0:T(1,128)S(1)} all-to-all(f32[32,1,1]{2,1,0:T(1,128)S(1)} %bitcast.437), channel_id=1, replica_groups=mesh['row'=32,'band'=16] {'row'}, dimensions={0} | all-to-all | bytes 256 | tf_op jit(solution)/shard_map/all_to_all | solution.py:24
  (255 shorter events, 64.1 us)
Async XLA Ops:
  2.4 21.6 %copy-start.1 = (bf16[32,1,128,128]{3,2,1,0:T(8,128)(2,1)S(1)}, bf16[32,1,128,128]{3,2,1,0:T(8,128)(2,1)}, u32[]{:S(2)}) copy-start(bf16[32,1,128,128]{3,2,1,0:T(8,128)(2,1)} %param.7) | copy-start | bytes 3145732
  3.6 24.6 %copy-start.18 = (s32[1,1,32,2]{2,3,1,0:T(2,128)S(1)}, s32[1,1,32,2]{2,3,1,0:T(2,128)}, u32[]{:S(2)}) copy-start(s32[1,1,32,2]{2,3,1,0:T(2,128)} %param.9) | copy-start | bytes 772
  5.1 29.8 %all-to-all-start = ((f32[32,3,128]{2,1,0:T(4,128)}), f32[32,3,128]{2,1,0:T(4,128)S(1)}, u32[]{:S(2)}, u32[]{:S(2)}) async-start(f32[32,3,128]{2,1,0:T(4,128)} %select_maximum_fusion), calls=%async_computation | async-start | bytes 131072 | tf_op jit(solution)/shard_map/all_to_all | solution.py:80
  21.9 6.5 %collective-permute-start = (bf16[16,128]{1,0:T(8,128)(2,1)S(1)}, bf16[16,128]{1,0:T(8,128)(2,1)S(1)}, u32[]{:S(2)}, u32[]{:S(2)}) collective-permute-start(bf16[16,128]{1,0:T(8,128)(2,1)S(1)} %slice.200), channel_id=1, source_target_pairs={{16,0},{32,16},{48,32},{64,48},{80,64},{96,80},{112,96},{128,112},... | collective-permute-start | bytes 12296 | tf_op jit(solution)/shard_map/ppermute | solution.py:13
  24.4 213.7 %copy-start.6 = (f32[32]{0:T(128)}, f32[32]{0:T(128)S(1)}, u32[]{:S(2)}) copy-start(f32[32]{0:T(128)S(1)} %compare_select_fusion) | copy-start | bytes 388
  24.7 10.6 %collective-permute-start.1 = (f32[16,128]{1,0:T(8,128)S(1)}, f32[16,128]{1,0:T(8,128)S(1)}, u32[]{:S(2)}, u32[]{:S(2)}) collective-permute-start(f32[16,128]{1,0:T(8,128)S(1)} %slice.261), channel_id=1, source_target_pairs={{0,16},{16,32},{32,48},{48,64},{64,80},{80,96},{96,112},{112,128},... | collective-permute-start | bytes 24584 | tf_op jit(solution)/shard_map/ppermute | solution.py:13
  28.4 199.3 %copy-start.8 = (s32[64]{0:T(128)}, s32[64]{0:T(128)S(1)}, u32[]{:S(2)}) copy-start(s32[64]{0:T(128)S(1)} %eq.23) | copy-start | bytes 772
  28.4 223.3 %copy-start.10 = (f32[32]{0:T(128)}, f32[32]{0:T(128)S(1)}, u32[]{:S(2)}) copy-start(f32[32]{0:T(128)S(1)} %compare_convert_fusion) | copy-start | bytes 388
  35.0 192.4 %copy-start.9 = (s32[64]{0:T(128)}, s32[64]{0:T(128)S(1)}, u32[]{:S(2)}) copy-start(s32[64]{0:T(128)S(1)} %convert_element_type.143) | copy-start | bytes 772
  50.0 17.1 %collective-permute-start.2 = (bf16[16,128]{1,0:T(8,128)(2,1)S(1)}, bf16[16,128]{1,0:T(8,128)(2,1)S(1)}, u32[]{:S(2)}, u32[]{:S(2)}) collective-permute-start(bf16[16,128]{1,0:T(8,128)(2,1)S(1)} %slice.263), channel_id=1, source_target_pairs={{16,0},{32,16},{48,32},{64,48},{80,64},{96,80},{112,96},{128,112},... | collective-permute-start | bytes 12296 | tf_op jit(solution)/shard_map/ppermute | solution.py:13
  56.3 19.6 %all-to-all-start.2 = ((f32[32,4,128]{2,1,0:T(4,128)}), f32[32,4,128]{2,1,0:T(4,128)S(1)}, u32[]{:S(2)}, u32[]{:S(2)}) async-start(f32[32,4,128]{2,1,0:T(4,128)} %pad_maximum_fusion), calls=%async_computation.2 | async-start | bytes 131072 | tf_op jit(solution)/shard_map/all_to_all | solution.py:89
  63.5 13.9 %collective-permute-start.3 = (f32[16,128]{1,0:T(8,128)S(1)}, f32[16,128]{1,0:T(8,128)S(1)}, u32[]{:S(2)}, u32[]{:S(2)}) collective-permute-start(f32[16,128]{1,0:T(8,128)S(1)} %slice.268), channel_id=1, source_target_pairs={{0,16},{16,32},{32,48},{48,64},{64,80},{80,96},{96,112},{112,128},... | collective-permute-start | bytes 24584 | tf_op jit(solution)/shard_map/ppermute | solution.py:13
  87.7 35.0 %copy-start.2 = (f32[32,128]{1,0:T(8,128)}, f32[32,128]{1,0:T(8,128)S(1)}, u32[]{:S(2)}) copy-start(f32[32,128]{1,0:T(8,128)S(1)} %get-tuple-element.51) | copy-start | bytes 49156
  88.1 14.0 %collective-permute-start.4 = (bf16[16,128]{1,0:T(8,128)(2,1)S(1)}, bf16[16,128]{1,0:T(8,128)(2,1)S(1)}, u32[]{:S(2)}, u32[]{:S(2)}) collective-permute-start(bf16[16,128]{1,0:T(8,128)(2,1)S(1)} %slice.270), channel_id=1, source_target_pairs={{16,0},{32,16},{48,32},{64,48},{80,64},{96,80},{112,96},{128,112},... | collective-permute-start | bytes 12296 | tf_op jit(solution)/shard_map/ppermute | solution.py:13
  94.1 16.7 %all-to-all-start.4 = ((f32[32,4,128]{2,1,0:T(4,128)}), f32[32,4,128]{2,1,0:T(4,128)S(1)}, u32[]{:S(2)}, u32[]{:S(2)}) async-start(f32[32,4,128]{2,1,0:T(4,128)} %pad_maximum_fusion.1), calls=%async_computation.4 | async-start | bytes 131072 | tf_op jit(solution)/shard_map/all_to_all | solution.py:89
  98.5 13.9 %collective-permute-start.5 = (f32[16,128]{1,0:T(8,128)S(1)}, f32[16,128]{1,0:T(8,128)S(1)}, u32[]{:S(2)}, u32[]{:S(2)}) collective-permute-start(f32[16,128]{1,0:T(8,128)S(1)} %slice.275), channel_id=1, source_target_pairs={{0,16},{16,32},{32,48},{48,64},{64,80},{80,96},{96,112},{112,128},... | collective-permute-start | bytes 24584 | tf_op jit(solution)/shard_map/ppermute | solution.py:13
  141.7 52.2 %copy-start.12 = (f32[128]{0:T(128)}, f32[128]{0:T(128)S(1)}, u32[]{:S(2)}) copy-start(f32[128]{0:T(128)S(1)} %get-tuple-element.25) | copy-start | bytes 1540
  141.7 52.2 %copy-start.14 = (f32[1,128]{1,0:T(1,128)}, f32[1,128]{1,0:T(1,128)S(1)}, u32[]{:S(2)}) copy-start(f32[1,128]{1,0:T(1,128)S(1)} %get-tuple-element.27) | copy-start | bytes 1540
  142.1 12.7 %collective-permute-start.6 = (bf16[16,128]{1,0:T(8,128)(2,1)S(1)}, bf16[16,128]{1,0:T(8,128)(2,1)S(1)}, u32[]{:S(2)}, u32[]{:S(2)}) collective-permute-start(bf16[16,128]{1,0:T(8,128)(2,1)S(1)} %slice.277), channel_id=1, source_target_pairs={{16,0},{32,16},{48,32},{64,48},{80,64},{96,80},{112,96},{128,112},... | collective-permute-start | bytes 12296 | tf_op jit(solution)/shard_map/ppermute | solution.py:13
  146.4 17.1 %all-to-all-start.7 = ((f32[32,4,128]{2,1,0:T(4,128)}), f32[32,4,128]{2,1,0:T(4,128)S(1)}, u32[]{:S(2)}, u32[]{:S(2)}) async-start(f32[32,4,128]{2,1,0:T(4,128)} %pad_maximum_fusion.4), calls=%async_computation.7 | async-start | bytes 131072 | tf_op jit(solution)/shard_map/all_to_all | solution.py:89
  151.1 13.9 %collective-permute-start.7 = (f32[16,128]{1,0:T(8,128)S(1)}, f32[16,128]{1,0:T(8,128)S(1)}, u32[]{:S(2)}, u32[]{:S(2)}) collective-permute-start(f32[16,128]{1,0:T(8,128)S(1)} %slice.282), channel_id=1, source_target_pairs={{0,16},{16,32},{32,48},{48,64},{64,80},{80,96},{96,112},{112,128},... | collective-permute-start | bytes 24584 | tf_op jit(solution)/shard_map/ppermute | solution.py:13
  155.6 38.2 %copy-start.20 = (f32[1,128]{1,0:T(1,128)S(1)}, f32[1,128]{1,0:T(1,128)}, u32[]{:S(2)}) copy-start(f32[1,128]{1,0:T(1,128)} %get-tuple-element.26) | copy-start | bytes 1540
  194.3 12.5 %collective-permute-start.8 = (bf16[16,128]{1,0:T(8,128)(2,1)S(1)}, bf16[16,128]{1,0:T(8,128)(2,1)S(1)}, u32[]{:S(2)}, u32[]{:S(2)}) collective-permute-start(bf16[16,128]{1,0:T(8,128)(2,1)S(1)} %slice.284), channel_id=1, source_target_pairs={{16,0},{32,16},{48,32},{64,48},{80,64},{96,80},{112,96},{128,112},... | collective-permute-start | bytes 12296 | tf_op jit(solution)/shard_map/ppermute | solution.py:13
  198.5 17.1 %all-to-all-start.10 = ((f32[32,4,128]{2,1,0:T(4,128)}), f32[32,4,128]{2,1,0:T(4,128)S(1)}, u32[]{:S(2)}, u32[]{:S(2)}) async-start(f32[32,4,128]{2,1,0:T(4,128)} %pad_maximum_fusion.5), calls=%async_computation.10 | async-start | bytes 131072 | tf_op jit(solution)/shard_map/all_to_all | solution.py:89
  203.3 13.9 %collective-permute-start.9 = (f32[16,128]{1,0:T(8,128)S(1)}, f32[16,128]{1,0:T(8,128)S(1)}, u32[]{:S(2)}, u32[]{:S(2)}) collective-permute-start(f32[16,128]{1,0:T(8,128)S(1)} %slice.289), channel_id=1, source_target_pairs={{0,16},{16,32},{32,48},{48,64},{64,80},{80,96},{96,112},{112,128},... | collective-permute-start | bytes 24584 | tf_op jit(solution)/shard_map/ppermute | solution.py:13
  227.8 13.8 %collective-permute-start.10 = (bf16[16,128]{1,0:T(8,128)(2,1)S(1)}, bf16[16,128]{1,0:T(8,128)(2,1)S(1)}, u32[]{:S(2)}, u32[]{:S(2)}) collective-permute-start(bf16[16,128]{1,0:T(8,128)(2,1)S(1)} %slice.291), channel_id=1, source_target_pairs={{16,0},{32,16},{48,32},{64,48},{80,64},{96,80},{112,96},{128,112},... | collective-permute-start | bytes 12296 | tf_op jit(solution)/shard_map/ppermute | solution.py:13
  234.2 16.2 %all-to-all-start.12 = ((f32[32,4,128]{2,1,0:T(4,128)}), f32[32,4,128]{2,1,0:T(4,128)S(1)}, u32[]{:S(2)}, u32[]{:S(2)}) async-start(f32[32,4,128]{2,1,0:T(4,128)} %pad_maximum_fusion.6), calls=%async_computation.12 | async-start | bytes 131072 | tf_op jit(solution)/shard_map/all_to_all | solution.py:89
  238.5 13.4 %collective-permute-start.11 = (f32[16,128]{1,0:T(8,128)S(1)}, f32[16,128]{1,0:T(8,128)S(1)}, u32[]{:S(2)}, u32[]{:S(2)}) collective-permute-start(f32[16,128]{1,0:T(8,128)S(1)} %slice.296), channel_id=1, source_target_pairs={{0,16},{16,32},{32,48},{48,64},{64,80},{80,96},{96,112},{112,128},... | collective-permute-start | bytes 24584 | tf_op jit(solution)/shard_map/ppermute | solution.py:13
  265.1 28.5 %copy-start.7 = (f32[32]{0:T(128)S(1)}, f32[32]{0:T(128)}, u32[]{:S(2)}) copy-start(f32[32]{0:T(128)} %copy-done.6) | copy-start | bytes 388
  284.8 12.8 %collective-permute-start.12 = (bf16[16,128]{1,0:T(8,128)(2,1)S(1)}, bf16[16,128]{1,0:T(8,128)(2,1)S(1)}, u32[]{:S(2)}, u32[]{:S(2)}) collective-permute-start(bf16[16,128]{1,0:T(8,128)(2,1)S(1)} %slice.298), channel_id=1, source_target_pairs={{16,0},{32,16},{48,32},{64,48},{80,64},{96,80},{112,96},{128,112},... | collective-permute-start | bytes 12296 | tf_op jit(solution)/shard_map/ppermute | solution.py:13
  289.1 17.1 %all-to-all-start.15 = ((f32[32,4,128]{2,1,0:T(4,128)}), f32[32,4,128]{2,1,0:T(4,128)S(1)}, u32[]{:S(2)}, u32[]{:S(2)}) async-start(f32[32,4,128]{2,1,0:T(4,128)} %pad_maximum_fusion.9), calls=%async_computation.15 | async-start | bytes 131072 | tf_op jit(solution)/shard_map/all_to_all | solution.py:89
  293.8 13.9 %collective-permute-start.13 = (f32[16,128]{1,0:T(8,128)S(1)}, f32[16,128]{1,0:T(8,128)S(1)}, u32[]{:S(2)}, u32[]{:S(2)}) collective-permute-start(f32[16,128]{1,0:T(8,128)S(1)} %slice.303), channel_id=1, source_target_pairs={{0,16},{16,32},{32,48},{48,64},{64,80},{80,96},{96,112},{112,128},... | collective-permute-start | bytes 24584 | tf_op jit(solution)/shard_map/ppermute | solution.py:13
  (10 other events, 150.0 us)

commit v10 on v9

--- a/solution.py
+++ b/solution.py
@@ -45,6 +45,11 @@
     targets = jnp.arange(rows_dev)[None, :]
     pick_in = (local_row_values.reshape(-1)[:, None] == targets).astype(jnp.float32)
     pick_rows = pick_in.astype(jnp.bfloat16)
+    identity_blocks = jnp.broadcast_to(
+        jnp.eye(block_size, dtype=jnp.bfloat16), (row_count, slots, block_size, block_size)
+    )
+    exchange_blocks = jnp.concatenate([identity_blocks, distant_local_part], 1)
+    exchange_mask = jnp.concatenate([jnp.ones_like(live_mask), live_mask], 1)
 
     def picked(selection, vector):
         product = jnp.dot(selection, vector, preferred_element_type=jnp.float32)
@@ -84,11 +89,22 @@
             gathered_values = jnp.ones((row_count, slots, block_size), jnp.bfloat16)
             returned = exchanged[:, 1:]
         else:
-            pick_out = (wanted.reshape(-1)[:, None] == targets).astype(jnp.bfloat16)
-            outgoing = picked(pick_out, narrow_band_part)
-            exchanged = lax.all_to_all(
-                jnp.concatenate([outgoing, far_backward], 1), "row", split_axis=0, concat_axis=0, tiled=True
+            selection_both = jnp.concatenate(
+                [wanted[..., None] == targets[None], local_row_values[..., None] == targets[None]], 1
+            ).astype(jnp.bfloat16)
+            vectors = jnp.dot(
+                selection_both.reshape(-1, rows_dev), narrow_band_part, preferred_element_type=jnp.float32
+            ).reshape(row_count, 2 * slots, block_size)
+            payload = (
+                jnp.einsum(
+                    "nquo,nqu->nqo",
+                    exchange_blocks,
+                    vectors.astype(jnp.bfloat16),
+                    preferred_element_type=jnp.float32,
+                )
+                * exchange_mask
             )
+            exchanged = lax.all_to_all(payload, "row", split_axis=0, concat_axis=0, tiled=True)
             gathered_values = exchanged[:, :slots].astype(jnp.bfloat16)
             returned = exchanged[:, slots:]
         selection_output = (wanted.reshape(-1)[:, None] == targets).astype(jnp.float32)

time: 339 us -> 355 us (1.047)
  blocking collectives: 145 us -> 131 us
  matrix products: 28.2 us -> 38.9 us
  waiting for transfers between devices: 53.9 us -> 61.2 us
  starting transfers between devices: 92.5 us -> 98.9 us
    dot_general x0 -> x12, matrix products: none -> 15.9 us  [the longest x6 15.1 us: multiply(): jnp.einsum('nquo,nqu->nqo', exchange_blocks, vectors.astype(jnp.bfloat16)...]
    all_to_all x7 -> x6, blocking collectives: 75.6 us -> 61.3 us  [all_sum(): return jnp.sum(lax.all_to_all(copies, axis, 0, 0, tiled=True), 0)]
    all_to_all x6 -> x7, starting transfers between devices: 26.1 us -> 35.1 us  [the longest x6 28.3 us: multiply(): lax.all_to_all(payload, 'row', split_axis=0, concat_axis=0, tiled=True)]
    all_to_all x1, starting transfers between devices: 16.7 us -> 10 us  [multiply(): lax.all_to_all(jnp.concatenate([column_row, far_backward], 1), 'row', spl...]
    all_to_all x6 -> x7, waiting for transfers between devices: 48 us -> 53.9 us  [the longest x6 46.5 us: multiply(): lax.all_to_all(payload, 'row', split_axis=0, concat_axis=0, tiled=True)]
    ppermute x14, starting transfers between devices: 49.6 us -> 53.8 us  [shifted(): lax.ppermute(value, axis, [(source, source + steps) for source in range(l...]
    concatenate x6 -> x0, other arithmetic: 3.89 us -> none  [multiply(): jnp.concatenate([outgoing, far_backward], 1)]
    dot_general x7 -> x1, matrix products: 4.57 us -> 0.68 us  [multiply(): jnp.einsum('nquo,nqu->nqo', distant_local_part, picked(pick_rows, narrow_...]
  transfers between devices with their start and end apart: 21 -> 22, of which waited for: 7 -> 8; matrix products, arithmetic and copies ran while one was open for 8% -> 12% of each run, Pallas kernels for 0% -> 0%
where the time goes in v10:
time: 355 us; the launch traced here: 353 us
  blocking collectives  131 us (37%)
  starting transfers between devices  98.9 us (28%)
  waiting for transfers between devices  61.2 us (17%)
  matrix products  38.9 us (11%)
  other arithmetic  14.5 us (4%)
  local copies, waits for them, and re-layouts  6.45 us (2%)
    all_to_all x4, blocking collectives, lane_totals(): received = lax.all_to_all(copies, axis, 0, 0, tiled=True)  69.8 us
    all_to_all x6, blocking collectives, all_sum(): return jnp.sum(lax.all_to_all(copies, axis, 0, 0, tiled=True), 0)  61.3 us
    ppermute x14, starting transfers between devices, shifted(): lax.ppermute(value, axis, [(source, source + steps) for source in range(l...  53.8 us
    all_to_all x6, waiting for transfers between devices, multiply(): lax.all_to_all(payload, 'row', split_axis=0, concat_axis=0, tiled=True)  46.5 us
    all_to_all x6, starting transfers between devices, multiply(): lax.all_to_all(payload, 'row', split_axis=0, concat_axis=0, tiled=True)  28.3 us
    dot_general x6, matrix products, multiply(): jnp.einsum('nquo,nqu->nqo', exchange_blocks, vectors.astype(jnp.bfloat16)...  15.1 us
    all_to_all x1, starting transfers between devices, multiply(): lax.all_to_all(jnp.concatenate([column_row, far_backward], 1), 'row', spl...  10 us
    dot_general x7, matrix products, multiply(): jnp.einsum('oqht,oqt->oqh', distant_local_part, gathered_values, preferre...  9.82 us
  transfers between devices with their start and end apart: 22, of which 8 were waited for; matrix products, arithmetic and copies ran while one was open for 12% of the time, Pallas kernels for 0%

profile of v10, /device:TPU:1, one launch (start us, length us, event | category | flops | bytes accessed | tf_op | source)
XLA Modules:
  0.0 352.9 jit_solution(6703224615339693645)
XLA Ops:
  0.7 9.0 %collective-permute-start = (bf16[16,128]{1,0:T(8,128)(2,1)S(1)}, bf16[16,128]{1,0:T(8,128)(2,1)S(1)}, u32[]{:S(2)}, u32[]{:S(2)}) collective-permute-start(bf16[16,128]{1,0:T(8,128)(2,1)S(1)} %slice.200), channel_id=1, source_target_pairs={{16,0},{32,16},{48,32},{64,48},{80,64},{96,80},{112,96},{128,112},... | collective-permute-start | bytes 12296 | tf_op jit(solution)/shard_map/ppermute | solution.py:13
  15.6 10.0 %all-to-all-start = ((f32[32,3,128]{2,1,0:T(4,128)}), f32[32,3,128]{2,1,0:T(4,128)S(1)}, u32[]{:S(2)}, u32[]{:S(2)}) async-start(f32[32,3,128]{2,1,0:T(4,128)} %select_maximum_fusion), calls=%async_computation | async-start | bytes 131072 | tf_op jit(solution)/shard_map/all_to_all | solution.py:85
  26.3 3.5 %collective-permute-start.1 = (f32[16,128]{1,0:T(8,128)S(1)}, f32[16,128]{1,0:T(8,128)S(1)}, u32[]{:S(2)}, u32[]{:S(2)}) collective-permute-start(f32[16,128]{1,0:T(8,128)S(1)} %slice.261), channel_id=1, source_target_pairs={{0,16},{16,32},{32,48},{48,64},{64,80},{80,96},{96,112},{112,128},... | collective-permute-start | bytes 24584 | tf_op jit(solution)/shard_map/ppermute | solution.py:13
  31.5 7.1 %all-to-all-done = f32[32,3,128]{2,1,0:T(4,128)S(1)} async-done(((f32[32,3,128]{2,1,0:T(4,128)}), f32[32,3,128]{2,1,0:T(4,128)S(1)}, u32[]{:S(2)}, u32[]{:S(2)}) %all-to-all-start) | async-done | bytes 49184 | tf_op jit(solution)/shard_map/all_to_all | solution.py:85
  39.9 6.8 %all-to-all-start.1 = ((f32[16,32,128]{2,1,0:T(8,128)}), f32[16,32,128]{2,1,0:T(8,128)S(1)}, u32[]{:S(2)}, u32[]{:S(2)}) async-start(f32[16,32,128]{2,1,0:T(8,128)} %broadcast_in_dim.19), calls=%async_computation.1 | async-start | bytes 524288 | tf_op jit(solution)/shard_map/all_to_all | solution.py:19
  46.8 7.4 %all-to-all-done.1 = f32[16,32,128]{2,1,0:T(8,128)S(1)} async-done(((f32[16,32,128]{2,1,0:T(8,128)}), f32[16,32,128]{2,1,0:T(8,128)S(1)}, u32[]{:S(2)}, u32[]{:S(2)}) %all-to-all-start.1) | async-done | bytes 262176 | tf_op jit(solution)/shard_map/all_to_all | solution.py:19
  57.7 7.0 %all-to-all-start.2 = ((f32[32,4,128]{2,1,0:T(4,128)}), f32[32,4,128]{2,1,0:T(4,128)S(1)}, u32[]{:S(2)}, u32[]{:S(2)}) async-start(f32[32,4,128]{2,1,0:T(4,128)} %broadcast_multiply_fusion.5), calls=%async_computation.2 | async-start | bytes 131072 | tf_op jit(solution)/shard_map/all_to_all | solution.py:107
  71.6 6.1 %all-to-all-done.2 = f32[32,4,128]{2,1,0:T(4,128)S(1)} async-done(((f32[32,4,128]{2,1,0:T(4,128)}), f32[32,4,128]{2,1,0:T(4,128)S(1)}, u32[]{:S(2)}, u32[]{:S(2)}) %all-to-all-start.2) | async-done | bytes 65568 | tf_op jit(solution)/shard_map/all_to_all | solution.py:107
  79.3 10.2 %all_to_all.116 = f32[16,32,128]{2,1,0:T(8,128)S(1)} all-to-all(f32[16,32,128]{2,1,0:T(8,128)S(1)} %broadcast_in_dim.21), channel_id=1, replica_groups=mesh['row'=32,'band'=16] {'band'}, dimensions={0} | all-to-all | bytes 524288 | tf_op jit(solution)/shard_map/all_to_all | solution.py:19
  89.7 4.9 %collective-permute-start.4 = (bf16[16,128]{1,0:T(8,128)(2,1)S(1)}, bf16[16,128]{1,0:T(8,128)(2,1)S(1)}, u32[]{:S(2)}, u32[]{:S(2)}) collective-permute-start(bf16[16,128]{1,0:T(8,128)(2,1)S(1)} %slice.270), channel_id=1, source_target_pairs={{16,0},{32,16},{48,32},{64,48},{80,64},{96,80},{112,96},{128,112},... | collective-permute-start | bytes 12296 | tf_op jit(solution)/shard_map/ppermute | solution.py:13
  98.1 5.5 %all-to-all-start.4 = ((f32[32,4,128]{2,1,0:T(4,128)}), f32[32,4,128]{2,1,0:T(4,128)S(1)}, u32[]{:S(2)}, u32[]{:S(2)}) async-start(f32[32,4,128]{2,1,0:T(4,128)} %broadcast_multiply_fusion.4), calls=%async_computation.4 | async-start | bytes 131072 | tf_op jit(solution)/shard_map/all_to_all | solution.py:107
  104.2 3.5 %collective-permute-start.5 = (f32[16,128]{1,0:T(8,128)S(1)}, f32[16,128]{1,0:T(8,128)S(1)}, u32[]{:S(2)}, u32[]{:S(2)}) collective-permute-start(f32[16,128]{1,0:T(8,128)S(1)} %slice.275), channel_id=1, source_target_pairs={{0,16},{16,32},{32,48},{48,64},{64,80},{80,96},{96,112},{112,128},... | collective-permute-start | bytes 24584 | tf_op jit(solution)/shard_map/ppermute | solution.py:13
  108.5 8.1 %all-to-all-done.4 = f32[32,4,128]{2,1,0:T(4,128)S(1)} async-done(((f32[32,4,128]{2,1,0:T(4,128)}), f32[32,4,128]{2,1,0:T(4,128)S(1)}, u32[]{:S(2)}, u32[]{:S(2)}) %all-to-all-start.4) | async-done | bytes 65568 | tf_op jit(solution)/shard_map/all_to_all | solution.py:107
  118.1 10.2 %all_to_all.117 = f32[16,32,128]{2,1,0:T(8,128)S(1)} all-to-all(f32[16,32,128]{2,1,0:T(8,128)S(1)} %broadcast_in_dim.22), channel_id=1, replica_groups=mesh['row'=32,'band'=16] {'band'}, dimensions={0} | all-to-all | bytes 524288 | tf_op jit(solution)/shard_map/all_to_all | solution.py:19
  129.1 17.5 %all_to_all.112 = f32[32,1,4]{2,1,0:T(1,128)S(1)} all-to-all(f32[32,1,4]{2,1,0:T(1,128)S(1)} %bitcast.407), channel_id=1, replica_groups=mesh['row'=32,'band'=16] {'row'}, dimensions={0} | all-to-all | bytes 1024 | tf_op jit(solution)/shard_map/all_to_all | solution.py:24
  154.0 4.1 %all-to-all-start.7 = ((f32[32,4,128]{2,1,0:T(4,128)}), f32[32,4,128]{2,1,0:T(4,128)S(1)}, u32[]{:S(2)}, u32[]{:S(2)}) async-start(f32[32,4,128]{2,1,0:T(4,128)} %broadcast_multiply_fusion.3), calls=%async_computation.7 | async-start | bytes 131072 | tf_op jit(solution)/shard_map/all_to_all | solution.py:107
  158.8 3.5 %collective-permute-start.7 = (f32[16,128]{1,0:T(8,128)S(1)}, f32[16,128]{1,0:T(8,128)S(1)}, u32[]{:S(2)}, u32[]{:S(2)}) collective-permute-start(f32[16,128]{1,0:T(8,128)S(1)} %slice.282), channel_id=1, source_target_pairs={{0,16},{16,32},{32,48},{48,64},{64,80},{80,96},{96,112},{112,128},... | collective-permute-start | bytes 24584 | tf_op jit(solution)/shard_map/ppermute | solution.py:13
  163.1 8.1 %all-to-all-done.7 = f32[32,4,128]{2,1,0:T(4,128)S(1)} async-done(((f32[32,4,128]{2,1,0:T(4,128)}), f32[32,4,128]{2,1,0:T(4,128)S(1)}, u32[]{:S(2)}, u32[]{:S(2)}) %all-to-all-start.7) | async-done | bytes 65568 | tf_op jit(solution)/shard_map/all_to_all | solution.py:107
  172.7 10.2 %all_to_all.118 = f32[16,32,128]{2,1,0:T(8,128)S(1)} all-to-all(f32[16,32,128]{2,1,0:T(8,128)S(1)} %broadcast_in_dim.23), channel_id=1, replica_groups=mesh['row'=32,'band'=16] {'band'}, dimensions={0} | all-to-all | bytes 524288 | tf_op jit(solution)/shard_map/all_to_all | solution.py:19
  184.1 17.5 %all_to_all.113 = f32[32,1,1]{2,1,0:T(1,128)S(1)} all-to-all(f32[32,1,1]{2,1,0:T(1,128)S(1)} %bitcast.409), channel_id=1, replica_groups=mesh['row'=32,'band'=16] {'row'}, dimensions={0} | all-to-all | bytes 256 | tf_op jit(solution)/shard_map/all_to_all | solution.py:24
  209.9 4.1 %all-to-all-start.10 = ((f32[32,4,128]{2,1,0:T(4,128)}), f32[32,4,128]{2,1,0:T(4,128)S(1)}, u32[]{:S(2)}, u32[]{:S(2)}) async-start(f32[32,4,128]{2,1,0:T(4,128)} %broadcast_multiply_fusion.2), calls=%async_computation.10 | async-start | bytes 131072 | tf_op jit(solution)/shard_map/all_to_all | solution.py:107
  218.9 8.1 %all-to-all-done.10 = f32[32,4,128]{2,1,0:T(4,128)S(1)} async-done(((f32[32,4,128]{2,1,0:T(4,128)}), f32[32,4,128]{2,1,0:T(4,128)S(1)}, u32[]{:S(2)}, u32[]{:S(2)}) %all-to-all-start.10) | async-done | bytes 65568 | tf_op jit(solution)/shard_map/all_to_all | solution.py:107
  228.6 10.2 %all_to_all.119 = f32[16,32,128]{2,1,0:T(8,128)S(1)} all-to-all(f32[16,32,128]{2,1,0:T(8,128)S(1)} %broadcast_in_dim.24), channel_id=1, replica_groups=mesh['row'=32,'band'=16] {'band'}, dimensions={0} | all-to-all | bytes 524288 | tf_op jit(solution)/shard_map/all_to_all | solution.py:19
  239.5 4.9 %collective-permute-start.10 = (bf16[16,128]{1,0:T(8,128)(2,1)S(1)}, bf16[16,128]{1,0:T(8,128)(2,1)S(1)}, u32[]{:S(2)}, u32[]{:S(2)}) collective-permute-start(bf16[16,128]{1,0:T(8,128)(2,1)S(1)} %slice.291), channel_id=1, source_target_pairs={{16,0},{32,16},{48,32},{64,48},{80,64},{96,80},{112,96},{128,112},... | collective-permute-start | bytes 12296 | tf_op jit(solution)/shard_map/ppermute | solution.py:13
  248.0 3.6 %all-to-all-start.12 = ((f32[32,4,128]{2,1,0:T(4,128)}), f32[32,4,128]{2,1,0:T(4,128)S(1)}, u32[]{:S(2)}, u32[]{:S(2)}) async-start(f32[32,4,128]{2,1,0:T(4,128)} %broadcast_multiply_fusion.1), calls=%async_computation.12 | async-start | bytes 131072 | tf_op jit(solution)/shard_map/all_to_all | solution.py:107
  256.2 8.1 %all-to-all-done.12 = f32[32,4,128]{2,1,0:T(4,128)S(1)} async-done(((f32[32,4,128]{2,1,0:T(4,128)}), f32[32,4,128]{2,1,0:T(4,128)S(1)}, u32[]{:S(2)}, u32[]{:S(2)}) %all-to-all-start.12) | async-done | bytes 65568 | tf_op jit(solution)/shard_map/all_to_all | solution.py:107
  265.9 10.3 %all_to_all.120 = f32[16,32,128]{2,1,0:T(8,128)S(1)} all-to-all(f32[16,32,128]{2,1,0:T(8,128)S(1)} %broadcast_in_dim.25), channel_id=1, replica_groups=mesh['row'=32,'band'=16] {'band'}, dimensions={0} | all-to-all | bytes 524288 | tf_op jit(solution)/shard_map/all_to_all | solution.py:19
  279.5 17.3 %all_to_all.114 = f32[32,1,4]{2,1,0:T(1,128)S(1)} all-to-all(f32[32,1,4]{2,1,0:T(1,128)S(1)} %bitcast.408), channel_id=1, replica_groups=mesh['row'=32,'band'=16] {'row'}, dimensions={0} | all-to-all | bytes 1024 | tf_op jit(solution)/shard_map/all_to_all | solution.py:24
  304.7 4.1 %all-to-all-start.15 = ((f32[32,4,128]{2,1,0:T(4,128)}), f32[32,4,128]{2,1,0:T(4,128)S(1)}, u32[]{:S(2)}, u32[]{:S(2)}) async-start(f32[32,4,128]{2,1,0:T(4,128)} %broadcast_multiply_fusion), calls=%async_computation.15 | async-start | bytes 131072 | tf_op jit(solution)/shard_map/all_to_all | solution.py:107
  313.8 8.0 %all-to-all-done.15 = f32[32,4,128]{2,1,0:T(4,128)S(1)} async-done(((f32[32,4,128]{2,1,0:T(4,128)}), f32[32,4,128]{2,1,0:T(4,128)S(1)}, u32[]{:S(2)}, u32[]{:S(2)}) %all-to-all-start.15) | async-done | bytes 65568 | tf_op jit(solution)/shard_map/all_to_all | solution.py:107
  323.4 10.2 %all_to_all.121 = f32[16,32,128]{2,1,0:T(8,128)S(1)} all-to-all(f32[16,32,128]{2,1,0:T(8,128)S(1)} %broadcast_in_dim.26), channel_id=1, replica_groups=mesh['row'=32,'band'=16] {'band'}, dimensions={0} | all-to-all | bytes 524288 | tf_op jit(solution)/shard_map/all_to_all | solution.py:19
  334.3 17.5 %all_to_all.115 = f32[32,1,1]{2,1,0:T(1,128)S(1)} all-to-all(f32[32,1,1]{2,1,0:T(1,128)S(1)} %bitcast.410), channel_id=1, replica_groups=mesh['row'=32,'band'=16] {'row'}, dimensions={0} | all-to-all | bytes 256 | tf_op jit(solution)/shard_map/all_to_all | solution.py:24
  (264 shorter events, 84.3 us)
Async XLA Ops:
  0.6 25.0 %copy-start = (bf16[32,1,128,128]{3,2,1,0:T(8,128)(2,1)S(1)}, bf16[32,1,128,128]{3,2,1,0:T(8,128)(2,1)}, u32[]{:S(2)}) copy-start(bf16[32,1,128,128]{3,2,1,0:T(8,128)(2,1)} %param.7) | copy-start | bytes 3145732
  0.7 30.2 %collective-permute-start = (bf16[16,128]{1,0:T(8,128)(2,1)S(1)}, bf16[16,128]{1,0:T(8,128)(2,1)S(1)}, u32[]{:S(2)}, u32[]{:S(2)}) collective-permute-start(bf16[16,128]{1,0:T(8,128)(2,1)S(1)} %slice.200), channel_id=1, source_target_pairs={{16,0},{32,16},{48,32},{64,48},{80,64},{96,80},{112,96},{128,112},... | collective-permute-start | bytes 12296 | tf_op jit(solution)/shard_map/ppermute | solution.py:13
  15.6 23.0 %all-to-all-start = ((f32[32,3,128]{2,1,0:T(4,128)}), f32[32,3,128]{2,1,0:T(4,128)S(1)}, u32[]{:S(2)}, u32[]{:S(2)}) async-start(f32[32,3,128]{2,1,0:T(4,128)} %select_maximum_fusion), calls=%async_computation | async-start | bytes 131072 | tf_op jit(solution)/shard_map/all_to_all | solution.py:85
  26.0 188.3 %copy-start.11 = (f32[32]{0:T(128)}, f32[32]{0:T(128)S(1)}, u32[]{:S(2)}) copy-start(f32[32]{0:T(128)S(1)} %compare_select_fusion) | copy-start | bytes 388
  26.3 12.8 %collective-permute-start.1 = (f32[16,128]{1,0:T(8,128)S(1)}, f32[16,128]{1,0:T(8,128)S(1)}, u32[]{:S(2)}, u32[]{:S(2)}) collective-permute-start(f32[16,128]{1,0:T(8,128)S(1)} %slice.261), channel_id=1, source_target_pairs={{0,16},{16,32},{32,48},{48,64},{64,80},{80,96},{96,112},{112,128},... | collective-permute-start | bytes 24584 | tf_op jit(solution)/shard_map/ppermute | solution.py:13
  30.7 197.6 %copy-start.14 = (f32[32]{0:T(128)}, f32[32]{0:T(128)S(1)}, u32[]{:S(2)}) copy-start(f32[32]{0:T(128)S(1)} %compare_convert_fusion) | copy-start | bytes 388
  38.9 189.5 %copy-start.3 = (pred[128,32]{0,1:T(32,128)(4,1)}, pred[128,32]{0,1:T(32,128)(4,1)S(1)}, u32[]{:S(2)}) copy-start(pred[128,32]{0,1:T(32,128)(4,1)S(1)} %pad_add_fusion.1) | copy-start | bytes 12292
  39.9 14.3 %all-to-all-start.1 = ((f32[16,32,128]{2,1,0:T(8,128)}), f32[16,32,128]{2,1,0:T(8,128)S(1)}, u32[]{:S(2)}, u32[]{:S(2)}) async-start(f32[16,32,128]{2,1,0:T(8,128)} %broadcast_in_dim.19), calls=%async_computation.1 | async-start | bytes 524288 | tf_op jit(solution)/shard_map/all_to_all | solution.py:19
  57.7 20.0 %all-to-all-start.2 = ((f32[32,4,128]{2,1,0:T(4,128)}), f32[32,4,128]{2,1,0:T(4,128)S(1)}, u32[]{:S(2)}, u32[]{:S(2)}) async-start(f32[32,4,128]{2,1,0:T(4,128)} %broadcast_multiply_fusion.5), calls=%async_computation.2 | async-start | bytes 131072 | tf_op jit(solution)/shard_map/all_to_all | solution.py:107
  64.7 6.3 %collective-permute-start.2 = (bf16[16,128]{1,0:T(8,128)(2,1)S(1)}, bf16[16,128]{1,0:T(8,128)(2,1)S(1)}, u32[]{:S(2)}, u32[]{:S(2)}) collective-permute-start(bf16[16,128]{1,0:T(8,128)(2,1)S(1)} %slice.263), channel_id=1, source_target_pairs={{16,0},{32,16},{48,32},{64,48},{80,64},{96,80},{112,96},{128,112},... | collective-permute-start | bytes 12296 | tf_op jit(solution)/shard_map/ppermute | solution.py:13
  67.5 11.7 %collective-permute-start.3 = (f32[16,128]{1,0:T(8,128)S(1)}, f32[16,128]{1,0:T(8,128)S(1)}, u32[]{:S(2)}, u32[]{:S(2)}) collective-permute-start(f32[16,128]{1,0:T(8,128)S(1)} %slice.268), channel_id=1, source_target_pairs={{0,16},{16,32},{32,48},{48,64},{64,80},{80,96},{96,112},{112,128},... | collective-permute-start | bytes 24584 | tf_op jit(solution)/shard_map/ppermute | solution.py:13
  89.5 38.9 %copy-start.7 = (f32[32,128]{1,0:T(8,128)}, f32[32,128]{1,0:T(8,128)S(1)}, u32[]{:S(2)}) copy-start(f32[32,128]{1,0:T(8,128)S(1)} %get-tuple-element.51) | copy-start | bytes 49156
  89.7 18.1 %collective-permute-start.4 = (bf16[16,128]{1,0:T(8,128)(2,1)S(1)}, bf16[16,128]{1,0:T(8,128)(2,1)S(1)}, u32[]{:S(2)}, u32[]{:S(2)}) collective-permute-start(bf16[16,128]{1,0:T(8,128)(2,1)S(1)} %slice.270), channel_id=1, source_target_pairs={{16,0},{32,16},{48,32},{64,48},{80,64},{96,80},{112,96},{128,112},... | collective-permute-start | bytes 12296 | tf_op jit(solution)/shard_map/ppermute | solution.py:13
  98.1 18.5 %all-to-all-start.4 = ((f32[32,4,128]{2,1,0:T(4,128)}), f32[32,4,128]{2,1,0:T(4,128)S(1)}, u32[]{:S(2)}, u32[]{:S(2)}) async-start(f32[32,4,128]{2,1,0:T(4,128)} %broadcast_multiply_fusion.4), calls=%async_computation.4 | async-start | bytes 131072 | tf_op jit(solution)/shard_map/all_to_all | solution.py:107
  104.2 13.8 %collective-permute-start.5 = (f32[16,128]{1,0:T(8,128)S(1)}, f32[16,128]{1,0:T(8,128)S(1)}, u32[]{:S(2)}, u32[]{:S(2)}) collective-permute-start(f32[16,128]{1,0:T(8,128)S(1)} %slice.275), channel_id=1, source_target_pairs={{0,16},{16,32},{32,48},{48,64},{64,80},{80,96},{96,112},{112,128},... | collective-permute-start | bytes 24584 | tf_op jit(solution)/shard_map/ppermute | solution.py:13
  128.5 24.8 %copy-start.8 = (f32[1,4096]{1,0:T(1,128)}, f32[1,4096]{1,0:T(1,128)S(1)}, u32[]{:S(2)}) copy-start(f32[1,4096]{1,0:T(1,128)S(1)} %get-tuple-element.29) | copy-start | bytes 49156
  147.3 55.4 %copy-start.17 = (f32[128]{0:T(128)}, f32[128]{0:T(128)S(1)}, u32[]{:S(2)}) copy-start(f32[128]{0:T(128)S(1)} %get-tuple-element.25) | copy-start | bytes 1540
  147.5 14.8 %collective-permute-start.6 = (bf16[16,128]{1,0:T(8,128)(2,1)S(1)}, bf16[16,128]{1,0:T(8,128)(2,1)S(1)}, u32[]{:S(2)}, u32[]{:S(2)}) collective-permute-start(bf16[16,128]{1,0:T(8,128)(2,1)S(1)} %slice.277), channel_id=1, source_target_pairs={{16,0},{32,16},{48,32},{64,48},{80,64},{96,80},{112,96},{128,112},... | collective-permute-start | bytes 12296 | tf_op jit(solution)/shard_map/ppermute | solution.py:13
  154.0 17.1 %all-to-all-start.7 = ((f32[32,4,128]{2,1,0:T(4,128)}), f32[32,4,128]{2,1,0:T(4,128)S(1)}, u32[]{:S(2)}, u32[]{:S(2)}) async-start(f32[32,4,128]{2,1,0:T(4,128)} %broadcast_multiply_fusion.3), calls=%async_computation.7 | async-start | bytes 131072 | tf_op jit(solution)/shard_map/all_to_all | solution.py:107
  158.8 13.8 %collective-permute-start.7 = (f32[16,128]{1,0:T(8,128)S(1)}, f32[16,128]{1,0:T(8,128)S(1)}, u32[]{:S(2)}, u32[]{:S(2)}) collective-permute-start(f32[16,128]{1,0:T(8,128)S(1)} %slice.282), channel_id=1, source_target_pairs={{0,16},{16,32},{32,48},{48,64},{64,80},{80,96},{96,112},{112,128},... | collective-permute-start | bytes 24584 | tf_op jit(solution)/shard_map/ppermute | solution.py:13
  203.6 14.6 %collective-permute-start.8 = (bf16[16,128]{1,0:T(8,128)(2,1)S(1)}, bf16[16,128]{1,0:T(8,128)(2,1)S(1)}, u32[]{:S(2)}, u32[]{:S(2)}) collective-permute-start(bf16[16,128]{1,0:T(8,128)(2,1)S(1)} %slice.284), channel_id=1, source_target_pairs={{16,0},{32,16},{48,32},{64,48},{80,64},{96,80},{112,96},{128,112},... | collective-permute-start | bytes 12296 | tf_op jit(solution)/shard_map/ppermute | solution.py:13
  209.9 17.1 %all-to-all-start.10 = ((f32[32,4,128]{2,1,0:T(4,128)}), f32[32,4,128]{2,1,0:T(4,128)S(1)}, u32[]{:S(2)}, u32[]{:S(2)}) async-start(f32[32,4,128]{2,1,0:T(4,128)} %broadcast_multiply_fusion.2), calls=%async_computation.10 | async-start | bytes 131072 | tf_op jit(solution)/shard_map/all_to_all | solution.py:107
  214.6 13.9 %collective-permute-start.9 = (f32[16,128]{1,0:T(8,128)S(1)}, f32[16,128]{1,0:T(8,128)S(1)}, u32[]{:S(2)}, u32[]{:S(2)}) collective-permute-start(f32[16,128]{1,0:T(8,128)S(1)} %slice.289), channel_id=1, source_target_pairs={{0,16},{16,32},{32,48},{48,64},{64,80},{80,96},{96,112},{112,128},... | collective-permute-start | bytes 24584 | tf_op jit(solution)/shard_map/ppermute | solution.py:13
  239.5 15.9 %collective-permute-start.10 = (bf16[16,128]{1,0:T(8,128)(2,1)S(1)}, bf16[16,128]{1,0:T(8,128)(2,1)S(1)}, u32[]{:S(2)}, u32[]{:S(2)}) collective-permute-start(bf16[16,128]{1,0:T(8,128)(2,1)S(1)} %slice.291), channel_id=1, source_target_pairs={{16,0},{32,16},{48,32},{64,48},{80,64},{96,80},{112,96},{128,112},... | collective-permute-start | bytes 12296 | tf_op jit(solution)/shard_map/ppermute | solution.py:13
  248.0 16.3 %all-to-all-start.12 = ((f32[32,4,128]{2,1,0:T(4,128)}), f32[32,4,128]{2,1,0:T(4,128)S(1)}, u32[]{:S(2)}, u32[]{:S(2)}) async-start(f32[32,4,128]{2,1,0:T(4,128)} %broadcast_multiply_fusion.1), calls=%async_computation.12 | async-start | bytes 131072 | tf_op jit(solution)/shard_map/all_to_all | solution.py:107
  252.3 13.5 %collective-permute-start.11 = (f32[16,128]{1,0:T(8,128)S(1)}, f32[16,128]{1,0:T(8,128)S(1)}, u32[]{:S(2)}, u32[]{:S(2)}) collective-permute-start(f32[16,128]{1,0:T(8,128)S(1)} %slice.296), channel_id=1, source_target_pairs={{0,16},{16,32},{32,48},{48,64},{64,80},{80,96},{96,112},{112,128},... | collective-permute-start | bytes 24584 | tf_op jit(solution)/shard_map/ppermute | solution.py:13
  298.4 14.7 %collective-permute-start.12 = (bf16[16,128]{1,0:T(8,128)(2,1)S(1)}, bf16[16,128]{1,0:T(8,128)(2,1)S(1)}, u32[]{:S(2)}, u32[]{:S(2)}) collective-permute-start(bf16[16,128]{1,0:T(8,128)(2,1)S(1)} %slice.298), channel_id=1, source_target_pairs={{16,0},{32,16},{48,32},{64,48},{80,64},{96,80},{112,96},{128,112},... | collective-permute-start | bytes 12296 | tf_op jit(solution)/shard_map/ppermute | solution.py:13
  304.7 17.1 %all-to-all-start.15 = ((f32[32,4,128]{2,1,0:T(4,128)}), f32[32,4,128]{2,1,0:T(4,128)S(1)}, u32[]{:S(2)}, u32[]{:S(2)}) async-start(f32[32,4,128]{2,1,0:T(4,128)} %broadcast_multiply_fusion), calls=%async_computation.15 | async-start | bytes 131072 | tf_op jit(solution)/shard_map/all_to_all | solution.py:107
  309.5 13.8 %collective-permute-start.13 = (f32[16,128]{1,0:T(8,128)S(1)}, f32[16,128]{1,0:T(8,128)S(1)}, u32[]{:S(2)}, u32[]{:S(2)}) collective-permute-start(f32[16,128]{1,0:T(8,128)S(1)} %slice.303), channel_id=1, source_target_pairs={{0,16},{16,32},{32,48},{48,64},{64,80},{80,96},{96,112},{112,128},... | collective-permute-start | bytes 24584 | tf_op jit(solution)/shard_map/ppermute | solution.py:13
  313.1 20.5 %copy-start.18 = (f32[128]{0:T(128)S(1)}, f32[128]{0:T(128)}, u32[]{:S(2)}) copy-start(f32[128]{0:T(128)} %copy-done.17) | copy-start | bytes 1540
  313.8 38.3 %copy-start.26 = (f32[1,128]{1,0:T(1,128)S(1)}, f32[1,128]{1,0:T(1,128)}, u32[]{:S(2)}) copy-start(f32[1,128]{1,0:T(1,128)} %get-tuple-element.15) | copy-start | bytes 1540
  313.8 38.5 %copy-start.6 = (f32[32,128]{1,0:T(8,128)S(1)}, f32[32,128]{1,0:T(8,128)}, u32[]{:S(2)}) copy-start(f32[32,128]{1,0:T(8,128)} %get-tuple-element.22) | copy-start | bytes 49156
  (17 other events, 221.8 us)

commit v11 on v9

--- a/solution.py
+++ b/solution.py
@@ -22,7 +22,7 @@
 def lane_totals(copies, axis, lanes):
     count = lax.axis_size(axis)
     received = lax.all_to_all(copies, axis, 0, 0, tiled=True)
-    return jnp.dot(received.T, jnp.ones((count, lanes), jnp.float32), precision=lax.Precision.HIGHEST)
+    return jnp.dot(received.T, jnp.ones((count, lanes), jnp.float32), precision=lax.Precision.HIGH)
 
 
 def on_device(band_blocks, distant_block_slots, far_rows, far_columns, far_counts):
@@ -106,7 +106,7 @@
             [far_forward.reshape(-1, block_size), returned.reshape(-1, block_size)], 0
         )
         summed = forward + spread[:rows_dev]
-        summed = summed + jnp.dot(selection.T, far_parts, precision=lax.Precision.HIGHEST)
+        summed = summed + jnp.dot(selection.T, far_parts, precision=lax.Precision.HIGH)
         carried = shifted(spread[rows_dev:], "row", 1)
         summed = jnp.concatenate([summed[:band_count] + carried, summed[band_count:]], 0)
         return all_sum(summed, "band"), wanted
@@ -132,7 +132,7 @@
                 parts.append(curved * curved / balance)
             stacked = jnp.stack(parts).reshape(len(parts), -1)
             copies = jnp.dot(
-                jnp.ones((row_count, stacked.shape[1]), jnp.float32), stacked.T, precision=lax.Precision.HIGHEST
+                jnp.ones((row_count, stacked.shape[1]), jnp.float32), stacked.T, precision=lax.Precision.HIGH
             )
             totals = lane_totals(copies, "row", block_size)
             curvature = totals[0]

time: 339 us -> 338 us (level)
  no operation moved by 1% of the time
where the time goes in v11:
time: 338 us; the launch traced here: 336 us
  blocking collectives  145 us (43%)
  starting transfers between devices  92.2 us (27%)
  waiting for transfers between devices  54.3 us (16%)
  matrix products  27.1 us (8%)
  other arithmetic  11 us (3%)
  local copies, waits for them, and re-layouts  4.14 us (1%)
    all_to_all x7, blocking collectives, all_sum(): return jnp.sum(lax.all_to_all(copies, axis, 0, 0, tiled=True), 0)  75.6 us
    all_to_all x4, blocking collectives, lane_totals(): received = lax.all_to_all(copies, axis, 0, 0, tiled=True)  69.9 us
    ppermute x14, starting transfers between devices, shifted(): lax.ppermute(value, axis, [(source, source + steps) for source in range(l...  49.4 us
    all_to_all x6, waiting for transfers between devices, multiply(): lax.all_to_all(jnp.concatenate([outgoing, far_backward], 1), 'row', split...  48.2 us
    all_to_all x6, starting transfers between devices, multiply(): lax.all_to_all(jnp.concatenate([outgoing, far_backward], 1), 'row', split...  26 us
    all_to_all x1, starting transfers between devices, multiply(): lax.all_to_all(jnp.concatenate([column_row, far_backward], 1), 'row', spl...  16.7 us
    dot_general x7, matrix products, multiply(): jnp.einsum('oqht,oqt->oqh', distant_local_part, gathered_values, preferre...  8.23 us
  transfers between devices with their start and end apart: 21, of which 7 were waited for; matrix products, arithmetic and copies ran while one was open for 8% of the time, Pallas kernels for 0%

profile of v11, /device:TPU:1, one launch (start us, length us, event | category | flops | bytes accessed | tf_op | source)
XLA Modules:
  0.0 336.1 jit_solution(16762682111633329983)
XLA Ops:
  5.1 16.7 %all-to-all-start = ((f32[32,3,128]{2,1,0:T(4,128)}), f32[32,3,128]{2,1,0:T(4,128)S(1)}, u32[]{:S(2)}, u32[]{:S(2)}) async-start(f32[32,3,128]{2,1,0:T(4,128)} %select_maximum_fusion), calls=%async_computation | async-start | bytes 131072 | tf_op jit(solution)/shard_map/all_to_all | solution.py:80
  29.1 5.8 %all-to-all-done = f32[32,3,128]{2,1,0:T(4,128)S(1)} async-done(((f32[32,3,128]{2,1,0:T(4,128)}), f32[32,3,128]{2,1,0:T(4,128)S(1)}, u32[]{:S(2)}, u32[]{:S(2)}) %all-to-all-start) | async-done | bytes 49184 | tf_op jit(solution)/shard_map/all_to_all | solution.py:80
  35.4 14.1 %all_to_all.116 = f32[16,32,128]{2,1,0:T(8,128)S(1)} all-to-all(f32[16,32,128]{2,1,0:T(8,128)S(1)} %broadcast_in_dim.17), channel_id=1, replica_groups=mesh['row'=32,'band'=16] {'band'}, dimensions={0} | all-to-all | bytes 524288 | tf_op jit(solution)/shard_map/all_to_all | solution.py:19
  50.0 4.9 %collective-permute-start.2 = (bf16[16,128]{1,0:T(8,128)(2,1)S(1)}, bf16[16,128]{1,0:T(8,128)(2,1)S(1)}, u32[]{:S(2)}, u32[]{:S(2)}) collective-permute-start(bf16[16,128]{1,0:T(8,128)(2,1)S(1)} %slice.263), channel_id=1, source_target_pairs={{16,0},{32,16},{48,32},{64,48},{80,64},{96,80},{112,96},{128,112},... | collective-permute-start | bytes 12296 | tf_op jit(solution)/shard_map/ppermute | solution.py:13
  56.3 6.5 %all-to-all-start.2 = ((f32[32,4,128]{2,1,0:T(4,128)}), f32[32,4,128]{2,1,0:T(4,128)S(1)}, u32[]{:S(2)}, u32[]{:S(2)}) async-start(f32[32,4,128]{2,1,0:T(4,128)} %pad_maximum_fusion), calls=%async_computation.2 | async-start | bytes 131072 | tf_op jit(solution)/shard_map/all_to_all | solution.py:89
  63.5 3.5 %collective-permute-start.3 = (f32[16,128]{1,0:T(8,128)S(1)}, f32[16,128]{1,0:T(8,128)S(1)}, u32[]{:S(2)}, u32[]{:S(2)}) collective-permute-start(f32[16,128]{1,0:T(8,128)S(1)} %slice.268), channel_id=1, source_target_pairs={{0,16},{16,32},{32,48},{48,64},{64,80},{80,96},{96,112},{112,128},... | collective-permute-start | bytes 24584 | tf_op jit(solution)/shard_map/ppermute | solution.py:13
  67.7 8.1 %all-to-all-done.2 = f32[32,4,128]{2,1,0:T(4,128)S(1)} async-done(((f32[32,4,128]{2,1,0:T(4,128)}), f32[32,4,128]{2,1,0:T(4,128)S(1)}, u32[]{:S(2)}, u32[]{:S(2)}) %all-to-all-start.2) | async-done | bytes 65568 | tf_op jit(solution)/shard_map/all_to_all | solution.py:89
  77.4 10.3 %all_to_all.117 = f32[16,32,128]{2,1,0:T(8,128)S(1)} all-to-all(f32[16,32,128]{2,1,0:T(8,128)S(1)} %broadcast_in_dim.18), channel_id=1, replica_groups=mesh['row'=32,'band'=16] {'band'}, dimensions={0} | all-to-all | bytes 524288 | tf_op jit(solution)/shard_map/all_to_all | solution.py:19
  88.1 4.6 %collective-permute-start.4 = (bf16[16,128]{1,0:T(8,128)(2,1)S(1)}, bf16[16,128]{1,0:T(8,128)(2,1)S(1)}, u32[]{:S(2)}, u32[]{:S(2)}) collective-permute-start(bf16[16,128]{1,0:T(8,128)(2,1)S(1)} %slice.270), channel_id=1, source_target_pairs={{16,0},{32,16},{48,32},{64,48},{80,64},{96,80},{112,96},{128,112},... | collective-permute-start | bytes 12296 | tf_op jit(solution)/shard_map/ppermute | solution.py:13
  94.1 3.6 %all-to-all-start.4 = ((f32[32,4,128]{2,1,0:T(4,128)}), f32[32,4,128]{2,1,0:T(4,128)S(1)}, u32[]{:S(2)}, u32[]{:S(2)}) async-start(f32[32,4,128]{2,1,0:T(4,128)} %pad_maximum_fusion.1), calls=%async_computation.4 | async-start | bytes 131072 | tf_op jit(solution)/shard_map/all_to_all | solution.py:89
  102.7 8.1 %all-to-all-done.4 = f32[32,4,128]{2,1,0:T(4,128)S(1)} async-done(((f32[32,4,128]{2,1,0:T(4,128)}), f32[32,4,128]{2,1,0:T(4,128)S(1)}, u32[]{:S(2)}, u32[]{:S(2)}) %all-to-all-start.4) | async-done | bytes 65568 | tf_op jit(solution)/shard_map/all_to_all | solution.py:89
  112.3 10.3 %all_to_all.118 = f32[16,32,128]{2,1,0:T(8,128)S(1)} all-to-all(f32[16,32,128]{2,1,0:T(8,128)S(1)} %broadcast_in_dim.19), channel_id=1, replica_groups=mesh['row'=32,'band'=16] {'band'}, dimensions={0} | all-to-all | bytes 524288 | tf_op jit(solution)/shard_map/all_to_all | solution.py:19
  123.1 17.5 %all_to_all.112 = f32[32,1,4]{2,1,0:T(1,128)S(1)} all-to-all(f32[32,1,4]{2,1,0:T(1,128)S(1)} %bitcast.434), channel_id=1, replica_groups=mesh['row'=32,'band'=16] {'row'}, dimensions={0} | all-to-all | bytes 1024 | tf_op jit(solution)/shard_map/all_to_all | solution.py:24
  146.0 4.1 %all-to-all-start.7 = ((f32[32,4,128]{2,1,0:T(4,128)}), f32[32,4,128]{2,1,0:T(4,128)S(1)}, u32[]{:S(2)}, u32[]{:S(2)}) async-start(f32[32,4,128]{2,1,0:T(4,128)} %pad_maximum_fusion.4), calls=%async_computation.7 | async-start | bytes 131072 | tf_op jit(solution)/shard_map/all_to_all | solution.py:89
  150.8 3.7 %collective-permute-start.7 = (f32[16,128]{1,0:T(8,128)S(1)}, f32[16,128]{1,0:T(8,128)S(1)}, u32[]{:S(2)}, u32[]{:S(2)}) collective-permute-start(f32[16,128]{1,0:T(8,128)S(1)} %slice.282), channel_id=1, source_target_pairs={{0,16},{16,32},{32,48},{48,64},{64,80},{80,96},{96,112},{112,128},... | collective-permute-start | bytes 24584 | tf_op jit(solution)/shard_map/ppermute | solution.py:13
  155.2 7.9 %all-to-all-done.7 = f32[32,4,128]{2,1,0:T(4,128)S(1)} async-done(((f32[32,4,128]{2,1,0:T(4,128)}), f32[32,4,128]{2,1,0:T(4,128)S(1)}, u32[]{:S(2)}, u32[]{:S(2)}) %all-to-all-start.7) | async-done | bytes 65568 | tf_op jit(solution)/shard_map/all_to_all | solution.py:89
  164.7 10.2 %all_to_all.119 = f32[16,32,128]{2,1,0:T(8,128)S(1)} all-to-all(f32[16,32,128]{2,1,0:T(8,128)S(1)} %broadcast_in_dim.20), channel_id=1, replica_groups=mesh['row'=32,'band'=16] {'band'}, dimensions={0} | all-to-all | bytes 524288 | tf_op jit(solution)/shard_map/all_to_all | solution.py:19
  175.3 17.5 %all_to_all.113 = f32[32,1,1]{2,1,0:T(1,128)S(1)} all-to-all(f32[32,1,1]{2,1,0:T(1,128)S(1)} %bitcast.436), channel_id=1, replica_groups=mesh['row'=32,'band'=16] {'row'}, dimensions={0} | all-to-all | bytes 256 | tf_op jit(solution)/shard_map/all_to_all | solution.py:24
  197.9 4.1 %all-to-all-start.10 = ((f32[32,4,128]{2,1,0:T(4,128)}), f32[32,4,128]{2,1,0:T(4,128)S(1)}, u32[]{:S(2)}, u32[]{:S(2)}) async-start(f32[32,4,128]{2,1,0:T(4,128)} %pad_maximum_fusion.5), calls=%async_computation.10 | async-start | bytes 131072 | tf_op jit(solution)/shard_map/all_to_all | solution.py:89
  202.7 3.5 %collective-permute-start.9 = (f32[16,128]{1,0:T(8,128)S(1)}, f32[16,128]{1,0:T(8,128)S(1)}, u32[]{:S(2)}, u32[]{:S(2)}) collective-permute-start(f32[16,128]{1,0:T(8,128)S(1)} %slice.289), channel_id=1, source_target_pairs={{0,16},{16,32},{32,48},{48,64},{64,80},{80,96},{96,112},{112,128},... | collective-permute-start | bytes 24584 | tf_op jit(solution)/shard_map/ppermute | solution.py:13
  206.9 8.1 %all-to-all-done.10 = f32[32,4,128]{2,1,0:T(4,128)S(1)} async-done(((f32[32,4,128]{2,1,0:T(4,128)}), f32[32,4,128]{2,1,0:T(4,128)S(1)}, u32[]{:S(2)}, u32[]{:S(2)}) %all-to-all-start.10) | async-done | bytes 65568 | tf_op jit(solution)/shard_map/all_to_all | solution.py:89
  216.6 10.2 %all_to_all.120 = f32[16,32,128]{2,1,0:T(8,128)S(1)} all-to-all(f32[16,32,128]{2,1,0:T(8,128)S(1)} %broadcast_in_dim.21), channel_id=1, replica_groups=mesh['row'=32,'band'=16] {'band'}, dimensions={0} | all-to-all | bytes 524288 | tf_op jit(solution)/shard_map/all_to_all | solution.py:19
  227.2 4.9 %collective-permute-start.10 = (bf16[16,128]{1,0:T(8,128)(2,1)S(1)}, bf16[16,128]{1,0:T(8,128)(2,1)S(1)}, u32[]{:S(2)}, u32[]{:S(2)}) collective-permute-start(bf16[16,128]{1,0:T(8,128)(2,1)S(1)} %slice.291), channel_id=1, source_target_pairs={{16,0},{32,16},{48,32},{64,48},{80,64},{96,80},{112,96},{128,112},... | collective-permute-start | bytes 12296 | tf_op jit(solution)/shard_map/ppermute | solution.py:13
  233.5 3.6 %all-to-all-start.12 = ((f32[32,4,128]{2,1,0:T(4,128)}), f32[32,4,128]{2,1,0:T(4,128)S(1)}, u32[]{:S(2)}, u32[]{:S(2)}) async-start(f32[32,4,128]{2,1,0:T(4,128)} %pad_maximum_fusion.6), calls=%async_computation.12 | async-start | bytes 131072 | tf_op jit(solution)/shard_map/all_to_all | solution.py:89
  241.7 8.0 %all-to-all-done.12 = f32[32,4,128]{2,1,0:T(4,128)S(1)} async-done(((f32[32,4,128]{2,1,0:T(4,128)}), f32[32,4,128]{2,1,0:T(4,128)S(1)}, u32[]{:S(2)}, u32[]{:S(2)}) %all-to-all-start.12) | async-done | bytes 65568 | tf_op jit(solution)/shard_map/all_to_all | solution.py:89
  251.3 10.4 %all_to_all.121 = f32[16,32,128]{2,1,0:T(8,128)S(1)} all-to-all(f32[16,32,128]{2,1,0:T(8,128)S(1)} %broadcast_in_dim.22), channel_id=1, replica_groups=mesh['row'=32,'band'=16] {'band'}, dimensions={0} | all-to-all | bytes 524288 | tf_op jit(solution)/shard_map/all_to_all | solution.py:19
  264.8 17.3 %all_to_all.114 = f32[32,1,4]{2,1,0:T(1,128)S(1)} all-to-all(f32[32,1,4]{2,1,0:T(1,128)S(1)} %bitcast.435), channel_id=1, replica_groups=mesh['row'=32,'band'=16] {'row'}, dimensions={0} | all-to-all | bytes 1024 | tf_op jit(solution)/shard_map/all_to_all | solution.py:24
  288.2 4.1 %all-to-all-start.15 = ((f32[32,4,128]{2,1,0:T(4,128)}), f32[32,4,128]{2,1,0:T(4,128)S(1)}, u32[]{:S(2)}, u32[]{:S(2)}) async-start(f32[32,4,128]{2,1,0:T(4,128)} %pad_maximum_fusion.9), calls=%async_computation.15 | async-start | bytes 131072 | tf_op jit(solution)/shard_map/all_to_all | solution.py:89
  292.9 3.5 %collective-permute-start.13 = (f32[16,128]{1,0:T(8,128)S(1)}, f32[16,128]{1,0:T(8,128)S(1)}, u32[]{:S(2)}, u32[]{:S(2)}) collective-permute-start(f32[16,128]{1,0:T(8,128)S(1)} %slice.303), channel_id=1, source_target_pairs={{0,16},{16,32},{32,48},{48,64},{64,80},{80,96},{96,112},{112,128},... | collective-permute-start | bytes 24584 | tf_op jit(solution)/shard_map/ppermute | solution.py:13
  297.2 8.1 %all-to-all-done.15 = f32[32,4,128]{2,1,0:T(4,128)S(1)} async-done(((f32[32,4,128]{2,1,0:T(4,128)}), f32[32,4,128]{2,1,0:T(4,128)S(1)}, u32[]{:S(2)}, u32[]{:S(2)}) %all-to-all-start.15) | async-done | bytes 65568 | tf_op jit(solution)/shard_map/all_to_all | solution.py:89
  306.8 10.2 %all_to_all.122 = f32[16,32,128]{2,1,0:T(8,128)S(1)} all-to-all(f32[16,32,128]{2,1,0:T(8,128)S(1)} %broadcast_in_dim.23), channel_id=1, replica_groups=mesh['row'=32,'band'=16] {'band'}, dimensions={0} | all-to-all | bytes 524288 | tf_op jit(solution)/shard_map/all_to_all | solution.py:19
  317.5 17.5 %all_to_all.115 = f32[32,1,1]{2,1,0:T(1,128)S(1)} all-to-all(f32[32,1,1]{2,1,0:T(1,128)S(1)} %bitcast.437), channel_id=1, replica_groups=mesh['row'=32,'band'=16] {'row'}, dimensions={0} | all-to-all | bytes 256 | tf_op jit(solution)/shard_map/all_to_all | solution.py:24
  (255 shorter events, 63.1 us)
Async XLA Ops:
  2.4 21.6 %copy-start.1 = (bf16[32,1,128,128]{3,2,1,0:T(8,128)(2,1)S(1)}, bf16[32,1,128,128]{3,2,1,0:T(8,128)(2,1)}, u32[]{:S(2)}) copy-start(bf16[32,1,128,128]{3,2,1,0:T(8,128)(2,1)} %param.7) | copy-start | bytes 3145732
  3.6 24.6 %copy-start.18 = (s32[1,1,32,2]{2,3,1,0:T(2,128)S(1)}, s32[1,1,32,2]{2,3,1,0:T(2,128)}, u32[]{:S(2)}) copy-start(s32[1,1,32,2]{2,3,1,0:T(2,128)} %param.9) | copy-start | bytes 772
  5.1 29.8 %all-to-all-start = ((f32[32,3,128]{2,1,0:T(4,128)}), f32[32,3,128]{2,1,0:T(4,128)S(1)}, u32[]{:S(2)}, u32[]{:S(2)}) async-start(f32[32,3,128]{2,1,0:T(4,128)} %select_maximum_fusion), calls=%async_computation | async-start | bytes 131072 | tf_op jit(solution)/shard_map/all_to_all | solution.py:80
  21.9 6.5 %collective-permute-start = (bf16[16,128]{1,0:T(8,128)(2,1)S(1)}, bf16[16,128]{1,0:T(8,128)(2,1)S(1)}, u32[]{:S(2)}, u32[]{:S(2)}) collective-permute-start(bf16[16,128]{1,0:T(8,128)(2,1)S(1)} %slice.200), channel_id=1, source_target_pairs={{16,0},{32,16},{48,32},{64,48},{80,64},{96,80},{112,96},{128,112},... | collective-permute-start | bytes 12296 | tf_op jit(solution)/shard_map/ppermute | solution.py:13
  24.4 213.1 %copy-start.6 = (f32[32]{0:T(128)}, f32[32]{0:T(128)S(1)}, u32[]{:S(2)}) copy-start(f32[32]{0:T(128)S(1)} %compare_select_fusion) | copy-start | bytes 388
  24.7 10.6 %collective-permute-start.1 = (f32[16,128]{1,0:T(8,128)S(1)}, f32[16,128]{1,0:T(8,128)S(1)}, u32[]{:S(2)}, u32[]{:S(2)}) collective-permute-start(f32[16,128]{1,0:T(8,128)S(1)} %slice.261), channel_id=1, source_target_pairs={{0,16},{16,32},{32,48},{48,64},{64,80},{80,96},{96,112},{112,128},... | collective-permute-start | bytes 24584 | tf_op jit(solution)/shard_map/ppermute | solution.py:13
  28.4 198.7 %copy-start.8 = (s32[64]{0:T(128)}, s32[64]{0:T(128)S(1)}, u32[]{:S(2)}) copy-start(s32[64]{0:T(128)S(1)} %eq.23) | copy-start | bytes 772
  28.4 222.7 %copy-start.10 = (f32[32]{0:T(128)}, f32[32]{0:T(128)S(1)}, u32[]{:S(2)}) copy-start(f32[32]{0:T(128)S(1)} %compare_convert_fusion) | copy-start | bytes 388
  35.0 191.8 %copy-start.9 = (s32[64]{0:T(128)}, s32[64]{0:T(128)S(1)}, u32[]{:S(2)}) copy-start(s32[64]{0:T(128)S(1)} %convert_element_type.143) | copy-start | bytes 772
  50.0 17.1 %collective-permute-start.2 = (bf16[16,128]{1,0:T(8,128)(2,1)S(1)}, bf16[16,128]{1,0:T(8,128)(2,1)S(1)}, u32[]{:S(2)}, u32[]{:S(2)}) collective-permute-start(bf16[16,128]{1,0:T(8,128)(2,1)S(1)} %slice.263), channel_id=1, source_target_pairs={{16,0},{32,16},{48,32},{64,48},{80,64},{96,80},{112,96},{128,112},... | collective-permute-start | bytes 12296 | tf_op jit(solution)/shard_map/ppermute | solution.py:13
  56.3 19.5 %all-to-all-start.2 = ((f32[32,4,128]{2,1,0:T(4,128)}), f32[32,4,128]{2,1,0:T(4,128)S(1)}, u32[]{:S(2)}, u32[]{:S(2)}) async-start(f32[32,4,128]{2,1,0:T(4,128)} %pad_maximum_fusion), calls=%async_computation.2 | async-start | bytes 131072 | tf_op jit(solution)/shard_map/all_to_all | solution.py:89
  63.5 13.8 %collective-permute-start.3 = (f32[16,128]{1,0:T(8,128)S(1)}, f32[16,128]{1,0:T(8,128)S(1)}, u32[]{:S(2)}, u32[]{:S(2)}) collective-permute-start(f32[16,128]{1,0:T(8,128)S(1)} %slice.268), channel_id=1, source_target_pairs={{0,16},{16,32},{32,48},{48,64},{64,80},{80,96},{96,112},{112,128},... | collective-permute-start | bytes 24584 | tf_op jit(solution)/shard_map/ppermute | solution.py:13
  87.7 34.9 %copy-start.2 = (f32[32,128]{1,0:T(8,128)}, f32[32,128]{1,0:T(8,128)S(1)}, u32[]{:S(2)}) copy-start(f32[32,128]{1,0:T(8,128)S(1)} %get-tuple-element.51) | copy-start | bytes 49156
  88.1 13.9 %collective-permute-start.4 = (bf16[16,128]{1,0:T(8,128)(2,1)S(1)}, bf16[16,128]{1,0:T(8,128)(2,1)S(1)}, u32[]{:S(2)}, u32[]{:S(2)}) collective-permute-start(bf16[16,128]{1,0:T(8,128)(2,1)S(1)} %slice.270), channel_id=1, source_target_pairs={{16,0},{32,16},{48,32},{64,48},{80,64},{96,80},{112,96},{128,112},... | collective-permute-start | bytes 12296 | tf_op jit(solution)/shard_map/ppermute | solution.py:13
  94.1 16.6 %all-to-all-start.4 = ((f32[32,4,128]{2,1,0:T(4,128)}), f32[32,4,128]{2,1,0:T(4,128)S(1)}, u32[]{:S(2)}, u32[]{:S(2)}) async-start(f32[32,4,128]{2,1,0:T(4,128)} %pad_maximum_fusion.1), calls=%async_computation.4 | async-start | bytes 131072 | tf_op jit(solution)/shard_map/all_to_all | solution.py:89
  98.4 13.8 %collective-permute-start.5 = (f32[16,128]{1,0:T(8,128)S(1)}, f32[16,128]{1,0:T(8,128)S(1)}, u32[]{:S(2)}, u32[]{:S(2)}) collective-permute-start(f32[16,128]{1,0:T(8,128)S(1)} %slice.275), channel_id=1, source_target_pairs={{0,16},{16,32},{32,48},{48,64},{64,80},{80,96},{96,112},{112,128},... | collective-permute-start | bytes 24584 | tf_op jit(solution)/shard_map/ppermute | solution.py:13
  141.4 51.9 %copy-start.12 = (f32[128]{0:T(128)}, f32[128]{0:T(128)S(1)}, u32[]{:S(2)}) copy-start(f32[128]{0:T(128)S(1)} %get-tuple-element.25) | copy-start | bytes 1540
  141.4 51.9 %copy-start.14 = (f32[1,128]{1,0:T(1,128)}, f32[1,128]{1,0:T(1,128)S(1)}, u32[]{:S(2)}) copy-start(f32[1,128]{1,0:T(1,128)S(1)} %get-tuple-element.27) | copy-start | bytes 1540
  141.8 12.7 %collective-permute-start.6 = (bf16[16,128]{1,0:T(8,128)(2,1)S(1)}, bf16[16,128]{1,0:T(8,128)(2,1)S(1)}, u32[]{:S(2)}, u32[]{:S(2)}) collective-permute-start(bf16[16,128]{1,0:T(8,128)(2,1)S(1)} %slice.277), channel_id=1, source_target_pairs={{16,0},{32,16},{48,32},{64,48},{80,64},{96,80},{112,96},{128,112},... | collective-permute-start | bytes 12296 | tf_op jit(solution)/shard_map/ppermute | solution.py:13
  146.0 17.1 %all-to-all-start.7 = ((f32[32,4,128]{2,1,0:T(4,128)}), f32[32,4,128]{2,1,0:T(4,128)S(1)}, u32[]{:S(2)}, u32[]{:S(2)}) async-start(f32[32,4,128]{2,1,0:T(4,128)} %pad_maximum_fusion.4), calls=%async_computation.7 | async-start | bytes 131072 | tf_op jit(solution)/shard_map/all_to_all | solution.py:89
  150.8 13.8 %collective-permute-start.7 = (f32[16,128]{1,0:T(8,128)S(1)}, f32[16,128]{1,0:T(8,128)S(1)}, u32[]{:S(2)}, u32[]{:S(2)}) collective-permute-start(f32[16,128]{1,0:T(8,128)S(1)} %slice.282), channel_id=1, source_target_pairs={{0,16},{16,32},{32,48},{48,64},{64,80},{80,96},{96,112},{112,128},... | collective-permute-start | bytes 24584 | tf_op jit(solution)/shard_map/ppermute | solution.py:13
  155.2 37.9 %copy-start.20 = (f32[1,128]{1,0:T(1,128)S(1)}, f32[1,128]{1,0:T(1,128)}, u32[]{:S(2)}) copy-start(f32[1,128]{1,0:T(1,128)} %get-tuple-element.26) | copy-start | bytes 1540
  193.7 12.5 %collective-permute-start.8 = (bf16[16,128]{1,0:T(8,128)(2,1)S(1)}, bf16[16,128]{1,0:T(8,128)(2,1)S(1)}, u32[]{:S(2)}, u32[]{:S(2)}) collective-permute-start(bf16[16,128]{1,0:T(8,128)(2,1)S(1)} %slice.284), channel_id=1, source_target_pairs={{16,0},{32,16},{48,32},{64,48},{80,64},{96,80},{112,96},{128,112},... | collective-permute-start | bytes 12296 | tf_op jit(solution)/shard_map/ppermute | solution.py:13
  197.9 17.1 %all-to-all-start.10 = ((f32[32,4,128]{2,1,0:T(4,128)}), f32[32,4,128]{2,1,0:T(4,128)S(1)}, u32[]{:S(2)}, u32[]{:S(2)}) async-start(f32[32,4,128]{2,1,0:T(4,128)} %pad_maximum_fusion.5), calls=%async_computation.10 | async-start | bytes 131072 | tf_op jit(solution)/shard_map/all_to_all | solution.py:89
  202.7 13.8 %collective-permute-start.9 = (f32[16,128]{1,0:T(8,128)S(1)}, f32[16,128]{1,0:T(8,128)S(1)}, u32[]{:S(2)}, u32[]{:S(2)}) collective-permute-start(f32[16,128]{1,0:T(8,128)S(1)} %slice.289), channel_id=1, source_target_pairs={{0,16},{16,32},{32,48},{48,64},{64,80},{80,96},{96,112},{112,128},... | collective-permute-start | bytes 24584 | tf_op jit(solution)/shard_map/ppermute | solution.py:13
  227.2 13.8 %collective-permute-start.10 = (bf16[16,128]{1,0:T(8,128)(2,1)S(1)}, bf16[16,128]{1,0:T(8,128)(2,1)S(1)}, u32[]{:S(2)}, u32[]{:S(2)}) collective-permute-start(bf16[16,128]{1,0:T(8,128)(2,1)S(1)} %slice.291), channel_id=1, source_target_pairs={{16,0},{32,16},{48,32},{64,48},{80,64},{96,80},{112,96},{128,112},... | collective-permute-start | bytes 12296 | tf_op jit(solution)/shard_map/ppermute | solution.py:13
  233.5 16.2 %all-to-all-start.12 = ((f32[32,4,128]{2,1,0:T(4,128)}), f32[32,4,128]{2,1,0:T(4,128)S(1)}, u32[]{:S(2)}, u32[]{:S(2)}) async-start(f32[32,4,128]{2,1,0:T(4,128)} %pad_maximum_fusion.6), calls=%async_computation.12 | async-start | bytes 131072 | tf_op jit(solution)/shard_map/all_to_all | solution.py:89
  237.8 13.4 %collective-permute-start.11 = (f32[16,128]{1,0:T(8,128)S(1)}, f32[16,128]{1,0:T(8,128)S(1)}, u32[]{:S(2)}, u32[]{:S(2)}) collective-permute-start(f32[16,128]{1,0:T(8,128)S(1)} %slice.296), channel_id=1, source_target_pairs={{0,16},{16,32},{32,48},{48,64},{64,80},{80,96},{96,112},{112,128},... | collective-permute-start | bytes 24584 | tf_op jit(solution)/shard_map/ppermute | solution.py:13
  264.4 28.3 %copy-start.7 = (f32[32]{0:T(128)S(1)}, f32[32]{0:T(128)}, u32[]{:S(2)}) copy-start(f32[32]{0:T(128)} %copy-done.6) | copy-start | bytes 388
  284.0 12.5 %collective-permute-start.12 = (bf16[16,128]{1,0:T(8,128)(2,1)S(1)}, bf16[16,128]{1,0:T(8,128)(2,1)S(1)}, u32[]{:S(2)}, u32[]{:S(2)}) collective-permute-start(bf16[16,128]{1,0:T(8,128)(2,1)S(1)} %slice.298), channel_id=1, source_target_pairs={{16,0},{32,16},{48,32},{64,48},{80,64},{96,80},{112,96},{128,112},... | collective-permute-start | bytes 12296 | tf_op jit(solution)/shard_map/ppermute | solution.py:13
  288.2 17.1 %all-to-all-start.15 = ((f32[32,4,128]{2,1,0:T(4,128)}), f32[32,4,128]{2,1,0:T(4,128)S(1)}, u32[]{:S(2)}, u32[]{:S(2)}) async-start(f32[32,4,128]{2,1,0:T(4,128)} %pad_maximum_fusion.9), calls=%async_computation.15 | async-start | bytes 131072 | tf_op jit(solution)/shard_map/all_to_all | solution.py:89
  292.9 13.8 %collective-permute-start.13 = (f32[16,128]{1,0:T(8,128)S(1)}, f32[16,128]{1,0:T(8,128)S(1)}, u32[]{:S(2)}, u32[]{:S(2)}) collective-permute-start(f32[16,128]{1,0:T(8,128)S(1)} %slice.303), channel_id=1, source_target_pairs={{0,16},{16,32},{32,48},{48,64},{64,80},{80,96},{96,112},{112,128},... | collective-permute-start | bytes 24584 | tf_op jit(solution)/shard_map/ppermute | solution.py:13
  (10 other events, 150.0 us)
